TPU v7x, 256 devices: a whole 4x4x8 slice. The times are simulated.
256 devices in a mesh: blk: 32 (over z, y), group: 8 (over x, core).
Axes of the slice: x: 4, y: 4, z: 8, core: 2. Of those that a mesh axis runs over, the one named last changes fastest.
Arguments:
- queries: bfloat16 [32, 2048, 2560], P('blk', 'group'), may hold values from -16 to 16
- new_kv: bfloat16 [32, 2048, 512], P('blk', 'group'), may hold values from -16 to 16
- kv_pool: bfloat16 [1024, 128, 512], P('blk'), may hold values from -16 to 16
- window_table: int32 [32, 16], replicated, may hold values from 0 to 1023, as said below
- append_table: int32 [32, 16], replicated, may hold values from 0 to 1023, as said below
- cache_lengths: int32 [32], replicated, may hold values from 0 to 16384, as said below
Outputs:
- attn_out: bfloat16 [32, 2048, 2560], P('blk', 'group')
- new_pool: bfloat16 [1024, 128, 512], P('blk')
Inputs may be any that keep to these rules, and one draw needn't show every extreme that they name: `window_table`: pool page p lies on blk index p // 32. The two tables together name every pool page exactly once. For each k, each blk index holds window page k of exactly one request; at most 1 window pages of one request lie on one blk index, and some request has that many there. `append_table`: for each k, each blk index receives appended page k of exactly one request; at most one appended page of one request goes to one blk index, and some request sends one there. `cache_lengths`: A multiple of 128; some request has no cached token and some has 16384.
All inputs are finite; a program needn't handle non-finite values.
Results may differ from a plain program's by a relative error of at most 0.0043.
Values may be sent and summed in bfloat16 or wider, within the bound.
No kernel may reach another device: no remote copies, remote signals or barrier semaphores. Data moves between devices by JAX's collectives and lax.ppermute only.
A program may use at most 128 MiB of HBM per device.

v0:
```python
import jax
import jax.numpy as jnp
from jax import lax
from jax.sharding import PartitionSpec as P


def earlier_same(owners):
    slot_count = owners.shape[1]
    same_owner = owners[:, :, None] == owners[:, None, :]
    before = jnp.arange(slot_count)[None, :] < jnp.arange(slot_count)[:, None]
    return jnp.sum(same_owner & before[None, :, :], axis=2)


def pick_rows(wanted, values):
    return jnp.sum(jnp.where(wanted, values[:, None, :], 0), axis=2)


def attend(qblock, keys_use, index_use, live_use, block_start, head_count, head_size, window_len):
    block_len = qblock.shape[0]
    query_rows = qblock.reshape(block_len, head_count, head_size)
    scores = jnp.einsum(
        "thd,kd->thk", query_rows, keys_use[:, :head_size], preferred_element_type=jnp.float32
    ) * head_size ** (-0.5)
    positions = block_start + jnp.arange(block_len)
    allowed = (
        (index_use[None, :] > positions[:, None])
        & (index_use[None, :] <= positions[:, None] + window_len)
        & live_use[None, :]
    )
    scores = jnp.where(allowed[:, None, :], scores, -jnp.inf)
    row_max = jnp.max(scores, axis=2, keepdims=True)
    raw_weights = jnp.exp(scores - row_max)
    row_total = jnp.sum(raw_weights, axis=2, keepdims=True)
    weights = raw_weights.astype(jnp.bfloat16)
    weighted = jnp.einsum(
        "thk,kd->thd", weights, keys_use[:, head_size:], preferred_element_type=jnp.float32
    )
    return (weighted / row_total).astype(jnp.bfloat16).reshape(block_len, head_count * head_size)


def shards(queries, new_kv, kv_pool, window_table, append_table, cache_lengths):
    blocks = lax.axis_size("blk")
    my_block = lax.axis_index("blk")
    piece_index = lax.axis_index("group")
    tok_rows = queries.shape[1]
    per_owner = kv_pool.shape[0]
    page_rows = kv_pool.shape[1]
    key_width = kv_pool.shape[2]
    head_size = key_width // 2
    head_count = queries.shape[2] // head_size
    win_pages = window_table.shape[1]
    new_pages = append_table.shape[1]
    win_rows = win_pages * page_rows
    cap_win = (win_pages + blocks - 1) // blocks
    cap_new = (new_pages + blocks - 1) // blocks
    fresh_keys = lax.all_gather(new_kv, "group", axis=1, tiled=True)[0]
    append_rows = fresh_keys.shape[0]
    win_owner = window_table // per_owner
    win_rank = earlier_same(win_owner)
    win_wanted = (win_owner == my_block)[:, None, :] & (
        win_rank[:, None, :] == jnp.arange(cap_win)[None, :, None]
    )
    send_ids = pick_rows(win_wanted, window_table % per_owner)
    send_live = jnp.any(win_wanted, axis=2)
    own_owner = lax.dynamic_index_in_dim(win_owner, my_block, 0, keepdims=False)
    own_rank = lax.dynamic_index_in_dim(win_rank, my_block, 0, keepdims=False)
    arrival = own_owner * cap_win + own_rank
    outgoing = jnp.where(send_live[:, :, None, None], kv_pool[send_ids], 0)
    received = lax.all_to_all(
        outgoing.reshape(blocks * cap_win, page_rows, key_width),
        "blk",
        split_axis=0,
        concat_axis=0,
        tiled=True,
    )
    cached = received[arrival]
    new_owner = append_table // per_owner
    new_rank = earlier_same(new_owner)
    mine_owner = lax.dynamic_index_in_dim(new_owner, my_block, 0, keepdims=False)
    mine_rank = lax.dynamic_index_in_dim(new_rank, my_block, 0, keepdims=False)
    dest_wanted = (mine_owner[None, None, :] == jnp.arange(blocks)[:, None, None]) & (
        mine_rank[None, None, :] == jnp.arange(cap_new)[None, :, None]
    )
    page_pick = jnp.sum(jnp.where(dest_wanted, jnp.arange(new_pages)[None, None, :], 0), axis=2)
    page_live = jnp.any(dest_wanted, axis=2)
    fresh_pages = fresh_keys.reshape(new_pages, page_rows, key_width)
    parcels = jnp.where(page_live[:, :, None, None], fresh_pages[page_pick], 0)
    arrived = lax.all_to_all(
        parcels.reshape(blocks * cap_new, page_rows, key_width),
        "blk",
        split_axis=0,
        concat_axis=0,
        tiled=True,
    )
    land_wanted = (new_owner == my_block)[:, None, :] & (
        new_rank[:, None, :] == jnp.arange(cap_new)[None, :, None]
    )
    land_ids = pick_rows(land_wanted, append_table % per_owner)
    land_live = jnp.any(land_wanted, axis=2)
    targets = jnp.where(land_live, land_ids, per_owner).reshape(-1)
    new_pool = kv_pool.at[targets].set(arrived, mode="drop")
    keys_all = jnp.concatenate([cached.reshape(win_rows, key_width), fresh_keys], axis=0)
    own_length = lax.dynamic_index_in_dim(cache_lengths, my_block, 0, keepdims=False)
    filled = jnp.minimum(own_length // page_rows, win_pages)
    key_index = jnp.arange(win_rows + append_rows)
    live_keys = (key_index >= win_rows) | (key_index // page_rows >= win_pages - filled)
    block_len = min(128, tok_rows)
    block_count = tok_rows // block_len
    query_blocks = queries[0].reshape(block_count, block_len, queries.shape[2])
    first_row = piece_index * tok_rows
    offsets = jnp.arange(block_count) * block_len

    def one_block(inputs):
        qblock, offset = inputs
        block_start = first_row + offset
        return attend(
            qblock, keys_all, key_index, live_keys, block_start, head_count, head_size, win_rows
        )

    attended = lax.map(one_block, (query_blocks, offsets))
    attn_out = attended.reshape(1, tok_rows, queries.shape[2])
    return (attn_out, new_pool)


def solution(mesh):
    in_specs = (
        P("blk", "group", None),
        P("blk", "group", None),
        P("blk", None, None),
        P(),
        P(),
        P(),
    )
    out_specs = (P("blk", "group", None), P("blk", None, None))
    return jax.shard_map(shards, mesh=mesh, in_specs=in_specs, out_specs=out_specs, check_vma=False)
```

profile of v0, /device:TPU:1, one launch (start us, length us, event | category | flops | bytes accessed | tf_op | source)
XLA Modules:
  0.0 246.1 jit_solution(13082711198995688565)
XLA Ops:
  7.2 4.7 %copy.51 = bf16[32,128,512]{2,1,0:T(8,128)(2,1)} copy(bf16[32,128,512]{2,1,0:T(8,128)(2,1)} %param.10) | data formatting | bytes 8388608
  12.1 4.9 %gather_fusion = bf16[32,128,512]{2,1,0:T(8,128)(2,1)} fusion(bf16[32,128,512]{2,1,0:T(8,128)(2,1)} %copy.51, s32[1024]{0:T(1024)S(1)} %pad_clamp_fusion.2), kind=kCustom, calls=%fused_computation | custom fusion | bytes 8388736 | tf_op jit(solution)/shard_map/gather | solution.py:68
  17.0 4.5 %broadcast_select_fusion.1 = bf16[32,128,512]{2,1,0:T(8,128)(2,1)} fusion(bf16[32,128,512]{2,1,0:T(8,128)(2,1)} %gather_fusion, pred[32]{0:T(512)(128)(4,1)S(1)} %get-tuple-element.118), kind=kLoop, calls=%fused_computation.41 | loop fusion | flops 2097152 | bytes 8388640 | tf_op jit(solution)/shard_map/jit(_where)/select_n | solution.py:68
  21.5 12.3 %all-to-all-start = ((bf16[32,128,512]{2,1,0:T(8,128)(2,1)}), bf16[32,128,512]{2,1,0:T(8,128)(2,1)}, u32[]{:S(2)}, u32[]{:S(2)}) async-start(bf16[32,128,512]{2,1,0:T(8,128)(2,1)} %broadcast_select_fusion.1), calls=%async_computation | async-start | bytes 8388608 | tf_op jit(solution)/shard_map/all_to_all | solution.py:69
  39.1 27.1 %all-gather.2.cloned.1.call-done = bf16[1,2048,512]{2,1,0:T(8,128)(2,1)} async-done(((bf16[1,256,512]{2,1,0:T(8,128)(2,1)}), bf16[1,2048,512]{2,1,0:T(8,128)(2,1)}) %all-gather.2.cloned.1.call-update) | async-done | bytes 2097168 | tf_op jit(solution)/shard_map/all_gather | solution.py:56
  66.2 4.4 %gather_fusion.2 = bf16[32,128,512]{2,1,0:T(8,128)(2,1)} fusion(bf16[16,128,512]{2,1,0:T(8,128)(2,1)} %bitcast.50, s32[1024]{0:T(1024)S(1)} %pad_clamp_fusion), kind=kCustom, calls=%fused_computation.2 | custom fusion | bytes 8388736 | tf_op jit(solution)/shard_map/gather | solution.py:87
  70.5 4.5 %broadcast_select_fusion = bf16[32,128,512]{2,1,0:T(8,128)(2,1)} fusion(bf16[32,128,512]{2,1,0:T(8,128)(2,1)} %gather_fusion.2, pred[32]{0:T(512)(128)(4,1)S(1)} %fusion.35), kind=kLoop, calls=%fused_computation.40 | loop fusion | flops 2097152 | bytes 8388640 | tf_op jit(solution)/shard_map/jit(_where)/select_n | solution.py:87
  75.0 51.8 %all-to-all-done = bf16[32,128,512]{2,1,0:T(8,128)(2,1)} async-done(((bf16[32,128,512]{2,1,0:T(8,128)(2,1)}), bf16[32,128,512]{2,1,0:T(8,128)(2,1)}, u32[]{:S(2)}, u32[]{:S(2)}) %all-to-all-start) | async-done | bytes 4194336 | tf_op jit(solution)/shard_map/all_to_all | solution.py:69
  126.8 8.6 %all-to-all-start.1 = ((bf16[32,128,512]{2,1,0:T(8,128)(2,1)}), bf16[32,128,512]{2,1,0:T(8,128)(2,1)}, u32[]{:S(2)}, u32[]{:S(2)}) async-start(bf16[32,128,512]{2,1,0:T(8,128)(2,1)} %broadcast_select_fusion), calls=%async_computation.1 | async-start | bytes 8388608 | tf_op jit(solution)/shard_map/all_to_all | solution.py:88
  135.4 4.3 %gather_fusion.1 = bf16[16,128,512]{2,1,0:T(8,128)(2,1)} fusion(bf16[32,128,512]{2,1,0:T(8,128)(2,1)} %all-to-all-done, s32[1024]{0:T(1024)S(1)} %pad_clamp_fusion.1), kind=kCustom, calls=%fused_computation.1 | custom fusion | bytes 4194368 | tf_op jit(solution)/shard_map/gather | solution.py:76
  139.8 3.8 %pad_maximum_fusion = bf16[4096,512]{1,0:T(8,128)(2,1)} fusion(bf16[2048,512]{1,0:T(8,128)(2,1)S(1)} %bitcast.51, bf16[2048,512]{1,0:T(8,128)(2,1)} %bitcast.53), kind=kLoop, calls=%fused_computation.39 | loop fusion | flops 8388608 | bytes 8388608 | tf_op jit(solution)/shard_map/concatenate | solution.py:102
  143.6 45.2 %while.12 = (s32[]{:T(128)}, bf16[2,128,2560]{2,1,0:T(8,128)(2,1)}, s32[2]{0:T(128)S(1)}, s32[]{:T(128)}, bf16[2,128,2560]{2,1,0:T(8,128)(2,1)}, /*index=5*/bf16[4096,512]{1,0:T(8,128)(2,1)}, s32[]{:T(128)}, s32[]{:T(128)}) while((s32[]{:T(128)}, bf16[2,128,2560]{2,1,0:T(8,128)(2,1)}, s32[2]{0:T(128)S(1)}, s32[]{:T(128)}, ...), condition=%wide.region_6.7_spmd.clone.clone, body=%wide.region_3.6_spmd.clone.clone.sunk | while | flops 5429176320 | bytes 77106312 | solution.py:120
  145.4 1.1 constant_dynamic-slice_fusion.2
  146.9 5.1 %fusion.57 = (f32[128,10]{0,1:T(8,128)S(1)}, f32[128,10,4096]{2,0,1:T(8,128)S(1)}) fusion(pred[128,4096]{1,0:T(8,128)(4,1)S(1)} %fusion.56, bf16[128,10,256]{0,2,1:T(8,128)(2,1)S(1)} %bitcast.52, bf16[4096,512]{1,0:T(8,128)(2,1)} %get-tuple-element.198), kind=kOutput, calls=%fused_computation.8.clone.1 | convolution fusion | flops 2700081920 | bytes 24253440 | tf_op jit(solution)/shard_map/while/body/eval_jaxpr/thd,kd->thk/dot_general | solution.py:21
  152.0 6.0 %fusion.58 = f32[128,10]{0,1:T(8,128)S(1)} fusion(f32[128,10,4096]{2,0,1:T(8,128)S(1)} %get-tuple-element.175, f32[128,10]{0,1:T(8,128)S(1)} %get-tuple-element.176, pred[128,4096]{1,0:T(8,128)(4,1)S(1)} %fusion.56), kind=kLoop, calls=%fused_computation.9.clone.1 | loop fusion | flops 20970240 | bytes 21506048 | tf_op jit(solution)/shard_map/while/body/eval_jaxpr/reduce_sum | solution.py:33
  158.0 6.7 %divide_convert_fusion.2 = bf16[128,10,256]{2,0,1:T(8,128)(2,1)S(1)} fusion(bf16[4096,512]{1,0:T(8,128)(2,1)} %get-tuple-element.198, f32[128,10,4096]{2,0,1:T(8,128)S(1)} %get-tuple-element.175, f32[128,10]{0,1:T(8,128)S(1)} %get-tuple-element.176, pred[128,4096]{1,0:T(8,128)(4,1)S(1)} %fusion.56, f32[128,10]{0,1:T(8,128)S(1)} %fusion.58), kind=kOutput, calls=%fused_computation.22.clone.1 | convolution fusion | flops 2705981440 | bytes 24258560 | tf_op jit(solution)/shard_map/while/body/eval_jaxpr/thk,kd->thd/dot_general | solution.py:35
  165.3 0.9 constant_dynamic-update-slice_fusion.2
  168.0 1.1 constant_dynamic-slice_fusion.2
  169.5 5.1 %fusion.57 = (f32[128,10]{0,1:T(8,128)S(1)}, f32[128,10,4096]{2,0,1:T(8,128)S(1)}) fusion(pred[128,4096]{1,0:T(8,128)(4,1)S(1)} %fusion.56, bf16[128,10,256]{0,2,1:T(8,128)(2,1)S(1)} %bitcast.52, bf16[4096,512]{1,0:T(8,128)(2,1)} %get-tuple-element.198), kind=kOutput, calls=%fused_computation.8.clone.1 | convolution fusion | flops 2700081920 | bytes 24253440 | tf_op jit(solution)/shard_map/while/body/eval_jaxpr/thd,kd->thk/dot_general | solution.py:21
  174.6 6.0 %fusion.58 = f32[128,10]{0,1:T(8,128)S(1)} fusion(f32[128,10,4096]{2,0,1:T(8,128)S(1)} %get-tuple-element.175, f32[128,10]{0,1:T(8,128)S(1)} %get-tuple-element.176, pred[128,4096]{1,0:T(8,128)(4,1)S(1)} %fusion.56), kind=kLoop, calls=%fused_computation.9.clone.1 | loop fusion | flops 20970240 | bytes 21506048 | tf_op jit(solution)/shard_map/while/body/eval_jaxpr/reduce_sum | solution.py:33
  180.6 6.7 %divide_convert_fusion.2 = bf16[128,10,256]{2,0,1:T(8,128)(2,1)S(1)} fusion(bf16[4096,512]{1,0:T(8,128)(2,1)} %get-tuple-element.198, f32[128,10,4096]{2,0,1:T(8,128)S(1)} %get-tuple-element.175, f32[128,10]{0,1:T(8,128)S(1)} %get-tuple-element.176, pred[128,4096]{1,0:T(8,128)(4,1)S(1)} %fusion.56, f32[128,10]{0,1:T(8,128)S(1)} %fusion.58), kind=kOutput, calls=%fused_computation.22.clone.1 | convolution fusion | flops 2705981440 | bytes 24258560 | tf_op jit(solution)/shard_map/while/body/eval_jaxpr/thk,kd->thd/dot_general | solution.py:35
  187.9 0.9 constant_dynamic-update-slice_fusion.2
  188.8 39.7 %all-to-all-done.1 = bf16[32,128,512]{2,1,0:T(8,128)(2,1)} async-done(((bf16[32,128,512]{2,1,0:T(8,128)(2,1)}), bf16[32,128,512]{2,1,0:T(8,128)(2,1)}, u32[]{:S(2)}, u32[]{:S(2)}) %all-to-all-start.1) | async-done | bytes 4194336 | tf_op jit(solution)/shard_map/all_to_all | solution.py:88
  228.5 10.7 %scatter_fusion = bf16[32,128,512]{2,1,0:T(8,128)(2,1)} fusion(bf16[32,128,512]{2,1,0:T(8,128)(2,1)} %copy.51, s32[32]{0:T(128)S(1)} %copy-done.3, bf16[32,128,512]{2,1,0:T(8,128)(2,1)} %all-to-all-done.1), kind=kCustom, calls=%fused_computation.3 | custom fusion | bytes 12583040 | tf_op jit(solution)/shard_map/scatter | solution.py:101
  (48 shorter events, 7.1 us)
Async XLA Ops:
  7.2 4.7 %copy-start.1 = (s32[32,16]{0,1:T(8,128)S(1)}, s32[32,16]{0,1:T(8,128)}, u32[]{:S(2)}) copy-start(s32[32,16]{0,1:T(8,128)} %param.11) | copy-start | bytes 6148
  7.2 4.7 %copy-start.2 = (s32[32,16]{0,1:T(8,128)S(1)}, s32[32,16]{0,1:T(8,128)}, u32[]{:S(2)}) copy-start(s32[32,16]{0,1:T(8,128)} %param.12) | copy-start | bytes 6148
  21.5 13.0 %copy-start.4 = (s32[32]{0:T(128)S(1)}, s32[32]{0:T(128)}, u32[]{:S(2)}) copy-start(s32[32]{0:T(128)} %param.13) | copy-start | bytes 388
  21.5 105.3 %all-to-all-start = ((bf16[32,128,512]{2,1,0:T(8,128)(2,1)}), bf16[32,128,512]{2,1,0:T(8,128)(2,1)}, u32[]{:S(2)}, u32[]{:S(2)}) async-start(bf16[32,128,512]{2,1,0:T(8,128)(2,1)} %broadcast_select_fusion.1), calls=%async_computation | async-start | bytes 8388608 | tf_op jit(solution)/shard_map/all_to_all | solution.py:69
  33.8 32.4 %all-gather.2.cloned.1.call-start = ((), (), s32[]{:S(2)}) async-start(), calls=%async_computation.2 | async-start | bytes 2359296 | tf_op jit(solution)/shard_map/all_gather | solution.py:56
  126.8 101.7 %all-to-all-start.1 = ((bf16[32,128,512]{2,1,0:T(8,128)(2,1)}), bf16[32,128,512]{2,1,0:T(8,128)(2,1)}, u32[]{:S(2)}, u32[]{:S(2)}) async-start(bf16[32,128,512]{2,1,0:T(8,128)(2,1)} %broadcast_select_fusion), calls=%async_computation.1 | async-start | bytes 8388608 | tf_op jit(solution)/shard_map/all_to_all | solution.py:88
  135.4 4.4 %copy-start = (bf16[1,2048,512]{2,1,0:T(8,128)(2,1)S(1)}, bf16[1,2048,512]{2,1,0:T(8,128)(2,1)}, u32[]{:S(2)}) copy-start(bf16[1,2048,512]{2,1,0:T(8,128)(2,1)} %all-gather.2.cloned.1.call-done) | copy-start | bytes 6291460
  143.6 84.9 %copy-start.3 = (s32[32]{0:T(128)S(1)}, s32[32]{0:T(128)}, u32[]{:S(2)}) copy-start(s32[32]{0:T(128)} %fusion.41) | copy-start | bytes 388
Sparse Core Ops, SparseCore 0:
  36.4 29.6 all-gather.1
where the time goes:
time: 250 us; the launch traced here: 246 us
  waiting for transfers between devices  119 us (48%)
  local copies, waits for them, and re-layouts  36.9 us (15%)
  other arithmetic  27.3 us (11%)
  matrix products  23.6 us (9%)
  starting transfers between devices  20.9 us (8%)
  between operations  16.7 us (7%)
    all_to_all x1, waiting for transfers between devices, shards(): lax.all_to_all(outgoing.reshape(blocks * cap_win, page_rows, key_width),...  51.8 us
    all_to_all x1, waiting for transfers between devices, shards(): lax.all_to_all(parcels.reshape(blocks * cap_new, page_rows, key_width), '...  39.7 us
    all_gather x1, waiting for transfers between devices, shards(): fresh_keys = lax.all_gather(new_kv, 'group', axis=1, tiled=True)[0]  27.1 us
    dot_general x2, matrix products, attend(): jnp.einsum('thk,kd->thd', weights, keys_use[:, head_size:], preferred_ele...  13.4 us
    all_to_all x1, starting transfers between devices, shards(): lax.all_to_all(outgoing.reshape(blocks * cap_win, page_rows, key_width),...  12.3 us
    reduce_sum x2, other arithmetic, attend(): row_total = jnp.sum(raw_weights, axis=2, keepdims=True)  12 us
    scatter x1, local copies, waits for them, and re-layouts, shards(): new_pool = kv_pool.at[targets].set(arrived, mode='drop')  10.7 us
    dot_general x2, matrix products, attend(): jnp.einsum('thd,kd->thk', query_rows, keys_use[:, :head_size], preferred_...  10.2 us
  transfers between devices with their start and end apart: 3, of which 3 were waited for; matrix products, arithmetic and copies ran while one was open for 26% of the time, Pallas kernels for 0%

commit v1 on v0

--- a/solution.py
+++ b/solution.py
@@ -38,8 +38,14 @@
     return (weighted / row_total).astype(jnp.bfloat16).reshape(block_len, head_count * head_size)
 
 
+def regroup(pieces):
+    groups, pages, piece_rows, width = pieces.shape
+    return pieces.transpose(1, 0, 2, 3).reshape(pages, groups * piece_rows, width)
+
+
 def shards(queries, new_kv, kv_pool, window_table, append_table, cache_lengths):
     blocks = lax.axis_size("blk")
+    groups = lax.axis_size("group")
     my_block = lax.axis_index("blk")
     piece_index = lax.axis_index("group")
     tok_rows = queries.shape[1]
@@ -53,27 +59,26 @@
     win_rows = win_pages * page_rows
     cap_win = (win_pages + blocks - 1) // blocks
     cap_new = (new_pages + blocks - 1) // blocks
+    piece_rows = page_rows // groups
+    piece_start = piece_index * piece_rows
     fresh_keys = lax.all_gather(new_kv, "group", axis=1, tiled=True)[0]
     append_rows = fresh_keys.shape[0]
+
     win_owner = window_table // per_owner
     win_rank = earlier_same(win_owner)
     win_wanted = (win_owner == my_block)[:, None, :] & (
         win_rank[:, None, :] == jnp.arange(cap_win)[None, :, None]
     )
     send_ids = pick_rows(win_wanted, window_table % per_owner)
-    send_live = jnp.any(win_wanted, axis=2)
     own_owner = lax.dynamic_index_in_dim(win_owner, my_block, 0, keepdims=False)
     own_rank = lax.dynamic_index_in_dim(win_rank, my_block, 0, keepdims=False)
     arrival = own_owner * cap_win + own_rank
-    outgoing = jnp.where(send_live[:, :, None, None], kv_pool[send_ids], 0)
-    received = lax.all_to_all(
-        outgoing.reshape(blocks * cap_win, page_rows, key_width),
-        "blk",
-        split_axis=0,
-        concat_axis=0,
-        tiled=True,
-    )
-    cached = received[arrival]
+    pool_piece = lax.dynamic_slice_in_dim(kv_pool, piece_start, piece_rows, axis=1)
+    outgoing = pool_piece[send_ids.reshape(-1)]
+    received = lax.all_to_all(outgoing, "blk", split_axis=0, concat_axis=0, tiled=True)
+    cached_piece = received[arrival]
+    cached = regroup(lax.all_gather(cached_piece, "group", axis=0, tiled=False))
+
     new_owner = append_table // per_owner
     new_rank = earlier_same(new_owner)
     mine_owner = lax.dynamic_index_in_dim(new_owner, my_block, 0, keepdims=False)
@@ -82,23 +87,19 @@
         mine_rank[None, None, :] == jnp.arange(cap_new)[None, :, None]
     )
     page_pick = jnp.sum(jnp.where(dest_wanted, jnp.arange(new_pages)[None, None, :], 0), axis=2)
-    page_live = jnp.any(dest_wanted, axis=2)
     fresh_pages = fresh_keys.reshape(new_pages, page_rows, key_width)
-    parcels = jnp.where(page_live[:, :, None, None], fresh_pages[page_pick], 0)
-    arrived = lax.all_to_all(
-        parcels.reshape(blocks * cap_new, page_rows, key_width),
-        "blk",
-        split_axis=0,
-        concat_axis=0,
-        tiled=True,
-    )
-    land_wanted = (new_owner == my_block)[:, None, :] & (
-        new_rank[:, None, :] == jnp.arange(cap_new)[None, :, None]
-    )
-    land_ids = pick_rows(land_wanted, append_table % per_owner)
-    land_live = jnp.any(land_wanted, axis=2)
-    targets = jnp.where(land_live, land_ids, per_owner).reshape(-1)
-    new_pool = kv_pool.at[targets].set(arrived, mode="drop")
+    fresh_piece = lax.dynamic_slice_in_dim(fresh_pages, piece_start, piece_rows, axis=1)
+    parcels = fresh_piece[page_pick.reshape(-1)]
+    arrived = lax.all_to_all(parcels, "blk", split_axis=0, concat_axis=0, tiled=True)
+    land_here = new_owner == my_block
+    land_source = jnp.argmax(land_here, axis=0)
+    land_slot = land_source * cap_new + jnp.take_along_axis(new_rank, land_source[None, :], axis=0)[0]
+    land_ids = jnp.take_along_axis(append_table % per_owner, land_source[None, :], axis=0)[0]
+    land_live = jnp.any(land_here, axis=0)
+    landed = regroup(lax.all_gather(arrived[land_slot], "group", axis=0, tiled=False))
+    targets = jnp.where(land_live, land_ids, per_owner)
+    new_pool = kv_pool.at[targets].set(landed, mode="drop")
+
     keys_all = jnp.concatenate([cached.reshape(win_rows, key_width), fresh_keys], axis=0)
     own_length = lax.dynamic_index_in_dim(cache_lengths, my_block, 0, keepdims=False)
     filled = jnp.minimum(own_length // page_rows, win_pages)
@@ -109,12 +110,16 @@
     query_blocks = queries[0].reshape(block_count, block_len, queries.shape[2])
     first_row = piece_index * tok_rows
     offsets = jnp.arange(block_count) * block_len
+    span = win_rows + block_len
 
     def one_block(inputs):
         qblock, offset = inputs
         block_start = first_row + offset
+        keys_use = lax.dynamic_slice_in_dim(keys_all, block_start, span, 0)
+        index_use = block_start + jnp.arange(span)
+        live_use = lax.dynamic_slice_in_dim(live_keys, block_start, span, 0)
         return attend(
-            qblock, keys_all, key_index, live_keys, block_start, head_count, head_size, win_rows
+            qblock, keys_use, index_use, live_use, block_start, head_count, head_size, win_rows
         )
 
     attended = lax.map(one_block, (query_blocks, offsets))

time: 250 us -> 122 us (0.49); the launches traced: 246 us -> 121 us
  waiting for transfers between devices: 119 us -> 28.7 us
  other arithmetic: 27.3 us -> 9.91 us
  local copies, waits for them, and re-layouts: 36.9 us -> 27.7 us
  matrix products: 23.6 us -> 16.8 us
    all_to_all x2, waiting for transfers between devices: 91.5 us -> 28.3 us  [the longest x1 16 us: shards(): lax.all_to_all(outgoing, 'blk', split_axis=0, concat_axis=0, tiled=True)]
    all_gather x1, waiting for transfers between devices: 27.1 us -> 0.02 us  [shards(): fresh_keys = lax.all_gather(new_kv, 'group', axis=1, tiled=True)[0]]
    select_n x7, other arithmetic: 9.5 us -> 0.06 us  [the longest x1 0.01 us: shards(): win_owner = window_table // per_owner]
    gather x3 -> x6, local copies, waits for them, and re-layouts: 13.7 us -> 6.6 us  [the longest x1 1.37 us: shards(): outgoing = pool_piece[send_ids.reshape(-1)]]
    reduce_sum x2, other arithmetic: 12 us -> 5.53 us  [attend(): row_total = jnp.sum(raw_weights, axis=2, keepdims=True)]
    scatter x1, local copies, waits for them, and re-layouts: 10.7 us -> 5.15 us  [shards(): new_pool = kv_pool.at[targets].set(landed, mode='drop')]
    transpose x0 -> x2, local copies, waits for them, and re-layouts: none -> 3.65 us  [regroup(): pieces.transpose(1, 0, 2, 3).reshape(pages, groups * piece_rows, width)]
    dot_general x2, matrix products: 13.4 us -> 9.93 us  [attend(): jnp.einsum('thk,kd->thd', weights, keys_use[:, head_size:], preferred_ele...]
  transfers between devices with their start and end apart: 3 -> 5, of which waited for: 3 -> 3; matrix products, arithmetic and copies ran while one was open for 26% -> 35% of each run, Pallas kernels for 0% -> 0%
where the time goes in v1:
time: 122 us; the launch traced here: 121 us
  waiting for transfers between devices  28.7 us (24%)
  local copies, waits for them, and re-layouts  27.7 us (23%)
  starting transfers between devices  20.4 us (17%)
  matrix products  16.8 us (14%)
  between operations  16.2 us (13%)
  other arithmetic  9.91 us (8%)
  loops' own time  1.4 us (1%)
    all_to_all x1, waiting for transfers between devices, shards(): lax.all_to_all(outgoing, 'blk', split_axis=0, concat_axis=0, tiled=True)  16 us
    all_to_all x1, waiting for transfers between devices, shards(): lax.all_to_all(parcels, 'blk', split_axis=0, concat_axis=0, tiled=True)  12.3 us
    all_to_all x1, starting transfers between devices, shards(): lax.all_to_all(outgoing, 'blk', split_axis=0, concat_axis=0, tiled=True)  12 us
    dot_general x2, matrix products, attend(): jnp.einsum('thk,kd->thd', weights, keys_use[:, head_size:], preferred_ele...  9.93 us
    all_to_all x1, starting transfers between devices, shards(): lax.all_to_all(parcels, 'blk', split_axis=0, concat_axis=0, tiled=True)  8.29 us
    dot_general x2, matrix products, attend(): jnp.einsum('thd,kd->thk', query_rows, keys_use[:, :head_size], preferred_...  6.91 us
    reduce_sum x2, other arithmetic, attend(): row_total = jnp.sum(raw_weights, axis=2, keepdims=True)  5.53 us
    scatter x1, local copies, waits for them, and re-layouts, shards(): new_pool = kv_pool.at[targets].set(landed, mode='drop')  5.15 us
  transfers between devices with their start and end apart: 5, of which 3 were waited for; matrix products, arithmetic and copies ran while one was open for 35% of the time, Pallas kernels for 0%

profile of v1, /device:TPU:1, one launch (start us, length us, event | category | flops | bytes accessed | tf_op | source)
XLA Modules:
  0.0 121.3 jit_solution(13711488125115085898)
XLA Ops:
  7.2 4.6 %copy.75 = bf16[32,128,512]{2,1,0:T(8,128)(2,1)} copy(bf16[32,128,512]{2,1,0:T(8,128)(2,1)} %param.12) | data formatting | bytes 8388608
  12.3 1.1 constant_dynamic-slice_fusion.2
  13.4 1.4 %gather_fusion = bf16[32,16,512]{2,1,0:T(8,128)(2,1)} fusion(bf16[32,16,512]{2,1,0:T(8,128)(2,1)S(1)} %constant_dynamic-slice_fusion.2, s32[1024]{0:T(1024)S(1)} %pad_clamp_fusion.3), kind=kCustom, calls=%fused_computation.2 | custom fusion | bytes 1048704 | tf_op jit(solution)/shard_map/gather | solution.py:77
  14.7 12.0 %all-to-all-start = ((bf16[32,16,512]{2,1,0:T(8,128)(2,1)}), bf16[32,16,512]{2,1,0:T(8,128)(2,1)S(1)}, u32[]{:S(2)}, u32[]{:S(2)}) async-start(bf16[32,16,512]{2,1,0:T(8,128)(2,1)} %gather_fusion), calls=%async_computation | async-start | bytes 1048576 | tf_op jit(solution)/shard_map/all_to_all | solution.py:78
  27.0 16.0 %all-to-all-done = bf16[32,16,512]{2,1,0:T(8,128)(2,1)S(1)} async-done(((bf16[32,16,512]{2,1,0:T(8,128)(2,1)}), bf16[32,16,512]{2,1,0:T(8,128)(2,1)S(1)}, u32[]{:S(2)}, u32[]{:S(2)}) %all-to-all-start) | async-done | bytes 524320 | tf_op jit(solution)/shard_map/all_to_all | solution.py:78
  43.1 1.3 %gather_fusion.1 = bf16[16,16,512]{2,1,0:T(8,128)(2,1)} fusion(bf16[32,16,512]{2,1,0:T(8,128)(2,1)S(1)} %all-to-all-done, s32[1024]{0:T(1024)S(1)} %pad_clamp_fusion.2), kind=kCustom, calls=%fused_computation.3 | custom fusion | bytes 524352 | tf_op jit(solution)/shard_map/gather | solution.py:79
  45.3 1.0 constant_dynamic-slice_fusion.1
  46.3 1.4 %gather_fusion.2 = bf16[32,16,512]{2,1,0:T(8,128)(2,1)} fusion(bf16[16,16,512]{2,1,0:T(8,128)(2,1)S(1)} %constant_dynamic-slice_fusion.1, s32[1024]{0:T(1024)S(1)} %pad_clamp_fusion.1), kind=kCustom, calls=%fused_computation.4 | custom fusion | bytes 1048704 | tf_op jit(solution)/shard_map/gather | solution.py:92
  47.7 8.3 %all-to-all-start.1 = ((bf16[32,16,512]{2,1,0:T(8,128)(2,1)}), bf16[32,16,512]{2,1,0:T(8,128)(2,1)S(1)}, u32[]{:S(2)}, u32[]{:S(2)}) async-start(bf16[32,16,512]{2,1,0:T(8,128)(2,1)} %gather_fusion.2), calls=%async_computation.1 | async-start | bytes 1048576 | tf_op jit(solution)/shard_map/all_to_all | solution.py:93
  60.3 12.3 %all-to-all-done.1 = bf16[32,16,512]{2,1,0:T(8,128)(2,1)S(1)} async-done(((bf16[32,16,512]{2,1,0:T(8,128)(2,1)}), bf16[32,16,512]{2,1,0:T(8,128)(2,1)S(1)}, u32[]{:S(2)}, u32[]{:S(2)}) %all-to-all-start.1) | async-done | bytes 524320 | tf_op jit(solution)/shard_map/all_to_all | solution.py:93
  72.6 1.3 %gather_fusion.3 = bf16[16,16,512]{2,1,0:T(8,128)(2,1)} fusion(bf16[32,16,512]{2,1,0:T(8,128)(2,1)S(1)} %all-to-all-done.1, s32[1024]{0:T(1024)S(1)} %pad_clamp_fusion), kind=kCustom, calls=%fused_computation.5 | custom fusion | bytes 524352 | tf_op jit(solution)/shard_map/gather | solution.py:99
  74.2 1.8 %copy.52 = bf16[16,8,16,512]{3,2,1,0:T(8,128)(2,1)S(1)} copy(bf16[16,8,16,512]{3,2,0,1:T(8,128)(2,1)} %bitcast.104) | data formatting | bytes 4194304 | tf_op jit(solution)/shard_map/transpose | solution.py:43
  76.1 2.2 %pad_maximum_fusion = bf16[4096,512]{1,0:T(8,128)(2,1)} fusion(bf16[2048,512]{1,0:T(8,128)(2,1)S(1)} %bitcast.103, bf16[2048,512]{1,0:T(8,128)(2,1)S(1)} %bitcast.100), kind=kLoop, calls=%fused_computation.27 | loop fusion | flops 8388608 | bytes 8388608 | tf_op jit(solution)/shard_map/concatenate | solution.py:103
  78.3 29.5 %while.10 = (s32[]{:T(128)}, bf16[2,128,2560]{2,1,0:T(8,128)(2,1)}, s32[2]{0:T(128)S(1)}, s32[]{:T(128)}, pred[4096]{0:T(1024)(128)(4,1)S(1)}, /*index=5*/bf16[2...) while((s32[]{:T(128)}, bf16[2,128,2560]{2,1,0:T(8,128)(2,1)}, ...), condition=%wide.region_5.6_spmd, body=%wide.region_2.5_spmd.sunk | while | flops 2884534272 | bytes 44681820 | solution.py:125
  80.3 3.4 %fusion.38 = (f32[128,10]{0,1:T(8,128)S(1)}, f32[128,10,2176]{2,0,1:T(8,128)S(1)}) fusion(pred[128,2176]{1,0:T(8,128)(4,1)S(1)} %and_and_fusion.2, bf16[128,10,256]{0,2,1:T(8,128)(2,1)S(1)} %bitcast.98, bf16[4096,512]{1,0:T(8,128)(2,1)} %get-tuple-element.175, s32[]{:T(128)S(6)} %select_n.228), kind=kOutput, calls=%fused_computation.9.clone.1 | convolution fusion | flops 1434417920 | bytes 13194244 | tf_op jit(solution)/shard_map/while/body/eval_jaxpr/thd,kd->thk/dot_general | solution.py:21
  83.8 2.8 %fusion.39 = f32[128,10]{0,1:T(8,128)S(1)} fusion(f32[128,10,2176]{2,0,1:T(8,128)S(1)} %get-tuple-element.145, f32[128,10]{0,1:T(8,128)S(1)} %get-tuple-element.146, pred[128,2176]{1,0:T(8,128)(4,1)S(1)} %and_and_fusion.2), kind=kLoop, calls=%fused_computation.10.clone.1 | loop fusion | flops 11139840 | bytes 11429888 | tf_op jit(solution)/shard_map/while/body/eval_jaxpr/reduce_sum | solution.py:33
  86.5 5.0 %divide_convert_fusion.2 = bf16[128,10,256]{2,0,1:T(8,128)(2,1)S(1)} fusion(bf16[4096,512]{1,0:T(8,128)(2,1)} %get-tuple-element.175, s32[]{:T(128)S(6)} %select_n.228, s32[]{:T(128)S(6)} %add.217, f32[128,10,2176]{2,0,1:T(8,128)S(1)} %get-tuple-element.145, f32[128,10]{0,1:T(8,128)S(1)} %get-tuple-element.146, ...), kind=kOutput, calls=%fused_computation.14.clone.1 | convolution fusion | flops 1437859840 | bytes 13199368 | tf_op jit(solution)/shard_map/while/body/eval_jaxpr/thk,kd->thd/dot_general | solution.py:35
  92.1 0.9 constant_dynamic-update-slice_fusion.2
  95.1 3.5 %fusion.38 = (f32[128,10]{0,1:T(8,128)S(1)}, f32[128,10,2176]{2,0,1:T(8,128)S(1)}) fusion(pred[128,2176]{1,0:T(8,128)(4,1)S(1)} %and_and_fusion.2, bf16[128,10,256]{0,2,1:T(8,128)(2,1)S(1)} %bitcast.98, bf16[4096,512]{1,0:T(8,128)(2,1)} %get-tuple-element.175, s32[]{:T(128)S(6)} %select_n.228), kind=kOutput, calls=%fused_computation.9.clone.1 | convolution fusion | flops 1434417920 | bytes 13194244 | tf_op jit(solution)/shard_map/while/body/eval_jaxpr/thd,kd->thk/dot_general | solution.py:21
  98.6 2.8 %fusion.39 = f32[128,10]{0,1:T(8,128)S(1)} fusion(f32[128,10,2176]{2,0,1:T(8,128)S(1)} %get-tuple-element.145, f32[128,10]{0,1:T(8,128)S(1)} %get-tuple-element.146, pred[128,2176]{1,0:T(8,128)(4,1)S(1)} %and_and_fusion.2), kind=kLoop, calls=%fused_computation.10.clone.1 | loop fusion | flops 11139840 | bytes 11429888 | tf_op jit(solution)/shard_map/while/body/eval_jaxpr/reduce_sum | solution.py:33
  101.3 4.9 %divide_convert_fusion.2 = bf16[128,10,256]{2,0,1:T(8,128)(2,1)S(1)} fusion(bf16[4096,512]{1,0:T(8,128)(2,1)} %get-tuple-element.175, s32[]{:T(128)S(6)} %select_n.228, s32[]{:T(128)S(6)} %add.217, f32[128,10,2176]{2,0,1:T(8,128)S(1)} %get-tuple-element.145, f32[128,10]{0,1:T(8,128)S(1)} %get-tuple-element.146, ...), kind=kOutput, calls=%fused_computation.14.clone.1 | convolution fusion | flops 1437859840 | bytes 13199368 | tf_op jit(solution)/shard_map/while/body/eval_jaxpr/thk,kd->thd/dot_general | solution.py:35
  106.9 0.9 constant_dynamic-update-slice_fusion.2
  107.7 1.8 %copy.55 = bf16[16,8,16,512]{3,2,1,0:T(8,128)(2,1)S(1)} copy(bf16[16,8,16,512]{3,2,0,1:T(8,128)(2,1)} %bitcast.105) | data formatting | bytes 4194304 | tf_op jit(solution)/shard_map/transpose | solution.py:43
  109.6 5.2 %scatter_fusion = bf16[32,128,512]{2,1,0:T(8,128)(2,1)} fusion(bf16[32,128,512]{2,1,0:T(8,128)(2,1)} %copy.75, s32[16]{0:T(128)S(1)} %fusion.28, bf16[16,128,512]{2,1,0:T(8,128)(2,1)S(1)} %bitcast.99), kind=kCustom, calls=%fused_computation.6 | custom fusion | bytes 6291520 | tf_op jit(solution)/shard_map/scatter | solution.py:101
  (66 shorter events, 7.9 us)
Async XLA Ops:
  7.2 4.8 %copy-start.2 = (s32[32,16]{0,1:T(8,128)S(1)}, s32[32,16]{0,1:T(8,128)}, u32[]{:S(2)}) copy-start(s32[32,16]{0,1:T(8,128)} %param.13) | copy-start | bytes 6148
  7.2 4.8 %copy-start.3 = (s32[32,16]{0,1:T(8,128)S(1)}, s32[32,16]{0,1:T(8,128)}, u32[]{:S(2)}) copy-start(s32[32,16]{0,1:T(8,128)} %param.14) | copy-start | bytes 6148
  7.2 38.1 %all-gather.6.cloned.1.call-start = ((), (), s32[]{:S(2)}) async-start(), calls=%async_computation.2 | async-start | bytes 2359296 | tf_op jit(solution)/shard_map/all_gather | solution.py:64
  11.9 44.2 %copy-start.4 = (s32[32]{0:T(128)S(1)}, s32[32]{0:T(128)}, u32[]{:S(2)}) copy-start(s32[32]{0:T(128)} %param.15) | copy-start | bytes 388
  14.7 28.3 %all-to-all-start = ((bf16[32,16,512]{2,1,0:T(8,128)(2,1)}), bf16[32,16,512]{2,1,0:T(8,128)(2,1)S(1)}, u32[]{:S(2)}, u32[]{:S(2)}) async-start(bf16[32,16,512]{2,1,0:T(8,128)(2,1)} %gather_fusion), calls=%async_computation | async-start | bytes 1048576 | tf_op jit(solution)/shard_map/all_to_all | solution.py:78
  26.8 47.4 %all-gather.8.cloned.1.call-start = ((), (), s32[]{:S(2)}) async-start(), calls=%async_computation.3 | async-start | bytes 2359296 | tf_op jit(solution)/shard_map/all_gather | solution.py:80
  46.3 29.7 %copy-start.1 = (bf16[1,2048,512]{2,1,0:T(8,128)(2,1)S(1)}, bf16[1,2048,512]{2,1,0:T(8,128)(2,1)}, u32[]{:S(2)}) copy-start(bf16[1,2048,512]{2,1,0:T(8,128)(2,1)} %all-gather.6.cloned.1.call-done) | copy-start | bytes 6291460
  47.7 24.9 %all-to-all-start.1 = ((bf16[32,16,512]{2,1,0:T(8,128)(2,1)}), bf16[32,16,512]{2,1,0:T(8,128)(2,1)S(1)}, u32[]{:S(2)}, u32[]{:S(2)}) async-start(bf16[32,16,512]{2,1,0:T(8,128)(2,1)} %gather_fusion.2), calls=%async_computation.1 | async-start | bytes 1048576 | tf_op jit(solution)/shard_map/all_to_all | solution.py:93
  56.0 51.8 %all-gather.10.cloned.1.call-start = ((), (), s32[]{:S(2)}) async-start(), calls=%async_computation.4 | async-start | bytes 2359296 | tf_op jit(solution)/shard_map/all_gather | solution.py:99
  76.0 2.2 %copy-start = (bf16[1,256,2560]{2,1,0:T(8,128)(2,1)S(1)}, bf16[1,256,2560]{2,1,0:T(8,128)(2,1)}, u32[]{:S(2)}) copy-start(bf16[1,256,2560]{2,1,0:T(8,128)(2,1)} %param.10) | copy-start | bytes 3932164
Sparse Core Ops, SparseCore 0:
  12.0 31.9 all-gather.5
  45.9 28.2 all-gather.7
  76.1 28.2 all-gather.9

commit v2 on v1

--- a/solution.py
+++ b/solution.py
@@ -1,7 +1,7 @@
 import jax
 import jax.numpy as jnp
 from jax import lax
-from jax.sharding import PartitionSpec as P
+from jax.sharding import Mesh, PartitionSpec as P
 
 
 def earlier_same(owners):
@@ -43,11 +43,24 @@
     return pieces.transpose(1, 0, 2, 3).reshape(pages, groups * piece_rows, width)
 
 
+def spread(pieces, axis_name, count):
+    copies = jnp.broadcast_to(pieces[None], (count,) + pieces.shape)
+    return lax.all_to_all(copies, axis_name, 0, 0, tiled=False)
+
+
+def group_gather(pieces, cores):
+    chips = lax.axis_size("gx")
+    over_chips = spread(pieces, "gx", chips)
+    both = spread(over_chips, "gc", cores)
+    return both.transpose(1, 0, *range(2, both.ndim)).reshape((chips * cores,) + pieces.shape)
+
+
 def shards(queries, new_kv, kv_pool, window_table, append_table, cache_lengths):
     blocks = lax.axis_size("blk")
-    groups = lax.axis_size("group")
+    cores = lax.axis_size("gc")
+    groups = lax.axis_size("gx") * cores
     my_block = lax.axis_index("blk")
-    piece_index = lax.axis_index("group")
+    piece_index = lax.axis_index("gx") * cores + lax.axis_index("gc")
     tok_rows = queries.shape[1]
     per_owner = kv_pool.shape[0]
     page_rows = kv_pool.shape[1]
@@ -61,7 +74,7 @@
     cap_new = (new_pages + blocks - 1) // blocks
     piece_rows = page_rows // groups
     piece_start = piece_index * piece_rows
-    fresh_keys = lax.all_gather(new_kv, "group", axis=1, tiled=True)[0]
+    fresh_keys = lax.all_gather(new_kv, ("gx", "gc"), axis=1, tiled=True)[0]
     append_rows = fresh_keys.shape[0]
 
     win_owner = window_table // per_owner
@@ -77,7 +90,7 @@
     outgoing = pool_piece[send_ids.reshape(-1)]
     received = lax.all_to_all(outgoing, "blk", split_axis=0, concat_axis=0, tiled=True)
     cached_piece = received[arrival]
-    cached = regroup(lax.all_gather(cached_piece, "group", axis=0, tiled=False))
+    cached = regroup(lax.all_gather(cached_piece, ("gx", "gc"), axis=0, tiled=False))
 
     new_owner = append_table // per_owner
     new_rank = earlier_same(new_owner)
@@ -87,8 +100,8 @@
         mine_rank[None, None, :] == jnp.arange(cap_new)[None, :, None]
     )
     page_pick = jnp.sum(jnp.where(dest_wanted, jnp.arange(new_pages)[None, None, :], 0), axis=2)
-    fresh_pages = fresh_keys.reshape(new_pages, page_rows, key_width)
-    fresh_piece = lax.dynamic_slice_in_dim(fresh_pages, piece_start, piece_rows, axis=1)
+    own_pages = new_kv[0].reshape(-1, groups, piece_rows, key_width).transpose(1, 0, 2, 3)
+    fresh_piece = lax.all_to_all(own_pages, ("gx", "gc"), 0, 0, tiled=True).reshape(new_pages, piece_rows, key_width)
     parcels = fresh_piece[page_pick.reshape(-1)]
     arrived = lax.all_to_all(parcels, "blk", split_axis=0, concat_axis=0, tiled=True)
     land_here = new_owner == my_block
@@ -96,7 +109,7 @@
     land_slot = land_source * cap_new + jnp.take_along_axis(new_rank, land_source[None, :], axis=0)[0]
     land_ids = jnp.take_along_axis(append_table % per_owner, land_source[None, :], axis=0)[0]
     land_live = jnp.any(land_here, axis=0)
-    landed = regroup(lax.all_gather(arrived[land_slot], "group", axis=0, tiled=False))
+    landed = regroup(group_gather(arrived[land_slot], cores))
     targets = jnp.where(land_live, land_ids, per_owner)
     new_pool = kv_pool.at[targets].set(landed, mode="drop")
 
@@ -128,13 +141,16 @@
 
 
 def solution(mesh):
+    chip_count = mesh.shape["group"] // 2
+    split = Mesh(mesh.devices.reshape(mesh.shape["blk"], chip_count, 2), ("blk", "gx", "gc"))
+    tokens = ("gx", "gc")
     in_specs = (
-        P("blk", "group", None),
-        P("blk", "group", None),
+        P("blk", tokens, None),
+        P("blk", tokens, None),
         P("blk", None, None),
         P(),
         P(),
         P(),
     )
-    out_specs = (P("blk", "group", None), P("blk", None, None))
-    return jax.shard_map(shards, mesh=mesh, in_specs=in_specs, out_specs=out_specs, check_vma=False)
+    out_specs = (P("blk", tokens, None), P("blk", None, None))
+    return jax.shard_map(shards, mesh=split, in_specs=in_specs, out_specs=out_specs, check_vma=False)

time: 122 us -> 177 us (1.45)
  waiting for transfers between devices: 28.7 us -> 55.8 us
  local copies, waits for them, and re-layouts: 27.7 us -> 35.4 us
  blocking collectives: 0 us -> 6.86 us
  starting transfers between devices: 20.4 us -> 26.2 us
  matrix products: 16.8 us -> 21.9 us
  other arithmetic: 9.91 us -> 11.7 us
    all_to_all x0 -> x2, waiting for transfers between devices: none -> 25.1 us  [the longest x1 18.3 us: spread(): return lax.all_to_all(copies, axis_name, 0, 0, tiled=False)]
    all_to_all x0 -> x2, starting transfers between devices: none -> 10.3 us  [the longest x1 6.72 us: shards(): lax.all_to_all(own_pages, ('gx', 'gc'), 0, 0, tiled=True)]
    while x0 -> x4, local copies, waits for them, and re-layouts: none -> 8.44 us
    all_to_all x0 -> x1, blocking collectives: none -> 6.86 us  [spread(): return lax.all_to_all(copies, axis_name, 0, 0, tiled=False)]
    dot_general x2, matrix products: 9.93 us -> 15.1 us  [attend(): jnp.einsum('thk,kd->thd', weights, keys_use[:, head_size:], preferred_ele...]
    all_to_all x1, starting transfers between devices: 8.29 us -> 3.89 us  [shards(): lax.all_to_all(parcels, 'blk', split_axis=0, concat_axis=0, tiled=True)]
    concatenate x1, other arithmetic: 2.2 us -> 4.02 us  [shards(): jnp.concatenate([cached.reshape(win_rows, key_width), fresh_keys], axis=0)]
  transfers between devices with their start and end apart: 5 -> 6, of which waited for: 3 -> 4; matrix products, arithmetic and copies ran while one was open for 35% -> 8% of each run, Pallas kernels for 0% -> 0%
where the time goes in v2:
time: 177 us; the launch traced here: 176 us
  waiting for transfers between devices  55.8 us (32%)
  local copies, waits for them, and re-layouts  35.4 us (20%)
  starting transfers between devices  26.2 us (15%)
  matrix products  21.9 us (12%)
  between operations  16.5 us (9%)
  other arithmetic  11.7 us (7%)
  blocking collectives  6.86 us (4%)
    all_to_all x1, waiting for transfers between devices, spread(): return lax.all_to_all(copies, axis_name, 0, 0, tiled=False)  18.3 us
    all_to_all x1, waiting for transfers between devices, shards(): lax.all_to_all(outgoing, 'blk', split_axis=0, concat_axis=0, tiled=True)  16 us
    dot_general x2, matrix products, attend(): jnp.einsum('thk,kd->thd', weights, keys_use[:, head_size:], preferred_ele...  15.1 us
    all_to_all x1, waiting for transfers between devices, shards(): lax.all_to_all(parcels, 'blk', split_axis=0, concat_axis=0, tiled=True)  14 us
    all_to_all x1, starting transfers between devices, shards(): lax.all_to_all(outgoing, 'blk', split_axis=0, concat_axis=0, tiled=True)  12 us
    while x4, local copies, waits for them, and re-layouts  8.44 us
    dot_general x2, matrix products, attend(): jnp.einsum('thd,kd->thk', query_rows, keys_use[:, :head_size], preferred_...  6.88 us
    all_to_all x1, blocking collectives, spread(): return lax.all_to_all(copies, axis_name, 0, 0, tiled=False)  6.86 us
  transfers between devices with their start and end apart: 6, of which 4 were waited for; matrix products, arithmetic and copies ran while one was open for 8% of the time, Pallas kernels for 0%

profile of v2, /device:TPU:1, one launch (start us, length us, event | category | flops | bytes accessed | tf_op | source)
XLA Modules:
  0.0 176.0 jit_solution(8638536570058856971)
XLA Ops:
  7.2 4.7 %copy.105 = bf16[32,128,512]{2,1,0:T(8,128)(2,1)} copy(bf16[32,128,512]{2,1,0:T(8,128)(2,1)} %param.12) | data formatting | bytes 8388608
  13.3 1.4 gather_fusion
  14.7 12.0 %all-to-all-start = ((bf16[32,16,512]{2,1,0:T(8,128)(2,1)}), bf16[32,16,512]{2,1,0:T(8,128)(2,1)S(1)}, u32[]{:S(2)}, u32[]{:S(2)}) async-start(bf16[32,16,512]{2,1,0:T(8,128)(2,1)} %gather_fusion), calls=%async_computation | async-start | bytes 1048576 | tf_op jit(solution)/shard_map/all_to_all | solution.py:91
  27.0 16.0 %all-to-all-done = bf16[32,16,512]{2,1,0:T(8,128)(2,1)S(1)} async-done(((bf16[32,16,512]{2,1,0:T(8,128)(2,1)}), bf16[32,16,512]{2,1,0:T(8,128)(2,1)S(1)}, u32[]{:S(2)}, u32[]{:S(2)}) %all-to-all-start) | async-done | bytes 524320 | tf_op jit(solution)/shard_map/all_to_all | solution.py:91
  45.8 6.7 %all-to-all-start.1 = ((bf16[8,2,16,512]{3,2,1,0:T(8,128)(2,1)}), bf16[8,2,16,512]{3,2,1,0:T(8,128)(2,1)S(1)}, u32[]{:S(2)}, u32[]{:S(2)}) async-start(bf16[8,2,16,512]{3,2,1,0:T(8,128)(2,1)} %copy.82), calls=%async_computation.1 | async-start | bytes 524288 | tf_op jit(solution)/shard_map/all_to_all | solution.py:104
  52.8 6.8 %all-to-all-done.1 = bf16[8,2,16,512]{3,2,1,0:T(8,128)(2,1)S(1)} async-done(((bf16[8,2,16,512]{3,2,1,0:T(8,128)(2,1)}), bf16[8,2,16,512]{3,2,1,0:T(8,128)(2,1)S(1)}, u32[]{:S(2)}, u32[]{:S(2)}) %all-to-all-start.1) | async-done | bytes 262176 | tf_op jit(solution)/shard_map/all_to_all | solution.py:104
  59.6 1.4 gather_fusion.2
  61.0 3.9 %all-to-all-start.2 = ((bf16[32,16,512]{2,1,0:T(8,128)(2,1)}), bf16[32,16,512]{2,1,0:T(8,128)(2,1)S(1)}, u32[]{:S(2)}, u32[]{:S(2)}) async-start(bf16[32,16,512]{2,1,0:T(8,128)(2,1)} %gather_fusion.2), calls=%async_computation.2 | async-start | bytes 1048576 | tf_op jit(solution)/shard_map/all_to_all | solution.py:106
  66.3 14.0 %all-to-all-done.2 = bf16[32,16,512]{2,1,0:T(8,128)(2,1)S(1)} async-done(((bf16[32,16,512]{2,1,0:T(8,128)(2,1)}), bf16[32,16,512]{2,1,0:T(8,128)(2,1)S(1)}, u32[]{:S(2)}, u32[]{:S(2)}) %all-to-all-start.2) | async-done | bytes 524320 | tf_op jit(solution)/shard_map/all_to_all | solution.py:106
  81.9 3.5 %all-to-all-start.3 = ((bf16[4,16,16,512]{3,2,1,0:T(8,128)(2,1)}), bf16[4,16,16,512]{3,2,1,0:T(8,128)(2,1)S(1)}, u32[]{:S(2)}, u32[]{:S(2)}) async-start(bf16[4,16,16,512]{3,2,1,0:T(8,128)(2,1)} %broadcast_in_dim.38), calls=%async_computation.3 | async-start | bytes 2097152 | tf_op jit(solution)/shard_map/all_to_all | solution.py:48
  89.0 18.3 %all-to-all-done.3 = bf16[4,16,16,512]{3,2,1,0:T(8,128)(2,1)S(1)} async-done(((bf16[4,16,16,512]{3,2,1,0:T(8,128)(2,1)}), bf16[4,16,16,512]{3,2,1,0:T(8,128)(2,1)S(1)}, u32[]{:S(2)}, u32[]{:S(2)}) %all-to-all-start.3) | async-done | bytes 1048608 | tf_op jit(solution)/shard_map/all_to_all | solution.py:48
  107.6 6.9 %all_to_all.25 = bf16[2,4,16,16,512]{4,3,1,2,0:T(8,128)(2,1)S(1)} all-to-all(bf16[2,4,16,16,512]{4,3,1,2,0:T(8,128)(2,1)S(1)} %broadcast_in_dim.39), channel_id=1, replica_groups=mesh['blk'=32,'gx'=4,'gc'=2] {'gc'}, dimensions={0} | all-to-all | bytes 4194304 | tf_op jit(solution)/shard_map/all_to_all | solution.py:48
  114.9 5.2 %scatter_fusion = bf16[32,128,512]{2,1,0:T(8,128)(2,1)} fusion(bf16[32,128,512]{2,1,0:T(8,128)(2,1)} %copy.105, s32[16]{0:T(128)S(1)} %fusion.28, bf16[16,128,512]{2,1,0:T(8,128)(2,1)S(1)} %bitcast.103), kind=kCustom, calls=%fused_computation.6 | custom fusion | bytes 6291520 | tf_op jit(solution)/shard_map/scatter | solution.py:114
  120.1 1.8 %copy.79 = bf16[16,8,16,512]{3,2,1,0:T(8,128)(2,1)S(1)} copy(bf16[16,8,16,512]{3,2,0,1:T(8,128)(2,1)} %bitcast.108) | data formatting | bytes 4194304 | tf_op jit(solution)/shard_map/transpose | solution.py:43
  121.9 4.0 %pad_maximum_fusion = bf16[4096,512]{1,0:T(8,128)(2,1)} fusion(bf16[2048,512]{1,0:T(8,128)(2,1)} %bitcast.109, bf16[2048,512]{1,0:T(8,128)(2,1)S(1)} %bitcast.105), kind=kLoop, calls=%fused_computation.27 | loop fusion | flops 8388608 | bytes 8388608 | tf_op jit(solution)/shard_map/concatenate | solution.py:116
  126.0 43.2 %while.10 = (s32[]{:T(128)}, bf16[2,128,2560]{2,1,0:T(8,128)(2,1)}, s32[2]{0:T(128)S(1)}, s32[]{:T(128)}, pred[4096]{0:T(1024)(128)(4,1)S(1)}, /*index=5*/bf16[2...) while((s32[]{:T(128)}, bf16[2,128,2560]{2,1,0:T(8,128)(2,1)}, ...), condition=%wide.region_5.6_spmd, body=%wide.region_2.5_spmd.sunk | while | flops 2884534272 | bytes 89246824 | solution.py:138
  128.2 3.4 %fusion.38 = (f32[128,10]{0,1:T(8,128)S(1)}, f32[128,10,2176]{2,0,1:T(8,128)S(1)}) fusion(pred[128,2176]{1,0:T(8,128)(4,1)S(1)} %and_and_fusion.2, bf16[128,10,256]{0,2,1:T(8,128)(2,1)S(1)} %bitcast.102, bf16[4096,512]{1,0:T(8,128)(2,1)} %get-tuple-element.189, s32[]{:T(128)S(6)} %select_n.227), kind=kOutput, calls=%fused_computation.9.clone.1 | convolution fusion | flops 1434417920 | bytes 13194244 | tf_op jit(solution)/shard_map/while/body/eval_jaxpr/thd,kd->thk/dot_general | solution.py:21
  131.6 4.2 %copy-done = f32[128,10,2176]{2,0,1:T(8,128)} copy-done((f32[128,10,2176]{2,0,1:T(8,128)}, f32[128,10,2176]{2,0,1:T(8,128)S(1)}, u32[]{:S(2)}) %copy-start) | copy-done | bytes 11141144 | tf_op jit(solution)/shard_map/while
  135.8 2.8 %fusion.39 = f32[128,10]{0,1:T(8,128)S(1)} fusion(f32[128,10,2176]{2,0,1:T(8,128)S(1)} %get-tuple-element.159, f32[128,10]{0,1:T(8,128)S(1)} %get-tuple-element.160, pred[128,2176]{1,0:T(8,128)(4,1)S(1)} %and_and_fusion.2), kind=kLoop, calls=%fused_computation.10.clone.1 | loop fusion | flops 11139840 | bytes 11429888 | tf_op jit(solution)/shard_map/while/body/eval_jaxpr/reduce_sum | solution.py:33
  138.6 7.5 %divide_convert_fusion.2 = bf16[128,10,256]{2,0,1:T(8,128)(2,1)S(1)} fusion(bf16[4096,512]{1,0:T(8,128)(2,1)} %get-tuple-element.189, s32[]{:T(128)S(6)} %select_n.227, s32[]{:T(128)S(6)} %add.220, f32[128,10,2176]{2,0,1:T(8,128)} %copy-done, f32[128,10]{0,1:T(8,128)S(1)} %get-tuple-element.160, pred[128,2176]{1,0:T(8,128)(4,1)S(1)} %and_and_fusion.2, ...), kind=kOutput, calls=%fused_computation.14.clone.1 | convolution fusion | flops 1437859840 | bytes 13199368 | tf_op jit(solution)/shard_map/while/body/eval_jaxpr/thk,kd->thd/dot_general | solution.py:35
  149.8 3.4 %fusion.38 = (f32[128,10]{0,1:T(8,128)S(1)}, f32[128,10,2176]{2,0,1:T(8,128)S(1)}) fusion(pred[128,2176]{1,0:T(8,128)(4,1)S(1)} %and_and_fusion.2, bf16[128,10,256]{0,2,1:T(8,128)(2,1)S(1)} %bitcast.102, bf16[4096,512]{1,0:T(8,128)(2,1)} %get-tuple-element.189, s32[]{:T(128)S(6)} %select_n.227), kind=kOutput, calls=%fused_computation.9.clone.1 | convolution fusion | flops 1434417920 | bytes 13194244 | tf_op jit(solution)/shard_map/while/body/eval_jaxpr/thd,kd->thk/dot_general | solution.py:21
  153.2 4.2 %copy-done = f32[128,10,2176]{2,0,1:T(8,128)} copy-done((f32[128,10,2176]{2,0,1:T(8,128)}, f32[128,10,2176]{2,0,1:T(8,128)S(1)}, u32[]{:S(2)}) %copy-start) | copy-done | bytes 11141144 | tf_op jit(solution)/shard_map/while
  157.4 2.8 %fusion.39 = f32[128,10]{0,1:T(8,128)S(1)} fusion(f32[128,10,2176]{2,0,1:T(8,128)S(1)} %get-tuple-element.159, f32[128,10]{0,1:T(8,128)S(1)} %get-tuple-element.160, pred[128,2176]{1,0:T(8,128)(4,1)S(1)} %and_and_fusion.2), kind=kLoop, calls=%fused_computation.10.clone.1 | loop fusion | flops 11139840 | bytes 11429888 | tf_op jit(solution)/shard_map/while/body/eval_jaxpr/reduce_sum | solution.py:33
  160.2 7.5 %divide_convert_fusion.2 = bf16[128,10,256]{2,0,1:T(8,128)(2,1)S(1)} fusion(bf16[4096,512]{1,0:T(8,128)(2,1)} %get-tuple-element.189, s32[]{:T(128)S(6)} %select_n.227, s32[]{:T(128)S(6)} %add.220, f32[128,10,2176]{2,0,1:T(8,128)} %copy-done, f32[128,10]{0,1:T(8,128)S(1)} %get-tuple-element.160, pred[128,2176]{1,0:T(8,128)(4,1)S(1)} %and_and_fusion.2, ...), kind=kOutput, calls=%fused_computation.14.clone.1 | convolution fusion | flops 1437859840 | bytes 13199368 | tf_op jit(solution)/shard_map/while/body/eval_jaxpr/thk,kd->thd/dot_general | solution.py:35
  (76 shorter events, 15.6 us)
Async XLA Ops:
  7.2 4.7 %copy-start.3 = (s32[32,16]{0,1:T(8,128)S(1)}, s32[32,16]{0,1:T(8,128)}, u32[]{:S(2)}) copy-start(s32[32,16]{0,1:T(8,128)} %param.13) | copy-start | bytes 6148
  7.2 4.7 %copy-start.4 = (s32[32,16]{0,1:T(8,128)S(1)}, s32[32,16]{0,1:T(8,128)}, u32[]{:S(2)}) copy-start(s32[32,16]{0,1:T(8,128)} %param.14) | copy-start | bytes 6148
  11.8 33.2 %copy-start.2 = (bf16[1,256,512]{2,1,0:T(8,128)(2,1)S(1)}, bf16[1,256,512]{2,1,0:T(8,128)(2,1)}, u32[]{:S(2)}) copy-start(bf16[1,256,512]{2,1,0:T(8,128)(2,1)} %param.11) | copy-start | bytes 786436
  14.7 28.3 %all-to-all-start = ((bf16[32,16,512]{2,1,0:T(8,128)(2,1)}), bf16[32,16,512]{2,1,0:T(8,128)(2,1)S(1)}, u32[]{:S(2)}, u32[]{:S(2)}) async-start(bf16[32,16,512]{2,1,0:T(8,128)(2,1)} %gather_fusion), calls=%async_computation | async-start | bytes 1048576 | tf_op jit(solution)/shard_map/all_to_all | solution.py:91
  26.7 93.4 %all-gather.6.cloned.1.call-start = ((), (), s32[]{:S(2)}) async-start(), calls=%async_computation.6 | async-start | bytes 2359296 | tf_op jit(solution)/shard_map/all_gather | solution.py:93
  44.3 41.2 %copy-start.5 = (s32[32]{0:T(128)S(1)}, s32[32]{0:T(128)}, u32[]{:S(2)}) copy-start(s32[32]{0:T(128)} %param.15) | copy-start | bytes 388
  44.3 77.6 %all-gather.4.cloned.1.call-start = ((), (), s32[]{:S(2)}) async-start(), calls=%async_computation.5 | async-start | bytes 2359296 | tf_op jit(solution)/shard_map/all_gather | solution.py:77
  45.8 13.8 %all-to-all-start.1 = ((bf16[8,2,16,512]{3,2,1,0:T(8,128)(2,1)}), bf16[8,2,16,512]{3,2,1,0:T(8,128)(2,1)S(1)}, u32[]{:S(2)}, u32[]{:S(2)}) async-start(bf16[8,2,16,512]{3,2,1,0:T(8,128)(2,1)} %copy.82), calls=%async_computation.1 | async-start | bytes 524288 | tf_op jit(solution)/shard_map/all_to_all | solution.py:104
  61.0 19.2 %all-to-all-start.2 = ((bf16[32,16,512]{2,1,0:T(8,128)(2,1)}), bf16[32,16,512]{2,1,0:T(8,128)(2,1)S(1)}, u32[]{:S(2)}, u32[]{:S(2)}) async-start(bf16[32,16,512]{2,1,0:T(8,128)(2,1)} %gather_fusion.2), calls=%async_computation.2 | async-start | bytes 1048576 | tf_op jit(solution)/shard_map/all_to_all | solution.py:106
  81.9 25.3 %all-to-all-start.3 = ((bf16[4,16,16,512]{3,2,1,0:T(8,128)(2,1)}), bf16[4,16,16,512]{3,2,1,0:T(8,128)(2,1)S(1)}, u32[]{:S(2)}, u32[]{:S(2)}) async-start(bf16[4,16,16,512]{3,2,1,0:T(8,128)(2,1)} %broadcast_in_dim.38), calls=%async_computation.3 | async-start | bytes 2097152 | tf_op jit(solution)/shard_map/all_to_all | solution.py:48
  121.9 4.0 %copy-start.1 = (bf16[1,256,2560]{2,1,0:T(8,128)(2,1)S(1)}, bf16[1,256,2560]{2,1,0:T(8,128)(2,1)}, u32[]{:S(2)}) copy-start(bf16[1,256,2560]{2,1,0:T(8,128)(2,1)} %param.10) | copy-start | bytes 3932164
  131.6 4.2 %copy-start = (f32[128,10,2176]{2,0,1:T(8,128)}, f32[128,10,2176]{2,0,1:T(8,128)S(1)}, u32[]{:S(2)}) copy-start(f32[128,10,2176]{2,0,1:T(8,128)S(1)} %get-tuple-element.159) | copy-start | bytes 33423364 | tf_op jit(solution)/shard_map/while
  153.2 4.2 %copy-start = (f32[128,10,2176]{2,0,1:T(8,128)}, f32[128,10,2176]{2,0,1:T(8,128)S(1)}, u32[]{:S(2)}) copy-start(f32[128,10,2176]{2,0,1:T(8,128)S(1)} %get-tuple-element.159) | copy-start | bytes 33423364 | tf_op jit(solution)/shard_map/while
Sparse Core Ops, SparseCore 0:
  44.4 26.7 all-gather.5
  73.1 32.1 all-gather.3

commit v3 on v1

--- a/solution.py
+++ b/solution.py
@@ -1,6 +1,10 @@
+import functools
+
 import jax
 import jax.numpy as jnp
 from jax import lax
+from jax.experimental import pallas as pl
+from jax.experimental.pallas import tpu as pltpu
 from jax.sharding import PartitionSpec as P
 
 
@@ -41,6 +45,91 @@
 def regroup(pieces):
     groups, pages, piece_rows, width = pieces.shape
     return pieces.transpose(1, 0, 2, 3).reshape(pages, groups * piece_rows, width)
+
+
+def window_kernel(meta, q_ref, cached_hbm, fresh_hbm, out_ref, keys, bias, sems, *, chunk, chunks,
+                  split, head_count, head_size, window_len):
+    first = meta[0]
+    live_from = meta[1]
+
+    def chunk_copy(c, begin):
+        j = first + c
+
+        @pl.when(j < split)
+        def _():
+            cp = pltpu.make_async_copy(
+                cached_hbm.at[pl.ds(j * chunk, chunk)], keys.at[pl.ds(c * chunk, chunk)], sems.at[c]
+            )
+            cp.start() if begin else cp.wait()
+
+        @pl.when(j >= split)
+        def _():
+            cp = pltpu.make_async_copy(
+                fresh_hbm.at[pl.ds((j - split) * chunk, chunk)], keys.at[pl.ds(c * chunk, chunk)], sems.at[c]
+            )
+            cp.start() if begin else cp.wait()
+
+    for c in range(chunks):
+        chunk_copy(c, True)
+    rows = lax.broadcasted_iota(jnp.int32, bias.shape, 0)
+    cols = lax.broadcasted_iota(jnp.int32, bias.shape, 1)
+    allowed = (cols > rows) & (cols <= rows + window_len) & (cols >= live_from)
+    bias[...] = jnp.where(allowed, 0.0, -jnp.inf).astype(jnp.float32)
+    for c in range(chunks):
+        chunk_copy(c, False)
+    scale = head_size ** (-0.5)
+
+    def one_head(h, carry):
+        lanes = pl.ds(pl.multiple_of(h * head_size, head_size), head_size)
+        scores = lax.dot_general(
+            q_ref[:, lanes], keys[:, :head_size], (((1,), (1,)), ((), ())),
+            preferred_element_type=jnp.float32,
+        )
+        scores = scores * scale + bias[...]
+        row_max = jnp.max(scores, axis=1, keepdims=True)
+        raw_weights = jnp.exp(scores - row_max)
+        row_total = jnp.sum(raw_weights, axis=1, keepdims=True)
+        weighted = jnp.dot(
+            raw_weights.astype(jnp.bfloat16), keys[:, head_size:], preferred_element_type=jnp.float32
+        )
+        out_ref[:, lanes] = (weighted / row_total).astype(out_ref.dtype)
+        return carry
+
+    lax.fori_loop(0, head_count, one_head, 0)
+
+
+def window_attention(query_rows, cached, fresh, first_chunk, live_from, head_count, head_size, window_len):
+    tok_rows, width = query_rows.shape
+    chunk = tok_rows
+    span = window_len + tok_rows
+    chunks = span // chunk
+    split = cached.shape[0] // chunk
+    key_width = cached.shape[1]
+    body = functools.partial(
+        window_kernel, chunk=chunk, chunks=chunks, split=split, head_count=head_count,
+        head_size=head_size, window_len=window_len,
+    )
+    meta = jnp.stack([first_chunk, live_from]).astype(jnp.int32)
+    return pl.pallas_call(
+        body,
+        out_shape=jax.ShapeDtypeStruct((tok_rows, width), query_rows.dtype),
+        grid_spec=pltpu.PrefetchScalarGridSpec(
+            num_scalar_prefetch=1,
+            grid=(1,),
+            in_specs=[
+                pl.BlockSpec((tok_rows, width), lambda i, m: (0, 0)),
+                pl.BlockSpec(memory_space=pl.ANY),
+                pl.BlockSpec(memory_space=pl.ANY),
+            ],
+            out_specs=pl.BlockSpec((tok_rows, width), lambda i, m: (0, 0)),
+            scratch_shapes=[
+                pltpu.VMEM((span, key_width), cached.dtype),
+                pltpu.VMEM((tok_rows, span), jnp.float32),
+                pltpu.SemaphoreType.DMA((chunks,)),
+            ],
+        ),
+        compiler_params=pltpu.CompilerParams(vmem_limit_bytes=48 * 1024 * 1024),
+    )(meta, query_rows, cached, fresh)
 
 
 def shards(queries, new_kv, kv_pool, window_table, append_table, cache_lengths):
@@ -100,29 +189,14 @@
     targets = jnp.where(land_live, land_ids, per_owner)
     new_pool = kv_pool.at[targets].set(landed, mode="drop")
 
-    keys_all = jnp.concatenate([cached.reshape(win_rows, key_width), fresh_keys], axis=0)
     own_length = lax.dynamic_index_in_dim(cache_lengths, my_block, 0, keepdims=False)
     filled = jnp.minimum(own_length // page_rows, win_pages)
-    key_index = jnp.arange(win_rows + append_rows)
-    live_keys = (key_index >= win_rows) | (key_index // page_rows >= win_pages - filled)
-    block_len = min(128, tok_rows)
-    block_count = tok_rows // block_len
-    query_blocks = queries[0].reshape(block_count, block_len, queries.shape[2])
     first_row = piece_index * tok_rows
-    offsets = jnp.arange(block_count) * block_len
-    span = win_rows + block_len
-
-    def one_block(inputs):
-        qblock, offset = inputs
-        block_start = first_row + offset
-        keys_use = lax.dynamic_slice_in_dim(keys_all, block_start, span, 0)
-        index_use = block_start + jnp.arange(span)
-        live_use = lax.dynamic_slice_in_dim(live_keys, block_start, span, 0)
-        return attend(
-            qblock, keys_use, index_use, live_use, block_start, head_count, head_size, win_rows
-        )
-
-    attended = lax.map(one_block, (query_blocks, offsets))
+    live_from = (win_pages - filled) * page_rows - first_row
+    attended = window_attention(
+        queries[0], cached.reshape(win_rows, key_width), fresh_keys, piece_index, live_from,
+        head_count, head_size, win_rows,
+    )
     attn_out = attended.reshape(1, tok_rows, queries.shape[2])
     return (attn_out, new_pool)
 

time: 122 us -> 118 us (0.967)
  Pallas kernels: 0 us -> 20.4 us
  matrix products: 16.8 us -> 0 us
  other arithmetic: 9.91 us -> 1.6 us
  waiting for transfers between devices: 28.7 us -> 34.8 us
  local copies, waits for them, and re-layouts: 27.7 us -> 23.4 us
  loops' own time: 1.4 us -> 0 us
    pallas_call x0 -> x1, Pallas kernels: none -> 20.4 us  [window_attention(): pl.pallas_call(body, out_shape=jax.ShapeDtypeStruct((tok_rows, width), qu...]
    dot_general x4 -> x0, matrix products: 16.8 us -> none  [the longest x2 9.93 us: attend(): jnp.einsum('thk,kd->thd', weights, keys_use[:, head_size:], preferred_ele...]
    reduce_sum x2 -> x0, other arithmetic: 5.53 us -> none  [attend(): row_total = jnp.sum(raw_weights, axis=2, keepdims=True)]
    all_gather x1, waiting for transfers between devices: 0.01 us -> 3.53 us  [shards(): lax.all_gather(arrived[land_slot], 'group', axis=0, tiled=False)]
    all_to_all x1, waiting for transfers between devices: 12.3 us -> 15.2 us  [shards(): lax.all_to_all(parcels, 'blk', split_axis=0, concat_axis=0, tiled=True)]
    dynamic_update_slice x4 -> x0, local copies, waits for them, and re-layouts: 2.27 us -> none  [shards(): attended = lax.map(one_block, (query_blocks, offsets))]
    concatenate x1 -> x0, other arithmetic: 2.2 us -> none  [shards(): jnp.concatenate([cached.reshape(win_rows, key_width), fresh_keys], axis=0)]
    dynamic_slice x8 -> x0, local copies, waits for them, and re-layouts: 2.13 us -> none  [the longest x6 1.96 us: shards(): attended = lax.map(one_block, (query_blocks, offsets))]
  transfers between devices with their start and end apart: 5 -> 5, of which waited for: 3 -> 3; matrix products, arithmetic and copies ran while one was open for 35% -> 11% of each run, Pallas kernels for 0% -> 17%
where the time goes in v3:
time: 118 us
  waiting for transfers between devices  34.8 us (29%)
  local copies, waits for them, and re-layouts  23.4 us (20%)
  starting transfers between devices  21.1 us (18%)
  Pallas kernels  20.4 us (17%)
  between operations  16.5 us (14%)
  other arithmetic  1.6 us (1%)
    pallas_call x1, Pallas kernels, window_attention(): pl.pallas_call(body, out_shape=jax.ShapeDtypeStruct((tok_rows, width), qu...  20.4 us
    all_to_all x1, waiting for transfers between devices, shards(): lax.all_to_all(outgoing, 'blk', split_axis=0, concat_axis=0, tiled=True)  16 us
    all_to_all x1, waiting for transfers between devices, shards(): lax.all_to_all(parcels, 'blk', split_axis=0, concat_axis=0, tiled=True)  15.2 us
    all_to_all x1, starting transfers between devices, shards(): lax.all_to_all(outgoing, 'blk', split_axis=0, concat_axis=0, tiled=True)  12 us
    all_to_all x1, starting transfers between devices, shards(): lax.all_to_all(parcels, 'blk', split_axis=0, concat_axis=0, tiled=True)  8.94 us
    unnamed x11, local copies, waits for them, and re-layouts  5.23 us
    scatter x1, local copies, waits for them, and re-layouts, shards(): new_pool = kv_pool.at[targets].set(landed, mode='drop')  5.15 us
    all_gather x1, waiting for transfers between devices, shards(): lax.all_gather(arrived[land_slot], 'group', axis=0, tiled=False)  3.53 us
  transfers between devices with their start and end apart: 5, of which 3 were waited for; matrix products, arithmetic and copies ran while one was open for 11% of the time, Pallas kernels for 17%

profile of v3, /device:TPU:1, one launch (start us, length us, event | category | flops | bytes accessed | tf_op | source)
XLA Modules:
  0.0 117.9 jit_solution(87254063582537471)
XLA Ops:
  7.2 4.6 %copy.33 = bf16[32,128,512]{2,1,0:T(8,128)(2,1)} copy(bf16[32,128,512]{2,1,0:T(8,128)(2,1)} %param.10) | data formatting | bytes 8388608
  12.3 1.1 constant_dynamic-slice_fusion.1
  13.4 1.4 %gather_fusion = bf16[32,16,512]{2,1,0:T(8,128)(2,1)} fusion(bf16[32,16,512]{2,1,0:T(8,128)(2,1)S(1)} %constant_dynamic-slice_fusion.1, s32[1024]{0:T(1024)S(1)} %pad_clamp_fusion.3), kind=kCustom, calls=%fused_computation.2 | custom fusion | bytes 1048704 | tf_op jit(solution)/shard_map/gather | solution.py:166
  14.7 12.0 %all-to-all-start = ((bf16[32,16,512]{2,1,0:T(8,128)(2,1)}), bf16[32,16,512]{2,1,0:T(8,128)(2,1)S(1)}, u32[]{:S(2)}, u32[]{:S(2)}) async-start(bf16[32,16,512]{2,1,0:T(8,128)(2,1)} %gather_fusion), calls=%async_computation | async-start | bytes 1048576 | tf_op jit(solution)/shard_map/all_to_all | solution.py:167
  26.8 0.2 dynamic-slice_reduce_fusion
  27.0 16.0 %all-to-all-done = bf16[32,16,512]{2,1,0:T(8,128)(2,1)S(1)} async-done(((bf16[32,16,512]{2,1,0:T(8,128)(2,1)}), bf16[32,16,512]{2,1,0:T(8,128)(2,1)S(1)}, u32[]{:S(2)}, u32[]{:S(2)}) %all-to-all-start) | async-done | bytes 524320 | tf_op jit(solution)/shard_map/all_to_all | solution.py:167
  43.0 1.3 %gather_fusion.1 = bf16[16,16,512]{2,1,0:T(8,128)(2,1)} fusion(bf16[32,16,512]{2,1,0:T(8,128)(2,1)S(1)} %all-to-all-done, s32[1024]{0:T(1024)S(1)} %pad_clamp_fusion.2), kind=kCustom, calls=%fused_computation.3 | custom fusion | bytes 524352 | tf_op jit(solution)/shard_map/gather | solution.py:168
  44.3 0.2 fusion.5
  44.7 1.0 constant_dynamic-slice_fusion
  45.7 1.4 %gather_fusion.2 = bf16[32,16,512]{2,1,0:T(8,128)(2,1)} fusion(bf16[16,16,512]{2,1,0:T(8,128)(2,1)S(1)} %constant_dynamic-slice_fusion, s32[1024]{0:T(1024)S(1)} %pad_clamp_fusion.1), kind=kCustom, calls=%fused_computation.4 | custom fusion | bytes 1048704 | tf_op jit(solution)/shard_map/gather | solution.py:181
  47.0 8.9 %all-to-all-start.1 = ((bf16[32,16,512]{2,1,0:T(8,128)(2,1)}), bf16[32,16,512]{2,1,0:T(8,128)(2,1)S(1)}, u32[]{:S(2)}, u32[]{:S(2)}) async-start(bf16[32,16,512]{2,1,0:T(8,128)(2,1)} %gather_fusion.2), calls=%async_computation.1 | async-start | bytes 1048576 | tf_op jit(solution)/shard_map/all_to_all | solution.py:182
  56.0 0.7 iota_reduce_fusion
  56.7 0.7 gather_fusion.5
  57.4 15.2 %all-to-all-done.1 = bf16[32,16,512]{2,1,0:T(8,128)(2,1)S(1)} async-done(((bf16[32,16,512]{2,1,0:T(8,128)(2,1)}), bf16[32,16,512]{2,1,0:T(8,128)(2,1)S(1)}, u32[]{:S(2)}, u32[]{:S(2)}) %all-to-all-start.1) | async-done | bytes 524320 | tf_op jit(solution)/shard_map/all_to_all | solution.py:182
  72.6 1.3 %gather_fusion.3 = bf16[16,16,512]{2,1,0:T(8,128)(2,1)} fusion(bf16[32,16,512]{2,1,0:T(8,128)(2,1)S(1)} %all-to-all-done.1, s32[1024]{0:T(1024)S(1)} %pad_clamp_fusion), kind=kCustom, calls=%fused_computation.5 | custom fusion | bytes 524352 | tf_op jit(solution)/shard_map/gather | solution.py:188
  73.9 0.6 dynamic_slice.25
  77.1 0.7 gather_fusion.4
  77.9 2.0 %copy.29 = bf16[8,16,16,512]{3,2,0,1:T(8,128)(2,1)S(1)} copy(bf16[8,16,16,512]{3,2,1,0:T(8,128)(2,1)} %bitcast.74) | data formatting | bytes 4194304 | tf_op jit(solution)/shard_map/all_gather | solution.py:169
  79.8 0.2 copy-done
  80.1 0.4 copy-done.1
  80.4 20.4 %shard_map.77 = bf16[256,2560]{1,0:T(8,128)(2,1)} custom-call(s32[2]{0:T(128)S(1)} %pad_add_fusion.meta, bf16[256,2560]{1,0:T(8,128)(2,1)S(1)} %bitcast.72, bf16[2048,512]{1,0:T(8,128)(2,1)S(1)} %bitcast.69, bf16[2048,512]{1,0:T(8,128)(2,1)S(1)} %bitcast.71), custom_call_target="tpu_custom_call" | custom-call | tf_op jit(solution)/shard_map/pallas_call | solution.py:113
  100.8 3.5 %all-gather.10.cloned.1.call-done = bf16[128,16,512]{2,1,0:T(8,128)(2,1)} async-done(((bf16[16,16,512]{2,1,0:T(8,128)(2,1)}), bf16[128,16,512]{2,1,0:T(8,128)(2,1)}) %all-gather.10.cloned.1.call-update) | async-done | bytes 2097168 | tf_op jit(solution)/shard_map/all_gather | solution.py:188
  104.3 1.8 %copy.30 = bf16[16,8,16,512]{3,2,1,0:T(8,128)(2,1)S(1)} copy(bf16[16,8,16,512]{3,2,0,1:T(8,128)(2,1)} %bitcast.75) | data formatting | bytes 4194304 | tf_op jit(solution)/shard_map/transpose | solution.py:47
  106.2 5.2 %scatter_fusion = bf16[32,128,512]{2,1,0:T(8,128)(2,1)} fusion(bf16[32,128,512]{2,1,0:T(8,128)(2,1)} %copy.33, s32[16]{0:T(128)S(1)} %fusion.11, bf16[16,128,512]{2,1,0:T(8,128)(2,1)S(1)} %bitcast.73), kind=kCustom, calls=%fused_computation.6 | custom fusion | bytes 6291520 | tf_op jit(solution)/shard_map/scatter | solution.py:190
  (37 shorter events, 0.8 us)
Async XLA Ops:
  7.2 4.8 %copy-start.2 = (s32[32,16]{0,1:T(8,128)S(1)}, s32[32,16]{0,1:T(8,128)}, u32[]{:S(2)}) copy-start(s32[32,16]{0,1:T(8,128)} %param.11) | copy-start | bytes 6148
  7.2 4.8 %copy-start.3 = (s32[32,16]{0,1:T(8,128)S(1)}, s32[32,16]{0,1:T(8,128)}, u32[]{:S(2)}) copy-start(s32[32,16]{0,1:T(8,128)} %param.12) | copy-start | bytes 6148
  7.2 37.5 %all-gather.6.cloned.1.call-start = ((), (), s32[]{:S(2)}) async-start(), calls=%async_computation.2 | async-start | bytes 2359296 | tf_op jit(solution)/shard_map/all_gather | solution.py:153
  14.7 28.3 %all-to-all-start = ((bf16[32,16,512]{2,1,0:T(8,128)(2,1)}), bf16[32,16,512]{2,1,0:T(8,128)(2,1)S(1)}, u32[]{:S(2)}, u32[]{:S(2)}) async-start(bf16[32,16,512]{2,1,0:T(8,128)(2,1)} %gather_fusion), calls=%async_computation | async-start | bytes 1048576 | tf_op jit(solution)/shard_map/all_to_all | solution.py:167
  26.8 51.1 %all-gather.8.cloned.1.call-start = ((), (), s32[]{:S(2)}) async-start(), calls=%async_computation.3 | async-start | bytes 2359296 | tf_op jit(solution)/shard_map/all_gather | solution.py:169
  44.3 29.5 %copy-start.4 = (s32[32]{0:T(128)S(1)}, s32[32]{0:T(128)}, u32[]{:S(2)}) copy-start(s32[32]{0:T(128)} %param.13) | copy-start | bytes 388
  47.0 25.5 %all-to-all-start.1 = ((bf16[32,16,512]{2,1,0:T(8,128)(2,1)}), bf16[32,16,512]{2,1,0:T(8,128)(2,1)S(1)}, u32[]{:S(2)}, u32[]{:S(2)}) async-start(bf16[32,16,512]{2,1,0:T(8,128)(2,1)} %gather_fusion.2), calls=%async_computation.1 | async-start | bytes 1048576 | tf_op jit(solution)/shard_map/all_to_all | solution.py:182
  56.0 48.4 %all-gather.10.cloned.1.call-start = ((), (), s32[]{:S(2)}) async-start(), calls=%async_computation.4 | async-start | bytes 2359296 | tf_op jit(solution)/shard_map/all_gather | solution.py:188
  77.8 2.2 %copy-start = (bf16[1,2048,512]{2,1,0:T(8,128)(2,1)S(1)}, bf16[1,2048,512]{2,1,0:T(8,128)(2,1)}, u32[]{:S(2)}) copy-start(bf16[1,2048,512]{2,1,0:T(8,128)(2,1)} %all-gather.6.cloned.1.call-done) | copy-start | bytes 6291460
  77.9 2.6 %copy-start.1 = (bf16[1,256,2560]{2,1,0:T(8,128)(2,1)S(1)}, bf16[1,256,2560]{2,1,0:T(8,128)(2,1)}, u32[]{:S(2)}) copy-start(bf16[1,256,2560]{2,1,0:T(8,128)(2,1)} %param.8) | copy-start | bytes 3932164
Sparse Core Ops, SparseCore 0:
  12.0 31.9 all-gather.5
  45.9 28.2 all-gather.7
  76.1 28.2 all-gather.9

commit v4 on v3

--- a/solution.py
+++ b/solution.py
@@ -49,6 +49,9 @@
 
 def window_kernel(meta, q_ref, cached_hbm, fresh_hbm, out_ref, keys, bias, sems, *, chunk, chunks,
                   split, head_count, head_size, window_len):
+    groups, _, piece_rows, _ = cached_hbm.shape
+    page_rows = groups * piece_rows
+    pages_per_chunk = chunk // page_rows
     first = meta[0]
     live_from = meta[1]
 
@@ -57,10 +60,18 @@
 
         @pl.when(j < split)
         def _():
-            cp = pltpu.make_async_copy(
-                cached_hbm.at[pl.ds(j * chunk, chunk)], keys.at[pl.ds(c * chunk, chunk)], sems.at[c]
-            )
-            cp.start() if begin else cp.wait()
+            if begin:
+                for p in range(pages_per_chunk):
+                    for grp in range(groups):
+                        pltpu.make_async_copy(
+                            cached_hbm.at[grp, j * pages_per_chunk + p],
+                            keys.at[pl.ds(c * chunk + p * page_rows + grp * piece_rows, piece_rows)],
+                            sems.at[c],
+                        ).start()
+            else:
+                pltpu.make_async_copy(
+                    fresh_hbm.at[pl.ds(0, chunk)], keys.at[pl.ds(c * chunk, chunk)], sems.at[c]
+                ).wait()
 
         @pl.when(j >= split)
         def _():
@@ -103,8 +114,8 @@
     chunk = tok_rows
     span = window_len + tok_rows
     chunks = span // chunk
-    split = cached.shape[0] // chunk
-    key_width = cached.shape[1]
+    groups, pages, piece_rows, key_width = cached.shape
+    split = pages * groups * piece_rows // chunk
     body = functools.partial(
         window_kernel, chunk=chunk, chunks=chunks, split=split, head_count=head_count,
         head_size=head_size, window_len=window_len,
@@ -132,6 +143,46 @@
     )(meta, query_rows, cached, fresh)
 
 
+def pool_kernel(source, pool_hbm, landed_hbm, out_hbm, sems):
+    groups, _, piece_rows, _ = landed_hbm.shape
+    for page in range(pool_hbm.shape[0]):
+        picked = source[page]
+
+        @pl.when(picked < 0)
+        def _():
+            pltpu.make_async_copy(pool_hbm.at[page], out_hbm.at[page], sems.at[page]).start()
+
+        @pl.when(picked >= 0)
+        def _():
+            for grp in range(groups):
+                pltpu.make_async_copy(
+                    landed_hbm.at[grp, picked],
+                    out_hbm.at[page, pl.ds(grp * piece_rows, piece_rows)],
+                    sems.at[page],
+                ).start()
+
+    for page in range(pool_hbm.shape[0]):
+        pltpu.make_async_copy(pool_hbm.at[page], out_hbm.at[page], sems.at[page]).wait()
+
+
+def write_pool(kv_pool, landed_pieces, targets):
+    pages = kv_pool.shape[0]
+    source = jnp.full((pages,), -1, jnp.int32).at[targets].set(
+        jnp.arange(targets.shape[0], dtype=jnp.int32), mode="drop"
+    )
+    return pl.pallas_call(
+        pool_kernel,
+        out_shape=jax.ShapeDtypeStruct(kv_pool.shape, kv_pool.dtype),
+        grid_spec=pltpu.PrefetchScalarGridSpec(
+            num_scalar_prefetch=1,
+            grid=(1,),
+            in_specs=[pl.BlockSpec(memory_space=pl.ANY), pl.BlockSpec(memory_space=pl.ANY)],
+            out_specs=pl.BlockSpec(memory_space=pl.ANY),
+            scratch_shapes=[pltpu.SemaphoreType.DMA((pages,))],
+        ),
+    )(source, kv_pool, landed_pieces)
+
+
 def shards(queries, new_kv, kv_pool, window_table, append_table, cache_lengths):
     blocks = lax.axis_size("blk")
     groups = lax.axis_size("group")
@@ -166,7 +217,7 @@
     outgoing = pool_piece[send_ids.reshape(-1)]
     received = lax.all_to_all(outgoing, "blk", split_axis=0, concat_axis=0, tiled=True)
     cached_piece = received[arrival]
-    cached = regroup(lax.all_gather(cached_piece, "group", axis=0, tiled=False))
+    cached_pieces = lax.all_gather(cached_piece, "group", axis=0, tiled=False)
 
     new_owner = append_table // per_owner
     new_rank = earlier_same(new_owner)
@@ -185,16 +236,16 @@
     land_slot = land_source * cap_new + jnp.take_along_axis(new_rank, land_source[None, :], axis=0)[0]
     land_ids = jnp.take_along_axis(append_table % per_owner, land_source[None, :], axis=0)[0]
     land_live = jnp.any(land_here, axis=0)
-    landed = regroup(lax.all_gather(arrived[land_slot], "group", axis=0, tiled=False))
+    landed = lax.all_gather(arrived[land_slot], "group", axis=0, tiled=False)
     targets = jnp.where(land_live, land_ids, per_owner)
-    new_pool = kv_pool.at[targets].set(landed, mode="drop")
+    new_pool = write_pool(kv_pool, landed, targets)
 
     own_length = lax.dynamic_index_in_dim(cache_lengths, my_block, 0, keepdims=False)
     filled = jnp.minimum(own_length // page_rows, win_pages)
     first_row = piece_index * tok_rows
     live_from = (win_pages - filled) * page_rows - first_row
     attended = window_attention(
-        queries[0], cached.reshape(win_rows, key_width), fresh_keys, piece_index, live_from,
+        queries[0], cached_pieces, fresh_keys, piece_index, live_from,
         head_count, head_size, win_rows,
     )
     attn_out = attended.reshape(1, tok_rows, queries.shape[2])

time: 118 us -> 241 us (2.04)
  Pallas kernels: 20.4 us -> 152 us
  local copies, waits for them, and re-layouts: 23.4 us -> 14.9 us
  waiting for transfers between devices: 34.8 us -> 32 us
    pallas_call x0 -> x1, Pallas kernels: none -> 129 us  [write_pool(): pl.pallas_call(pool_kernel, out_shape=jax.ShapeDtypeStruct(kv_pool.shape,...]
    scatter x1, local copies, waits for them, and re-layouts: 5.15 us -> 1.18 us  [write_pool(): jnp.full((pages,), -1, jnp.int32).at[targets]]
    unnamed x11 -> x10, local copies, waits for them, and re-layouts: 5.23 us -> 1.6 us
    all_gather x2, waiting for transfers between devices: 3.55 us -> 0.02 us  [the longest x1 0.02 us: shards(): landed = lax.all_gather(arrived[land_slot], 'group', axis=0, tiled=False)]
  transfers between devices with their start and end apart: 5 -> 5, of which waited for: 3 -> 2; matrix products, arithmetic and copies ran while one was open for 11% -> 7% of each run, Pallas kernels for 17% -> 9%
where the time goes in v4:
time: 241 us; the launch traced here: 240 us
  Pallas kernels  152 us (63%)
  waiting for transfers between devices  32 us (13%)
  starting transfers between devices  21 us (9%)
  between operations  16.5 us (7%)
  local copies, waits for them, and re-layouts  14.9 us (6%)
  other arithmetic  3.64 us (2%)
    pallas_call x1, Pallas kernels, write_pool(): pl.pallas_call(pool_kernel, out_shape=jax.ShapeDtypeStruct(kv_pool.shape,...  129 us
    pallas_call x1, Pallas kernels, window_attention(): pl.pallas_call(body, out_shape=jax.ShapeDtypeStruct((tok_rows, width), qu...  22.7 us
    all_to_all x1, waiting for transfers between devices, shards(): lax.all_to_all(outgoing, 'blk', split_axis=0, concat_axis=0, tiled=True)  16 us
    all_to_all x1, waiting for transfers between devices, shards(): lax.all_to_all(parcels, 'blk', split_axis=0, concat_axis=0, tiled=True)  15.2 us
    all_to_all x1, starting transfers between devices, shards(): lax.all_to_all(outgoing, 'blk', split_axis=0, concat_axis=0, tiled=True)  12 us
    all_to_all x1, starting transfers between devices, shards(): lax.all_to_all(parcels, 'blk', split_axis=0, concat_axis=0, tiled=True)  8.82 us
  transfers between devices with their start and end apart: 5, of which 2 were waited for; matrix products, arithmetic and copies ran while one was open for 7% of the time, Pallas kernels for 9%

profile of v4, /device:TPU:1, one launch (start us, length us, event | category | flops | bytes accessed | tf_op | source)
XLA Modules:
  0.0 239.7 jit_solution(11374131958619541742)
XLA Ops:
  7.2 0.7 all-gather.6.cloned.1.call-update
  7.9 0.7 add_select_fusion.3
  8.6 0.8 fusion.15
  9.6 0.7 fusion.1
  10.3 1.1 constant_dynamic-slice_fusion.1
  11.4 1.4 gather_fusion
  12.8 12.0 %all-to-all-start = ((bf16[32,16,512]{2,1,0:T(8,128)(2,1)}), bf16[32,16,512]{2,1,0:T(8,128)(2,1)S(1)}, u32[]{:S(2)}, u32[]{:S(2)}) async-start(bf16[32,16,512]{2,1,0:T(8,128)(2,1)} %gather_fusion), calls=%async_computation | async-start | bytes 1048576 | tf_op jit(solution)/shard_map/all_to_all | solution.py:218
  24.9 0.2 dynamic-slice_reduce_fusion
  25.1 16.0 %all-to-all-done = bf16[32,16,512]{2,1,0:T(8,128)(2,1)S(1)} async-done(((bf16[32,16,512]{2,1,0:T(8,128)(2,1)}), bf16[32,16,512]{2,1,0:T(8,128)(2,1)S(1)}, u32[]{:S(2)}, u32[]{:S(2)}) %all-to-all-start) | async-done | bytes 524320 | tf_op jit(solution)/shard_map/all_to_all | solution.py:218
  41.1 1.3 gather_fusion.1
  42.4 0.2 fusion.5
  42.7 1.7 constant_dynamic-slice_fusion
  44.4 2.5 %gather_fusion.2 = bf16[32,16,512]{2,1,0:T(8,128)(2,1)} fusion(bf16[16,16,512]{2,1,0:T(8,128)(2,1)} %constant_dynamic-slice_fusion, s32[1024]{0:T(1024)S(1)} %pad_clamp_fusion.1), kind=kCustom, calls=%fused_computation.4 | custom fusion | bytes 1048704 | tf_op jit(solution)/shard_map/gather | solution.py:232
  46.9 8.8 %all-to-all-start.1 = ((bf16[32,16,512]{2,1,0:T(8,128)(2,1)}), bf16[32,16,512]{2,1,0:T(8,128)(2,1)}, u32[]{:S(2)}, u32[]{:S(2)}) async-start(bf16[32,16,512]{2,1,0:T(8,128)(2,1)} %gather_fusion.2), calls=%async_computation.1 | async-start | bytes 1048576 | tf_op jit(solution)/shard_map/all_to_all | solution.py:233
  55.8 0.6 iota_reduce_fusion
  56.4 0.7 gather_fusion.5
  57.1 15.2 %all-to-all-done.1 = bf16[32,16,512]{2,1,0:T(8,128)(2,1)} async-done(((bf16[32,16,512]{2,1,0:T(8,128)(2,1)}), bf16[32,16,512]{2,1,0:T(8,128)(2,1)}, u32[]{:S(2)}, u32[]{:S(2)}) %all-to-all-start.1) | async-done | bytes 524320 | tf_op jit(solution)/shard_map/all_to_all | solution.py:233
  72.3 2.3 gather_fusion.3
  74.6 0.6 dynamic_slice.25
  77.8 0.7 gather_fusion.4
  78.5 1.2 scatter_custom_fusion.source
  79.8 1.6 copy-done.1
  81.4 22.7 %shard_map.77 = bf16[256,2560]{1,0:T(8,128)(2,1)} custom-call(s32[2]{0:T(128)S(1)} %pad_add_fusion.meta, bf16[256,2560]{1,0:T(8,128)(2,1)S(1)} %bitcast.66, bf16[8,16,16,512]{3,2,1,0:T(8,128)(2,1)S(1)} %bitcast.65, bf16[2048,512]{1,0:T(8,128)(2,1)S(1)} %bitcast.64), custom_call_target="tpu_custom_call" | custom-call | tf_op jit(solution)/shard_map/pallas_call | solution.py:124
  104.1 129.1 %shard_map.78 = bf16[32,128,512]{2,1,0:T(8,128)(2,1)} custom-call(s32[32]{0:T(128)} %scatter_custom_fusion.source, bf16[32,128,512]{2,1,0:T(8,128)(2,1)} %pool_hbm.1, bf16[8,16,16,512]{3,2,1,0:T(8,128)(2,1)} %bitcast.67), custom_call_target="tpu_custom_call" | custom-call | tf_op jit(solution)/shard_map/pallas_call | solution.py:173
  (36 shorter events, 0.6 us)
Async XLA Ops:
  7.2 35.6 %all-gather.6.cloned.1.call-start = ((), (), s32[]{:S(2)}) async-start(), calls=%async_computation.2 | async-start | bytes 2359296 | tf_op jit(solution)/shard_map/all_gather | solution.py:204
  12.8 28.3 %all-to-all-start = ((bf16[32,16,512]{2,1,0:T(8,128)(2,1)}), bf16[32,16,512]{2,1,0:T(8,128)(2,1)S(1)}, u32[]{:S(2)}, u32[]{:S(2)}) async-start(bf16[32,16,512]{2,1,0:T(8,128)(2,1)} %gather_fusion), calls=%async_computation | async-start | bytes 1048576 | tf_op jit(solution)/shard_map/all_to_all | solution.py:218
  24.8 54.9 %all-gather.8.cloned.1.call-start = ((), (), s32[]{:S(2)}) async-start(), calls=%async_computation.3 | async-start | bytes 2359296 | tf_op jit(solution)/shard_map/all_gather | solution.py:220
  42.4 32.2 %copy-start.4 = (s32[32]{0:T(128)S(1)}, s32[32]{0:T(128)}, u32[]{:S(2)}) copy-start(s32[32]{0:T(128)} %param.13) | copy-start | bytes 388
  42.4 35.4 %copy-start.3 = (s32[32,16]{0,1:T(8,128)S(1)}, s32[32,16]{0,1:T(8,128)}, u32[]{:S(2)}) copy-start(s32[32,16]{0,1:T(8,128)} %param.12) | copy-start | bytes 6148
  44.4 35.4 %copy-start = (bf16[1,2048,512]{2,1,0:T(8,128)(2,1)S(1)}, bf16[1,2048,512]{2,1,0:T(8,128)(2,1)}, u32[]{:S(2)}) copy-start(bf16[1,2048,512]{2,1,0:T(8,128)(2,1)} %all-gather.6.cloned.1.call-done) | copy-start | bytes 6291460
  44.4 35.4 %copy-start.2 = (bf16[1,256,2560]{2,1,0:T(8,128)(2,1)S(1)}, bf16[1,256,2560]{2,1,0:T(8,128)(2,1)}, u32[]{:S(2)}) copy-start(bf16[1,256,2560]{2,1,0:T(8,128)(2,1)} %param.8) | copy-start | bytes 3932164
  46.9 25.4 %all-to-all-start.1 = ((bf16[32,16,512]{2,1,0:T(8,128)(2,1)}), bf16[32,16,512]{2,1,0:T(8,128)(2,1)}, u32[]{:S(2)}, u32[]{:S(2)}) async-start(bf16[32,16,512]{2,1,0:T(8,128)(2,1)} %gather_fusion.2), calls=%async_computation.1 | async-start | bytes 1048576 | tf_op jit(solution)/shard_map/all_to_all | solution.py:233
  55.7 48.4 %all-gather.10.cloned.1.call-start = ((), (), s32[]{:S(2)}) async-start(), calls=%async_computation.4 | async-start | bytes 2359296 | tf_op jit(solution)/shard_map/all_gather | solution.py:239
  79.8 1.6 copy-start.1
Sparse Core Ops, SparseCore 0:
  9.8 31.9 all-gather.5
  44.3 28.2 all-gather.7
  74.7 28.0 all-gather.9

commit v5 on v3

--- a/solution.py
+++ b/solution.py
@@ -185,9 +185,11 @@
     land_slot = land_source * cap_new + jnp.take_along_axis(new_rank, land_source[None, :], axis=0)[0]
     land_ids = jnp.take_along_axis(append_table % per_owner, land_source[None, :], axis=0)[0]
     land_live = jnp.any(land_here, axis=0)
-    landed = regroup(lax.all_gather(arrived[land_slot], "group", axis=0, tiled=False))
+    landed = lax.all_gather(arrived[land_slot], "group", axis=0, tiled=False)
     targets = jnp.where(land_live, land_ids, per_owner)
-    new_pool = kv_pool.at[targets].set(landed, mode="drop")
+    pool_pieces = kv_pool.reshape(per_owner, groups, piece_rows, key_width)
+    new_pool = pool_pieces.at[targets[None, :], jnp.arange(groups)[:, None]].set(landed, mode="drop")
+    new_pool = new_pool.reshape(kv_pool.shape)
 
     own_length = lax.dynamic_index_in_dim(cache_lengths, my_block, 0, keepdims=False)
     filled = jnp.minimum(own_length // page_rows, win_pages)

time: 118 us -> 131 us (1.11)
  local copies, waits for them, and re-layouts: 23.4 us -> 36 us
    scatter x1, local copies, waits for them, and re-layouts: 5.15 us -> 19.1 us  [shards(): pool_pieces.at[targets[None, :], jnp.arange(groups)[:, None]]]
    transpose x1 -> x0, local copies, waits for them, and re-layouts: 1.82 us -> none  [regroup(): pieces.transpose(1, 0, 2, 3).reshape(pages, groups * piece_rows, width)]
  transfers between devices with their start and end apart: 5 -> 5, of which waited for: 3 -> 3; matrix products, arithmetic and copies ran while one was open for 11% -> 10% of each run, Pallas kernels for 17% -> 16%
where the time goes in v5:
time: 131 us; the launch traced here: 130 us
  local copies, waits for them, and re-layouts  36 us (27%)
  waiting for transfers between devices  34.1 us (26%)
  starting transfers between devices  21.1 us (16%)
  Pallas kernels  20.4 us (16%)
  between operations  16.6 us (13%)
  other arithmetic  1.85 us (1%)
    pallas_call x1, Pallas kernels, window_attention(): pl.pallas_call(body, out_shape=jax.ShapeDtypeStruct((tok_rows, width), qu...  20.4 us
    scatter x1, local copies, waits for them, and re-layouts, shards(): pool_pieces.at[targets[None, :], jnp.arange(groups)[:, None]]  19.1 us
    all_to_all x1, waiting for transfers between devices, shards(): lax.all_to_all(outgoing, 'blk', split_axis=0, concat_axis=0, tiled=True)  16 us
    all_to_all x1, waiting for transfers between devices, shards(): lax.all_to_all(parcels, 'blk', split_axis=0, concat_axis=0, tiled=True)  14.9 us
    all_to_all x1, starting transfers between devices, shards(): lax.all_to_all(outgoing, 'blk', split_axis=0, concat_axis=0, tiled=True)  12 us
    all_to_all x1, starting transfers between devices, shards(): lax.all_to_all(parcels, 'blk', split_axis=0, concat_axis=0, tiled=True)  8.94 us
    unnamed x11, local copies, waits for them, and re-layouts  5.25 us
    all_gather x1, waiting for transfers between devices, shards(): landed = lax.all_gather(arrived[land_slot], 'group', axis=0, tiled=False)  3.1 us
  transfers between devices with their start and end apart: 5, of which 3 were waited for; matrix products, arithmetic and copies ran while one was open for 10% of the time, Pallas kernels for 16%

profile of v5, /device:TPU:1, one launch (start us, length us, event | category | flops | bytes accessed | tf_op | source)
XLA Modules:
  0.0 130.0 jit_solution(9217142259140217025)
XLA Ops:
  7.2 4.6 %copy.38 = bf16[32,128,512]{2,1,0:T(8,128)(2,1)} copy(bf16[32,128,512]{2,1,0:T(8,128)(2,1)} %param.10) | data formatting | bytes 8388608
  12.1 0.1 convert_reduce_fusion
  12.3 1.1 constant_dynamic-slice_fusion.1
  13.4 1.4 %gather_fusion = bf16[32,16,512]{2,1,0:T(8,128)(2,1)} fusion(bf16[32,16,512]{2,1,0:T(8,128)(2,1)S(1)} %constant_dynamic-slice_fusion.1, s32[1024]{0:T(1024)S(1)} %pad_clamp_fusion.3), kind=kCustom, calls=%fused_computation.2 | custom fusion | bytes 1048704 | tf_op jit(solution)/shard_map/gather | solution.py:166
  14.7 12.0 %all-to-all-start = ((bf16[32,16,512]{2,1,0:T(8,128)(2,1)}), bf16[32,16,512]{2,1,0:T(8,128)(2,1)S(1)}, u32[]{:S(2)}, u32[]{:S(2)}) async-start(bf16[32,16,512]{2,1,0:T(8,128)(2,1)} %gather_fusion), calls=%async_computation | async-start | bytes 1048576 | tf_op jit(solution)/shard_map/all_to_all | solution.py:167
  26.8 0.2 dynamic-slice_reduce_fusion
  27.0 16.0 %all-to-all-done = bf16[32,16,512]{2,1,0:T(8,128)(2,1)S(1)} async-done(((bf16[32,16,512]{2,1,0:T(8,128)(2,1)}), bf16[32,16,512]{2,1,0:T(8,128)(2,1)S(1)}, u32[]{:S(2)}, u32[]{:S(2)}) %all-to-all-start) | async-done | bytes 524320 | tf_op jit(solution)/shard_map/all_to_all | solution.py:167
  43.0 1.3 gather_fusion.1
  44.3 0.2 fusion.6
  44.7 1.0 constant_dynamic-slice_fusion
  45.7 1.4 %gather_fusion.2 = bf16[32,16,512]{2,1,0:T(8,128)(2,1)} fusion(bf16[16,16,512]{2,1,0:T(8,128)(2,1)S(1)} %constant_dynamic-slice_fusion, s32[1024]{0:T(1024)S(1)} %pad_clamp_fusion.1), kind=kCustom, calls=%fused_computation.4 | custom fusion | bytes 1048704 | tf_op jit(solution)/shard_map/gather | solution.py:181
  47.0 8.9 %all-to-all-start.1 = ((bf16[32,16,512]{2,1,0:T(8,128)(2,1)}), bf16[32,16,512]{2,1,0:T(8,128)(2,1)S(1)}, u32[]{:S(2)}, u32[]{:S(2)}) async-start(bf16[32,16,512]{2,1,0:T(8,128)(2,1)} %gather_fusion.2), calls=%async_computation.1 | async-start | bytes 1048576 | tf_op jit(solution)/shard_map/all_to_all | solution.py:182
  56.0 0.7 iota_reduce_fusion
  56.9 0.7 gather_fusion.5
  57.6 14.9 %all-to-all-done.1 = bf16[32,16,512]{2,1,0:T(8,128)(2,1)S(1)} async-done(((bf16[32,16,512]{2,1,0:T(8,128)(2,1)}), bf16[32,16,512]{2,1,0:T(8,128)(2,1)S(1)}, u32[]{:S(2)}, u32[]{:S(2)}) %all-to-all-start.1) | async-done | bytes 524320 | tf_op jit(solution)/shard_map/all_to_all | solution.py:182
  72.6 1.3 gather_fusion.3
  73.9 0.6 dynamic_slice.25
  77.2 0.7 gather_fusion.4
  78.2 2.0 %copy.30 = bf16[8,16,16,512]{3,2,0,1:T(8,128)(2,1)S(1)} copy(bf16[8,16,16,512]{3,2,1,0:T(8,128)(2,1)} %bitcast.57) | data formatting | bytes 4194304 | tf_op jit(solution)/shard_map/all_gather | solution.py:169
  80.2 0.2 copy-done
  80.5 0.4 copy-done.1
  80.8 20.4 %shard_map.77 = bf16[256,2560]{1,0:T(8,128)(2,1)} custom-call(s32[2]{0:T(128)S(1)} %pad_add_fusion.2.meta, bf16[256,2560]{1,0:T(8,128)(2,1)S(1)} %bitcast.54, bf16[2048,512]{1,0:T(8,128)(2,1)S(1)} %bitcast.51, bf16[2048,512]{1,0:T(8,128)(2,1)S(1)} %bitcast.53), custom_call_target="tpu_custom_call" | custom-call | tf_op jit(solution)/shard_map/pallas_call | solution.py:113
  101.2 3.1 %all-gather.10.cloned.1.call-done = bf16[128,16,512]{2,1,0:T(8,128)(2,1)} async-done(((bf16[16,16,512]{2,1,0:T(8,128)(2,1)}), bf16[128,16,512]{2,1,0:T(8,128)(2,1)}) %all-gather.10.cloned.1.call-update) | async-done | bytes 2097168 | tf_op jit(solution)/shard_map/all_gather | solution.py:188
  104.3 19.1 %scatter_fusion = bf16[32,8,16,512]{3,2,1,0:T(8,128)(2,1)} fusion(bf16[32,8,16,512]{3,2,1,0:T(8,128)(2,1)} %bitcast.55, s32[128]{0:T(128)S(1)} %reshape.250, bf16[128,16,512]{2,1,0:T(8,128)(2,1)} %all-gather.10.cloned.1.call-done), kind=kCustom, calls=%fused_computation.6 | custom fusion | bytes 6292480 | tf_op jit(solution)/shard_map/scatter | solution.py:191
  (44 shorter events, 1.2 us)
Async XLA Ops:
  7.2 4.8 %copy-start.2 = (s32[32,16]{0,1:T(8,128)S(1)}, s32[32,16]{0,1:T(8,128)}, u32[]{:S(2)}) copy-start(s32[32,16]{0,1:T(8,128)} %param.11) | copy-start | bytes 6148
  7.2 4.8 %copy-start.3 = (s32[32,16]{0,1:T(8,128)S(1)}, s32[32,16]{0,1:T(8,128)}, u32[]{:S(2)}) copy-start(s32[32,16]{0,1:T(8,128)} %param.12) | copy-start | bytes 6148
  7.2 37.5 %all-gather.6.cloned.1.call-start = ((), (), s32[]{:S(2)}) async-start(), calls=%async_computation.2 | async-start | bytes 2359296 | tf_op jit(solution)/shard_map/all_gather | solution.py:153
  14.7 28.3 %all-to-all-start = ((bf16[32,16,512]{2,1,0:T(8,128)(2,1)}), bf16[32,16,512]{2,1,0:T(8,128)(2,1)S(1)}, u32[]{:S(2)}, u32[]{:S(2)}) async-start(bf16[32,16,512]{2,1,0:T(8,128)(2,1)} %gather_fusion), calls=%async_computation | async-start | bytes 1048576 | tf_op jit(solution)/shard_map/all_to_all | solution.py:167
  26.8 51.5 %all-gather.8.cloned.1.call-start = ((), (), s32[]{:S(2)}) async-start(), calls=%async_computation.3 | async-start | bytes 2359296 | tf_op jit(solution)/shard_map/all_gather | solution.py:169
  44.3 29.5 %copy-start.4 = (s32[32]{0:T(128)S(1)}, s32[32]{0:T(128)}, u32[]{:S(2)}) copy-start(s32[32]{0:T(128)} %param.13) | copy-start | bytes 388
  47.0 25.5 %all-to-all-start.1 = ((bf16[32,16,512]{2,1,0:T(8,128)(2,1)}), bf16[32,16,512]{2,1,0:T(8,128)(2,1)S(1)}, u32[]{:S(2)}, u32[]{:S(2)}) async-start(bf16[32,16,512]{2,1,0:T(8,128)(2,1)} %gather_fusion.2), calls=%async_computation.1 | async-start | bytes 1048576 | tf_op jit(solution)/shard_map/all_to_all | solution.py:182
  56.0 48.3 %all-gather.10.cloned.1.call-start = ((), (), s32[]{:S(2)}) async-start(), calls=%async_computation.4 | async-start | bytes 2359296 | tf_op jit(solution)/shard_map/all_gather | solution.py:188
  78.2 2.2 %copy-start = (bf16[1,2048,512]{2,1,0:T(8,128)(2,1)S(1)}, bf16[1,2048,512]{2,1,0:T(8,128)(2,1)}, u32[]{:S(2)}) copy-start(bf16[1,2048,512]{2,1,0:T(8,128)(2,1)} %all-gather.6.cloned.1.call-done) | copy-start | bytes 6291460
  78.2 2.6 %copy-start.1 = (bf16[1,256,2560]{2,1,0:T(8,128)(2,1)S(1)}, bf16[1,256,2560]{2,1,0:T(8,128)(2,1)}, u32[]{:S(2)}) copy-start(bf16[1,256,2560]{2,1,0:T(8,128)(2,1)} %param.8) | copy-start | bytes 3932164
Sparse Core Ops, SparseCore 0:
  12.0 31.9 all-gather.5
  45.9 28.2 all-gather.7
  76.1 28.1 all-gather.9

commit v6 on v5

--- a/solution.py
+++ b/solution.py
@@ -132,6 +132,50 @@
     )(meta, query_rows, cached, fresh)
 
 
+def pool_kernel(targets, landed, pool_hbm, out_hbm, sems):
+    groups, pages, piece_rows, _ = landed.shape
+    for page in range(pages):
+        target = targets[page]
+
+        @pl.when(target < pool_hbm.shape[0])
+        def _():
+            for grp in range(groups):
+                pltpu.make_async_copy(
+                    landed.at[grp, page], out_hbm.at[target, pl.ds(grp * piece_rows, piece_rows)],
+                    sems.at[page, grp],
+                ).start()
+
+    for page in range(pages):
+        target = targets[page]
+
+        @pl.when(target < pool_hbm.shape[0])
+        def _():
+            for grp in range(groups):
+                pltpu.make_async_copy(
+                    landed.at[grp, page], out_hbm.at[target, pl.ds(grp * piece_rows, piece_rows)],
+                    sems.at[page, grp],
+                ).wait()
+
+
+def write_pool(kv_pool, landed, targets):
+    groups, pages = landed.shape[:2]
+    return pl.pallas_call(
+        pool_kernel,
+        out_shape=jax.ShapeDtypeStruct(kv_pool.shape, kv_pool.dtype),
+        grid_spec=pltpu.PrefetchScalarGridSpec(
+            num_scalar_prefetch=1,
+            grid=(1,),
+            in_specs=[
+                pl.BlockSpec(landed.shape, lambda i, t: (0, 0, 0, 0)),
+                pl.BlockSpec(memory_space=pl.ANY),
+            ],
+            out_specs=pl.BlockSpec(memory_space=pl.ANY),
+            scratch_shapes=[pltpu.SemaphoreType.DMA((pages, groups))],
+        ),
+        input_output_aliases={2: 0},
+    )(targets.astype(jnp.int32), landed, kv_pool)
+
+
 def shards(queries, new_kv, kv_pool, window_table, append_table, cache_lengths):
     blocks = lax.axis_size("blk")
     groups = lax.axis_size("group")
@@ -187,9 +231,7 @@
     land_live = jnp.any(land_here, axis=0)
     landed = lax.all_gather(arrived[land_slot], "group", axis=0, tiled=False)
     targets = jnp.where(land_live, land_ids, per_owner)
-    pool_pieces = kv_pool.reshape(per_owner, groups, piece_rows, key_width)
-    new_pool = pool_pieces.at[targets[None, :], jnp.arange(groups)[:, None]].set(landed, mode="drop")
-    new_pool = new_pool.reshape(kv_pool.shape)
+    new_pool = write_pool(kv_pool, landed, targets)
 
     own_length = lax.dynamic_index_in_dim(cache_lengths, my_block, 0, keepdims=False)
     filled = jnp.minimum(own_length // page_rows, win_pages)

time: 131 us -> 116 us (0.89)
  local copies, waits for them, and re-layouts: 36 us -> 16.5 us
  Pallas kernels: 20.4 us -> 25.1 us
    scatter x1 -> x0, local copies, waits for them, and re-layouts: 19.1 us -> none  [shards(): pool_pieces.at[targets[None, :], jnp.arange(groups)[:, None]]]
    pallas_call x0 -> x1, Pallas kernels: none -> 4.67 us  [write_pool(): pl.pallas_call(pool_kernel, out_shape=jax.ShapeDtypeStruct(kv_pool.shape,...]
  transfers between devices with their start and end apart: 5 -> 5, of which waited for: 3 -> 3; matrix products, arithmetic and copies ran while one was open for 10% -> 12% of each run, Pallas kernels for 16% -> 18%
where the time goes in v6:
time: 116 us
  waiting for transfers between devices  34.8 us (30%)
  Pallas kernels  25.1 us (22%)
  starting transfers between devices  20.5 us (18%)
  between operations  16.6 us (14%)
  local copies, waits for them, and re-layouts  16.5 us (14%)
  other arithmetic  2.16 us (2%)
    pallas_call x1, Pallas kernels, window_attention(): pl.pallas_call(body, out_shape=jax.ShapeDtypeStruct((tok_rows, width), qu...  20.4 us
    all_to_all x1, waiting for transfers between devices, shards(): lax.all_to_all(outgoing, 'blk', split_axis=0, concat_axis=0, tiled=True)  16 us
    all_to_all x1, waiting for transfers between devices, shards(): lax.all_to_all(parcels, 'blk', split_axis=0, concat_axis=0, tiled=True)  14.5 us
    all_to_all x1, starting transfers between devices, shards(): lax.all_to_all(outgoing, 'blk', split_axis=0, concat_axis=0, tiled=True)  12 us
    all_to_all x1, starting transfers between devices, shards(): lax.all_to_all(parcels, 'blk', split_axis=0, concat_axis=0, tiled=True)  8.34 us
    unnamed x11, local copies, waits for them, and re-layouts  5.25 us
    pallas_call x1, Pallas kernels, write_pool(): pl.pallas_call(pool_kernel, out_shape=jax.ShapeDtypeStruct(kv_pool.shape,...  4.67 us
    all_gather x1, waiting for transfers between devices, shards(): landed = lax.all_gather(arrived[land_slot], 'group', axis=0, tiled=False)  4.24 us
  transfers between devices with their start and end apart: 5, of which 3 were waited for; matrix products, arithmetic and copies ran while one was open for 12% of the time, Pallas kernels for 18%

profile of v6, /device:TPU:1, one launch (start us, length us, event | category | flops | bytes accessed | tf_op | source)
XLA Modules:
  0.0 115.6 jit_solution(13791305771433119401)
XLA Ops:
  7.2 4.6 %copy.29.pool_hbm = bf16[32,128,512]{2,1,0:T(8,128)(2,1)} copy(bf16[32,128,512]{2,1,0:T(8,128)(2,1)} %param.10) | data formatting | bytes 8388608
  12.3 1.1 constant_dynamic-slice_fusion.1
  13.4 1.4 %gather_fusion = bf16[32,16,512]{2,1,0:T(8,128)(2,1)} fusion(bf16[32,16,512]{2,1,0:T(8,128)(2,1)S(1)} %constant_dynamic-slice_fusion.1, s32[1024]{0:T(1024)S(1)} %pad_clamp_fusion.3), kind=kCustom, calls=%fused_computation.2 | custom fusion | bytes 1048704 | tf_op jit(solution)/shard_map/gather | solution.py:210
  14.7 12.0 %all-to-all-start = ((bf16[32,16,512]{2,1,0:T(8,128)(2,1)}), bf16[32,16,512]{2,1,0:T(8,128)(2,1)S(1)}, u32[]{:S(2)}, u32[]{:S(2)}) async-start(bf16[32,16,512]{2,1,0:T(8,128)(2,1)} %gather_fusion), calls=%async_computation | async-start | bytes 1048576 | tf_op jit(solution)/shard_map/all_to_all | solution.py:211
  26.8 0.2 dynamic-slice_reduce_fusion
  27.0 16.0 %all-to-all-done = bf16[32,16,512]{2,1,0:T(8,128)(2,1)S(1)} async-done(((bf16[32,16,512]{2,1,0:T(8,128)(2,1)}), bf16[32,16,512]{2,1,0:T(8,128)(2,1)S(1)}, u32[]{:S(2)}, u32[]{:S(2)}) %all-to-all-start) | async-done | bytes 524320 | tf_op jit(solution)/shard_map/all_to_all | solution.py:211
  43.0 1.3 %gather_fusion.1 = bf16[16,16,512]{2,1,0:T(8,128)(2,1)} fusion(bf16[32,16,512]{2,1,0:T(8,128)(2,1)S(1)} %all-to-all-done, s32[1024]{0:T(1024)S(1)} %pad_clamp_fusion.2), kind=kCustom, calls=%fused_computation.3 | custom fusion | bytes 524352 | tf_op jit(solution)/shard_map/gather | solution.py:212
  44.3 0.2 fusion.5
  44.6 0.6 iota_reduce_fusion
  45.3 1.0 constant_dynamic-slice_fusion
  46.3 1.4 %gather_fusion.2 = bf16[32,16,512]{2,1,0:T(8,128)(2,1)} fusion(bf16[16,16,512]{2,1,0:T(8,128)(2,1)S(1)} %constant_dynamic-slice_fusion, s32[1024]{0:T(1024)S(1)} %pad_clamp_fusion.1), kind=kCustom, calls=%fused_computation.4 | custom fusion | bytes 1048704 | tf_op jit(solution)/shard_map/gather | solution.py:225
  47.6 8.3 %all-to-all-start.1 = ((bf16[32,16,512]{2,1,0:T(8,128)(2,1)}), bf16[32,16,512]{2,1,0:T(8,128)(2,1)S(1)}, u32[]{:S(2)}, u32[]{:S(2)}) async-start(bf16[32,16,512]{2,1,0:T(8,128)(2,1)} %gather_fusion.2), calls=%async_computation.1 | async-start | bytes 1048576 | tf_op jit(solution)/shard_map/all_to_all | solution.py:226
  56.1 0.7 gather_fusion.5
  56.8 0.7 gather_fusion.4
  57.4 0.6 compare_select_fusion.1
  58.0 14.5 %all-to-all-done.1 = bf16[32,16,512]{2,1,0:T(8,128)(2,1)S(1)} async-done(((bf16[32,16,512]{2,1,0:T(8,128)(2,1)}), bf16[32,16,512]{2,1,0:T(8,128)(2,1)S(1)}, u32[]{:S(2)}, u32[]{:S(2)}) %all-to-all-start.1) | async-done | bytes 524320 | tf_op jit(solution)/shard_map/all_to_all | solution.py:226
  72.6 1.3 %gather_fusion.3 = bf16[16,16,512]{2,1,0:T(8,128)(2,1)} fusion(bf16[32,16,512]{2,1,0:T(8,128)(2,1)S(1)} %all-to-all-done.1, s32[1024]{0:T(1024)S(1)} %pad_clamp_fusion), kind=kCustom, calls=%fused_computation.5 | custom fusion | bytes 524352 | tf_op jit(solution)/shard_map/gather | solution.py:232
  73.9 0.6 dynamic_slice.25
  77.1 2.0 %copy.26 = bf16[8,16,16,512]{3,2,0,1:T(8,128)(2,1)S(1)} copy(bf16[8,16,16,512]{3,2,1,0:T(8,128)(2,1)} %bitcast.58) | data formatting | bytes 4194304 | tf_op jit(solution)/shard_map/all_gather | solution.py:213
  79.1 0.2 copy-done
  79.4 0.4 copy-done.1
  79.7 20.4 %shard_map.77 = bf16[256,2560]{1,0:T(8,128)(2,1)} custom-call(s32[2]{0:T(128)S(1)} %pad_add_fusion.meta, bf16[256,2560]{1,0:T(8,128)(2,1)S(1)} %bitcast.57, bf16[2048,512]{1,0:T(8,128)(2,1)S(1)} %bitcast.54, bf16[2048,512]{1,0:T(8,128)(2,1)S(1)} %bitcast.56), custom_call_target="tpu_custom_call" | custom-call | tf_op jit(solution)/shard_map/pallas_call | solution.py:113
  100.1 4.2 %all-gather.10.cloned.1.call-done = bf16[128,16,512]{2,1,0:T(8,128)(2,1)} async-done(((bf16[16,16,512]{2,1,0:T(8,128)(2,1)}), bf16[128,16,512]{2,1,0:T(8,128)(2,1)}) %all-gather.10.cloned.1.call-update) | async-done | bytes 2097168 | tf_op jit(solution)/shard_map/all_gather | solution.py:232
  104.4 4.7 %shard_map.78 = bf16[32,128,512]{2,1,0:T(8,128)(2,1)} custom-call(s32[16]{0:T(128)} %get-tuple-element.11.targets, bf16[8,16,16,512]{3,2,1,0:T(8,128)(2,1)} %bitcast.59, bf16[32,128,512]{2,1,0:T(8,128)(2,1)} %copy.29.pool_hbm), custom_call_target="tpu_custom_call", output_to_operand_aliasing={{}: (2, {})} | custom-call | tf_op jit(solution)/shard_map/pallas_call | solution.py:162
  (35 shorter events, 0.7 us)
Async XLA Ops:
  7.2 4.8 %copy-start.2 = (s32[32,16]{0,1:T(8,128)S(1)}, s32[32,16]{0,1:T(8,128)}, u32[]{:S(2)}) copy-start(s32[32,16]{0,1:T(8,128)} %param.11) | copy-start | bytes 6148
  7.2 4.8 %copy-start.3 = (s32[32,16]{0,1:T(8,128)S(1)}, s32[32,16]{0,1:T(8,128)}, u32[]{:S(2)}) copy-start(s32[32,16]{0,1:T(8,128)} %param.12) | copy-start | bytes 6148
  7.2 38.1 %all-gather.6.cloned.1.call-start = ((), (), s32[]{:S(2)}) async-start(), calls=%async_computation.2 | async-start | bytes 2359296 | tf_op jit(solution)/shard_map/all_gather | solution.py:197
  14.7 28.3 %all-to-all-start = ((bf16[32,16,512]{2,1,0:T(8,128)(2,1)}), bf16[32,16,512]{2,1,0:T(8,128)(2,1)S(1)}, u32[]{:S(2)}, u32[]{:S(2)}) async-start(bf16[32,16,512]{2,1,0:T(8,128)(2,1)} %gather_fusion), calls=%async_computation | async-start | bytes 1048576 | tf_op jit(solution)/shard_map/all_to_all | solution.py:211
  26.8 50.4 %all-gather.8.cloned.1.call-start = ((), (), s32[]{:S(2)}) async-start(), calls=%async_computation.3 | async-start | bytes 2359296 | tf_op jit(solution)/shard_map/all_gather | solution.py:213
  46.3 27.6 %copy-start.4 = (s32[32]{0:T(128)S(1)}, s32[32]{0:T(128)}, u32[]{:S(2)}) copy-start(s32[32]{0:T(128)} %param.13) | copy-start | bytes 388
  47.6 24.9 %all-to-all-start.1 = ((bf16[32,16,512]{2,1,0:T(8,128)(2,1)}), bf16[32,16,512]{2,1,0:T(8,128)(2,1)S(1)}, u32[]{:S(2)}, u32[]{:S(2)}) async-start(bf16[32,16,512]{2,1,0:T(8,128)(2,1)} %gather_fusion.2), calls=%async_computation.1 | async-start | bytes 1048576 | tf_op jit(solution)/shard_map/all_to_all | solution.py:226
  56.0 48.4 %all-gather.10.cloned.1.call-start = ((), (), s32[]{:S(2)}) async-start(), calls=%async_computation.4 | async-start | bytes 2359296 | tf_op jit(solution)/shard_map/all_gather | solution.py:232
  77.1 2.2 %copy-start = (bf16[1,2048,512]{2,1,0:T(8,128)(2,1)S(1)}, bf16[1,2048,512]{2,1,0:T(8,128)(2,1)}, u32[]{:S(2)}) copy-start(bf16[1,2048,512]{2,1,0:T(8,128)(2,1)} %all-gather.6.cloned.1.call-done) | copy-start | bytes 6291460
  77.1 2.6 %copy-start.1 = (bf16[1,256,2560]{2,1,0:T(8,128)(2,1)S(1)}, bf16[1,256,2560]{2,1,0:T(8,128)(2,1)}, u32[]{:S(2)}) copy-start(bf16[1,256,2560]{2,1,0:T(8,128)(2,1)} %param.8) | copy-start | bytes 3932164
Sparse Core Ops, SparseCore 0:
  12.0 31.9 all-gather.5
  45.9 28.2 all-gather.7
  76.1 28.2 all-gather.9

commit v7 on v6

--- a/solution.py
+++ b/solution.py
@@ -17,29 +17,6 @@
 
 def pick_rows(wanted, values):
     return jnp.sum(jnp.where(wanted, values[:, None, :], 0), axis=2)
-
-
-def attend(qblock, keys_use, index_use, live_use, block_start, head_count, head_size, window_len):
-    block_len = qblock.shape[0]
-    query_rows = qblock.reshape(block_len, head_count, head_size)
-    scores = jnp.einsum(
-        "thd,kd->thk", query_rows, keys_use[:, :head_size], preferred_element_type=jnp.float32
-    ) * head_size ** (-0.5)
-    positions = block_start + jnp.arange(block_len)
-    allowed = (
-        (index_use[None, :] > positions[:, None])
-        & (index_use[None, :] <= positions[:, None] + window_len)
-        & live_use[None, :]
-    )
-    scores = jnp.where(allowed[:, None, :], scores, -jnp.inf)
-    row_max = jnp.max(scores, axis=2, keepdims=True)
-    raw_weights = jnp.exp(scores - row_max)
-    row_total = jnp.sum(raw_weights, axis=2, keepdims=True)
-    weights = raw_weights.astype(jnp.bfloat16)
-    weighted = jnp.einsum(
-        "thk,kd->thd", weights, keys_use[:, head_size:], preferred_element_type=jnp.float32
-    )
-    return (weighted / row_total).astype(jnp.bfloat16).reshape(block_len, head_count * head_size)
 
 
 def regroup(pieces):
@@ -157,6 +134,22 @@
                 ).wait()
 
 
+def copy_kernel(src_ref, dst_ref):
+    dst_ref[...] = src_ref[...]
+
+
+def copy_pool(kv_pool):
+    pages = kv_pool.shape[0]
+    block = (8,) + kv_pool.shape[1:]
+    return pl.pallas_call(
+        copy_kernel,
+        out_shape=jax.ShapeDtypeStruct(kv_pool.shape, kv_pool.dtype),
+        grid=(pages // 8,),
+        in_specs=[pl.BlockSpec(block, lambda i: (i, 0, 0))],
+        out_specs=pl.BlockSpec(block, lambda i: (i, 0, 0)),
+    )(kv_pool)
+
+
 def write_pool(kv_pool, landed, targets):
     groups, pages = landed.shape[:2]
     return pl.pallas_call(
@@ -176,7 +169,7 @@
     )(targets.astype(jnp.int32), landed, kv_pool)
 
 
-def shards(queries, new_kv, kv_pool, window_table, append_table, cache_lengths):
+def shards_body(queries, new_kv, kv_pool, window_table, append_table, cache_lengths):
     blocks = lax.axis_size("blk")
     groups = lax.axis_size("group")
     my_block = lax.axis_index("blk")
@@ -195,7 +188,6 @@
     piece_rows = page_rows // groups
     piece_start = piece_index * piece_rows
     fresh_keys = lax.all_gather(new_kv, "group", axis=1, tiled=True)[0]
-    append_rows = fresh_keys.shape[0]
 
     win_owner = window_table // per_owner
     win_rank = earlier_same(win_owner)
@@ -209,6 +201,7 @@
     pool_piece = lax.dynamic_slice_in_dim(kv_pool, piece_start, piece_rows, axis=1)
     outgoing = pool_piece[send_ids.reshape(-1)]
     received = lax.all_to_all(outgoing, "blk", split_axis=0, concat_axis=0, tiled=True)
+    pool_out = copy_pool(kv_pool)
     cached_piece = received[arrival]
     cached = regroup(lax.all_gather(cached_piece, "group", axis=0, tiled=False))
 
@@ -231,7 +224,7 @@
     land_live = jnp.any(land_here, axis=0)
     landed = lax.all_gather(arrived[land_slot], "group", axis=0, tiled=False)
     targets = jnp.where(land_live, land_ids, per_owner)
-    new_pool = write_pool(kv_pool, landed, targets)
+    new_pool = write_pool(pool_out, landed, targets)
 
     own_length = lax.dynamic_index_in_dim(cache_lengths, my_block, 0, keepdims=False)
     filled = jnp.minimum(own_length // page_rows, win_pages)
@@ -255,4 +248,4 @@
         P(),
     )
     out_specs = (P("blk", "group", None), P("blk", None, None))
-    return jax.shard_map(shards, mesh=mesh, in_specs=in_specs, out_specs=out_specs, check_vma=False)
+    return jax.shard_map(shards_body, mesh=mesh, in_specs=in_specs, out_specs=out_specs, check_vma=False)

time: 116 us -> 115 us (level)
  Pallas kernels: 25.1 us -> 29.8 us
  local copies, waits for them, and re-layouts: 16.5 us -> 11.8 us
  waiting for transfers between devices: 34.8 us -> 31.3 us
  other arithmetic: 2.16 us -> 4.25 us
    pallas_call x0 -> x1, Pallas kernels: none -> 4.74 us  [copy_pool(): pl.pallas_call(copy_kernel, out_shape=jax.ShapeDtypeStruct(kv_pool.shape,...]
    unnamed x11 -> x8, local copies, waits for them, and re-layouts: 5.25 us -> 0.61 us
    all_gather x3, waiting for transfers between devices: 4.24 us -> 0.02 us  [the longest x1 0.02 us: shards_body(): landed = lax.all_gather(arrived[land_slot], 'group', axis=0, tiled=False)]
  transfers between devices with their start and end apart: 5 -> 5, of which waited for: 3 -> 2; matrix products, arithmetic and copies ran while one was open for 12% -> 14% of each run, Pallas kernels for 18% -> 22%
where the time goes in v7:
time: 115 us; the launch traced here: 114 us
  waiting for transfers between devices  31.3 us (27%)
  Pallas kernels  29.8 us (26%)
  starting transfers between devices  20.2 us (18%)
  between operations  16.5 us (14%)
  local copies, waits for them, and re-layouts  11.8 us (10%)
  other arithmetic  4.25 us (4%)
    pallas_call x1, Pallas kernels, window_attention(): pl.pallas_call(body, out_shape=jax.ShapeDtypeStruct((tok_rows, width), qu...  20.4 us
    all_to_all x1, waiting for transfers between devices, shards_body(): lax.all_to_all(outgoing, 'blk', split_axis=0, concat_axis=0, tiled=True)  16 us
    all_to_all x1, waiting for transfers between devices, shards_body(): lax.all_to_all(parcels, 'blk', split_axis=0, concat_axis=0, tiled=True)  14.5 us
    all_to_all x1, starting transfers between devices, shards_body(): lax.all_to_all(outgoing, 'blk', split_axis=0, concat_axis=0, tiled=True)  12 us
    all_to_all x1, starting transfers between devices, shards_body(): lax.all_to_all(parcels, 'blk', split_axis=0, concat_axis=0, tiled=True)  8.09 us
    pallas_call x1, Pallas kernels, copy_pool(): pl.pallas_call(copy_kernel, out_shape=jax.ShapeDtypeStruct(kv_pool.shape,...  4.74 us
    pallas_call x1, Pallas kernels, write_pool(): pl.pallas_call(pool_kernel, out_shape=jax.ShapeDtypeStruct(kv_pool.shape,...  4.67 us
  transfers between devices with their start and end apart: 5, of which 2 were waited for; matrix products, arithmetic and copies ran while one was open for 14% of the time, Pallas kernels for 22%

profile of v7, /device:TPU:1, one launch (start us, length us, event | category | flops | bytes accessed | tf_op | source)
XLA Modules:
  0.0 113.9 jit_solution(6442304644642565899)
XLA Ops:
  7.2 0.7 all-gather.6.cloned.1.call-update
  7.9 0.7 add_select_fusion.3
  8.6 0.8 fusion.12
  9.6 0.7 fusion.1
  10.3 1.1 constant_dynamic-slice_fusion.1
  11.4 1.4 %gather_fusion = bf16[32,16,512]{2,1,0:T(8,128)(2,1)} fusion(bf16[32,16,512]{2,1,0:T(8,128)(2,1)S(1)} %constant_dynamic-slice_fusion.1, s32[1024]{0:T(1024)S(1)} %pad_clamp_fusion.3), kind=kCustom, calls=%fused_computation.2 | custom fusion | bytes 1048704 | tf_op jit(solution)/shard_map/gather | solution.py:202
  12.8 12.0 %all-to-all-start = ((bf16[32,16,512]{2,1,0:T(8,128)(2,1)}), bf16[32,16,512]{2,1,0:T(8,128)(2,1)S(1)}, u32[]{:S(2)}, u32[]{:S(2)}) async-start(bf16[32,16,512]{2,1,0:T(8,128)(2,1)} %gather_fusion), calls=%async_computation | async-start | bytes 1048576 | tf_op jit(solution)/shard_map/all_to_all | solution.py:203
  25.1 16.0 %all-to-all-done = bf16[32,16,512]{2,1,0:T(8,128)(2,1)S(1)} async-done(((bf16[32,16,512]{2,1,0:T(8,128)(2,1)}), bf16[32,16,512]{2,1,0:T(8,128)(2,1)S(1)}, u32[]{:S(2)}, u32[]{:S(2)}) %all-to-all-start) | async-done | bytes 524320 | tf_op jit(solution)/shard_map/all_to_all | solution.py:203
  41.1 1.3 %gather_fusion.1 = bf16[16,16,512]{2,1,0:T(8,128)(2,1)} fusion(bf16[32,16,512]{2,1,0:T(8,128)(2,1)S(1)} %all-to-all-done, s32[1024]{0:T(1024)S(1)} %pad_clamp_fusion.2), kind=kCustom, calls=%fused_computation.3 | custom fusion | bytes 524352 | tf_op jit(solution)/shard_map/gather | solution.py:205
  42.7 0.6 iota_reduce_fusion
  43.3 1.0 constant_dynamic-slice_fusion
  44.3 1.4 %gather_fusion.2 = bf16[32,16,512]{2,1,0:T(8,128)(2,1)} fusion(bf16[16,16,512]{2,1,0:T(8,128)(2,1)S(1)} %constant_dynamic-slice_fusion, s32[1024]{0:T(1024)S(1)} %pad_clamp_fusion.1), kind=kCustom, calls=%fused_computation.4 | custom fusion | bytes 1048704 | tf_op jit(solution)/shard_map/gather | solution.py:218
  45.7 8.1 %all-to-all-start.1 = ((bf16[32,16,512]{2,1,0:T(8,128)(2,1)}), bf16[32,16,512]{2,1,0:T(8,128)(2,1)S(1)}, u32[]{:S(2)}, u32[]{:S(2)}) async-start(bf16[32,16,512]{2,1,0:T(8,128)(2,1)} %gather_fusion.2), calls=%async_computation.1 | async-start | bytes 1048576 | tf_op jit(solution)/shard_map/all_to_all | solution.py:219
  53.9 0.7 gather_fusion.5
  54.6 0.7 gather_fusion.4
  55.3 0.6 compare_select_fusion.1
  55.9 14.5 %all-to-all-done.1 = bf16[32,16,512]{2,1,0:T(8,128)(2,1)S(1)} async-done(((bf16[32,16,512]{2,1,0:T(8,128)(2,1)}), bf16[32,16,512]{2,1,0:T(8,128)(2,1)S(1)}, u32[]{:S(2)}, u32[]{:S(2)}) %all-to-all-start.1) | async-done | bytes 524320 | tf_op jit(solution)/shard_map/all_to_all | solution.py:219
  70.4 1.3 %gather_fusion.3 = bf16[16,16,512]{2,1,0:T(8,128)(2,1)} fusion(bf16[32,16,512]{2,1,0:T(8,128)(2,1)S(1)} %all-to-all-done.1, s32[1024]{0:T(1024)S(1)} %pad_clamp_fusion), kind=kCustom, calls=%fused_computation.5 | custom fusion | bytes 524352 | tf_op jit(solution)/shard_map/gather | solution.py:225
  71.7 0.6 dynamic_slice.25
  74.2 4.7 %shard_map.78.pool_hbm = bf16[32,128,512]{2,1,0:T(8,128)(2,1)} custom-call(bf16[32,128,512]{2,1,0:T(8,128)(2,1)} %src_ref.1), custom_call_target="tpu_custom_call" | custom-call | tf_op jit(solution)/shard_map/pallas_call | solution.py:144
  79.7 2.0 %copy.26 = bf16[8,16,16,512]{3,2,0,1:T(8,128)(2,1)S(1)} copy(bf16[8,16,16,512]{3,2,1,0:T(8,128)(2,1)} %bitcast.58) | data formatting | bytes 4194304 | tf_op jit(solution)/shard_map/all_gather | solution.py:206
  81.9 0.4 copy-done.1
  82.3 20.4 %shard_map.77 = bf16[256,2560]{1,0:T(8,128)(2,1)} custom-call(s32[2]{0:T(128)S(1)} %pad_add_fusion.meta, bf16[256,2560]{1,0:T(8,128)(2,1)S(1)} %bitcast.57, bf16[2048,512]{1,0:T(8,128)(2,1)S(1)} %bitcast.54, bf16[2048,512]{1,0:T(8,128)(2,1)S(1)} %bitcast.56), custom_call_target="tpu_custom_call" | custom-call | tf_op jit(solution)/shard_map/pallas_call | solution.py:90
  102.7 4.7 %shard_map.79 = bf16[32,128,512]{2,1,0:T(8,128)(2,1)} custom-call(s32[16]{0:T(128)} %get-tuple-element.11.targets, bf16[8,16,16,512]{3,2,1,0:T(8,128)(2,1)} %bitcast.59, bf16[32,128,512]{2,1,0:T(8,128)(2,1)} %shard_map.78.pool_hbm), custom_call_target="tpu_custom_call", output_to_operand_aliasing={{}: (2, {})} | custom-call | tf_op jit(solution)/shard_map/pallas_call | solution.py:155
  (33 shorter events, 1.2 us)
Async XLA Ops:
  7.2 36.2 %all-gather.6.cloned.1.call-start = ((), (), s32[]{:S(2)}) async-start(), calls=%async_computation.2 | async-start | bytes 2359296 | tf_op jit(solution)/shard_map/all_gather | solution.py:190
  12.8 28.3 %all-to-all-start = ((bf16[32,16,512]{2,1,0:T(8,128)(2,1)}), bf16[32,16,512]{2,1,0:T(8,128)(2,1)S(1)}, u32[]{:S(2)}, u32[]{:S(2)}) async-start(bf16[32,16,512]{2,1,0:T(8,128)(2,1)} %gather_fusion), calls=%async_computation | async-start | bytes 1048576 | tf_op jit(solution)/shard_map/all_to_all | solution.py:203
  24.8 29.7 %copy-start.2 = (s32[32,16]{0,1:T(8,128)S(1)}, s32[32,16]{0,1:T(8,128)}, u32[]{:S(2)}) copy-start(s32[32,16]{0,1:T(8,128)} %param.12) | copy-start | bytes 6148
  24.8 54.9 %all-gather.8.cloned.1.call-start = ((), (), s32[]{:S(2)}) async-start(), calls=%async_computation.3 | async-start | bytes 2359296 | tf_op jit(solution)/shard_map/all_gather | solution.py:206
  44.3 27.4 %copy-start.3 = (s32[32]{0:T(128)S(1)}, s32[32]{0:T(128)}, u32[]{:S(2)}) copy-start(s32[32]{0:T(128)} %param.13) | copy-start | bytes 388
  45.7 24.7 %all-to-all-start.1 = ((bf16[32,16,512]{2,1,0:T(8,128)(2,1)}), bf16[32,16,512]{2,1,0:T(8,128)(2,1)S(1)}, u32[]{:S(2)}, u32[]{:S(2)}) async-start(bf16[32,16,512]{2,1,0:T(8,128)(2,1)} %gather_fusion.2), calls=%async_computation.1 | async-start | bytes 1048576 | tf_op jit(solution)/shard_map/all_to_all | solution.py:219
  53.8 48.9 %all-gather.10.cloned.1.call-start = ((), (), s32[]{:S(2)}) async-start(), calls=%async_computation.4 | async-start | bytes 2359296 | tf_op jit(solution)/shard_map/all_gather | solution.py:225
  79.7 2.2 %copy-start = (bf16[1,2048,512]{2,1,0:T(8,128)(2,1)S(1)}, bf16[1,2048,512]{2,1,0:T(8,128)(2,1)}, u32[]{:S(2)}) copy-start(bf16[1,2048,512]{2,1,0:T(8,128)(2,1)} %all-gather.6.cloned.1.call-done) | copy-start | bytes 6291460
  79.7 2.6 %copy-start.1 = (bf16[1,256,2560]{2,1,0:T(8,128)(2,1)S(1)}, bf16[1,256,2560]{2,1,0:T(8,128)(2,1)}, u32[]{:S(2)}) copy-start(bf16[1,256,2560]{2,1,0:T(8,128)(2,1)} %param.8) | copy-start | bytes 3932164
Sparse Core Ops, SparseCore 0:
  9.8 31.9 all-gather.5
  43.7 28.2 all-gather.7
  73.9 28.2 all-gather.9

commit v8 on v7

--- a/solution.py
+++ b/solution.py
@@ -109,29 +109,48 @@
     )(meta, query_rows, cached, fresh)
 
 
-def pool_kernel(targets, landed, pool_hbm, out_hbm, sems):
-    groups, pages, piece_rows, _ = landed.shape
-    for page in range(pages):
-        target = targets[page]
-
-        @pl.when(target < pool_hbm.shape[0])
-        def _():
-            for grp in range(groups):
-                pltpu.make_async_copy(
-                    landed.at[grp, page], out_hbm.at[target, pl.ds(grp * piece_rows, piece_rows)],
-                    sems.at[page, grp],
-                ).start()
-
-    for page in range(pages):
-        target = targets[page]
-
-        @pl.when(target < pool_hbm.shape[0])
-        def _():
-            for grp in range(groups):
-                pltpu.make_async_copy(
-                    landed.at[grp, page], out_hbm.at[target, pl.ds(grp * piece_rows, piece_rows)],
-                    sems.at[page, grp],
-                ).wait()
+def pool_kernel(targets, landed_hbm, pool_hbm, out_hbm, staged, in_sems, out_sems):
+    groups, pages, piece_rows, _ = landed_hbm.shape
+    for grp in range(groups):
+        pltpu.make_async_copy(landed_hbm.at[grp], staged.at[grp], in_sems.at[grp]).start()
+
+    def each_target(grp, begin):
+        for page in range(pages):
+            target = targets[page]
+
+            @pl.when(target < pool_hbm.shape[0])
+            def _():
+                cp = pltpu.make_async_copy(
+                    staged.at[grp, page], out_hbm.at[target, pl.ds(grp * piece_rows, piece_rows)],
+                    out_sems.at[page, grp],
+                )
+                cp.start() if begin else cp.wait()
+
+    for grp in range(groups):
+        pltpu.make_async_copy(landed_hbm.at[grp], staged.at[grp], in_sems.at[grp]).wait()
+        each_target(grp, True)
+    for grp in range(groups):
+        each_target(grp, False)
+
+
+def write_pool(kv_pool, landed, targets):
+    groups, pages = landed.shape[:2]
+    return pl.pallas_call(
+        pool_kernel,
+        out_shape=jax.ShapeDtypeStruct(kv_pool.shape, kv_pool.dtype),
+        grid_spec=pltpu.PrefetchScalarGridSpec(
+            num_scalar_prefetch=1,
+            grid=(1,),
+            in_specs=[pl.BlockSpec(memory_space=pl.ANY), pl.BlockSpec(memory_space=pl.ANY)],
+            out_specs=pl.BlockSpec(memory_space=pl.ANY),
+            scratch_shapes=[
+                pltpu.VMEM(landed.shape, landed.dtype),
+                pltpu.SemaphoreType.DMA((groups,)),
+                pltpu.SemaphoreType.DMA((pages, groups)),
+            ],
+        ),
+        input_output_aliases={2: 0},
+    )(targets.astype(jnp.int32), landed, kv_pool)
 
 
 def copy_kernel(src_ref, dst_ref):
@@ -148,25 +167,6 @@
         in_specs=[pl.BlockSpec(block, lambda i: (i, 0, 0))],
         out_specs=pl.BlockSpec(block, lambda i: (i, 0, 0)),
     )(kv_pool)
-
-
-def write_pool(kv_pool, landed, targets):
-    groups, pages = landed.shape[:2]
-    return pl.pallas_call(
-        pool_kernel,
-        out_shape=jax.ShapeDtypeStruct(kv_pool.shape, kv_pool.dtype),
-        grid_spec=pltpu.PrefetchScalarGridSpec(
-            num_scalar_prefetch=1,
-            grid=(1,),
-            in_specs=[
-                pl.BlockSpec(landed.shape, lambda i, t: (0, 0, 0, 0)),
-                pl.BlockSpec(memory_space=pl.ANY),
-            ],
-            out_specs=pl.BlockSpec(memory_space=pl.ANY),
-            scratch_shapes=[pltpu.SemaphoreType.DMA((pages, groups))],
-        ),
-        input_output_aliases={2: 0},
-    )(targets.astype(jnp.int32), landed, kv_pool)
 
 
 def shards_body(queries, new_kv, kv_pool, window_table, append_table, cache_lengths):

time: 115 us -> 114 us (level)
  no operation moved by 1% of the time
where the time goes in v8:
time: 114 us; the launch traced here: 113 us
  waiting for transfers between devices  31.3 us (27%)
  Pallas kernels  29.2 us (26%)
  starting transfers between devices  20.2 us (18%)
  between operations  16.5 us (14%)
  local copies, waits for them, and re-layouts  11.8 us (10%)
  other arithmetic  4.25 us (4%)
    pallas_call x1, Pallas kernels, window_attention(): pl.pallas_call(body, out_shape=jax.ShapeDtypeStruct((tok_rows, width), qu...  20.4 us
    all_to_all x1, waiting for transfers between devices, shards_body(): lax.all_to_all(outgoing, 'blk', split_axis=0, concat_axis=0, tiled=True)  16 us
    all_to_all x1, waiting for transfers between devices, shards_body(): lax.all_to_all(parcels, 'blk', split_axis=0, concat_axis=0, tiled=True)  14.5 us
    all_to_all x1, starting transfers between devices, shards_body(): lax.all_to_all(outgoing, 'blk', split_axis=0, concat_axis=0, tiled=True)  12 us
    all_to_all x1, starting transfers between devices, shards_body(): lax.all_to_all(parcels, 'blk', split_axis=0, concat_axis=0, tiled=True)  8.09 us
    pallas_call x1, Pallas kernels, copy_pool(): pl.pallas_call(copy_kernel, out_shape=jax.ShapeDtypeStruct(kv_pool.shape,...  4.74 us
    pallas_call x1, Pallas kernels, write_pool(): pl.pallas_call(pool_kernel, out_shape=jax.ShapeDtypeStruct(kv_pool.shape,...  4.1 us
  transfers between devices with their start and end apart: 5, of which 2 were waited for; matrix products, arithmetic and copies ran while one was open for 14% of the time, Pallas kernels for 22%

profile of v8, /device:TPU:1, one launch (start us, length us, event | category | flops | bytes accessed | tf_op | source)
XLA Modules:
  0.0 113.4 jit_solution(3298556839331420904)
XLA Ops:
  7.2 0.7 all-gather.6.cloned.1.call-update
  7.9 0.7 add_select_fusion.3
  8.6 0.8 fusion.12
  9.6 0.7 fusion.1
  10.3 1.1 constant_dynamic-slice_fusion.1
  11.4 1.4 %gather_fusion = bf16[32,16,512]{2,1,0:T(8,128)(2,1)} fusion(bf16[32,16,512]{2,1,0:T(8,128)(2,1)S(1)} %constant_dynamic-slice_fusion.1, s32[1024]{0:T(1024)S(1)} %pad_clamp_fusion.3), kind=kCustom, calls=%fused_computation.2 | custom fusion | bytes 1048704 | tf_op jit(solution)/shard_map/gather | solution.py:202
  12.8 12.0 %all-to-all-start = ((bf16[32,16,512]{2,1,0:T(8,128)(2,1)}), bf16[32,16,512]{2,1,0:T(8,128)(2,1)S(1)}, u32[]{:S(2)}, u32[]{:S(2)}) async-start(bf16[32,16,512]{2,1,0:T(8,128)(2,1)} %gather_fusion), calls=%async_computation | async-start | bytes 1048576 | tf_op jit(solution)/shard_map/all_to_all | solution.py:203
  25.1 16.0 %all-to-all-done = bf16[32,16,512]{2,1,0:T(8,128)(2,1)S(1)} async-done(((bf16[32,16,512]{2,1,0:T(8,128)(2,1)}), bf16[32,16,512]{2,1,0:T(8,128)(2,1)S(1)}, u32[]{:S(2)}, u32[]{:S(2)}) %all-to-all-start) | async-done | bytes 524320 | tf_op jit(solution)/shard_map/all_to_all | solution.py:203
  41.1 1.3 %gather_fusion.1 = bf16[16,16,512]{2,1,0:T(8,128)(2,1)} fusion(bf16[32,16,512]{2,1,0:T(8,128)(2,1)S(1)} %all-to-all-done, s32[1024]{0:T(1024)S(1)} %pad_clamp_fusion.2), kind=kCustom, calls=%fused_computation.3 | custom fusion | bytes 524352 | tf_op jit(solution)/shard_map/gather | solution.py:205
  42.7 0.6 iota_reduce_fusion
  43.3 1.0 constant_dynamic-slice_fusion
  44.3 1.4 %gather_fusion.2 = bf16[32,16,512]{2,1,0:T(8,128)(2,1)} fusion(bf16[16,16,512]{2,1,0:T(8,128)(2,1)S(1)} %constant_dynamic-slice_fusion, s32[1024]{0:T(1024)S(1)} %pad_clamp_fusion.1), kind=kCustom, calls=%fused_computation.4 | custom fusion | bytes 1048704 | tf_op jit(solution)/shard_map/gather | solution.py:218
  45.7 8.1 %all-to-all-start.1 = ((bf16[32,16,512]{2,1,0:T(8,128)(2,1)}), bf16[32,16,512]{2,1,0:T(8,128)(2,1)S(1)}, u32[]{:S(2)}, u32[]{:S(2)}) async-start(bf16[32,16,512]{2,1,0:T(8,128)(2,1)} %gather_fusion.2), calls=%async_computation.1 | async-start | bytes 1048576 | tf_op jit(solution)/shard_map/all_to_all | solution.py:219
  53.9 0.7 gather_fusion.5
  54.6 0.7 gather_fusion.4
  55.3 0.6 compare_select_fusion.1
  55.9 14.5 %all-to-all-done.1 = bf16[32,16,512]{2,1,0:T(8,128)(2,1)S(1)} async-done(((bf16[32,16,512]{2,1,0:T(8,128)(2,1)}), bf16[32,16,512]{2,1,0:T(8,128)(2,1)S(1)}, u32[]{:S(2)}, u32[]{:S(2)}) %all-to-all-start.1) | async-done | bytes 524320 | tf_op jit(solution)/shard_map/all_to_all | solution.py:219
  70.4 1.3 %gather_fusion.3 = bf16[16,16,512]{2,1,0:T(8,128)(2,1)} fusion(bf16[32,16,512]{2,1,0:T(8,128)(2,1)S(1)} %all-to-all-done.1, s32[1024]{0:T(1024)S(1)} %pad_clamp_fusion), kind=kCustom, calls=%fused_computation.5 | custom fusion | bytes 524352 | tf_op jit(solution)/shard_map/gather | solution.py:225
  71.7 0.6 dynamic_slice.25
  74.2 4.7 %shard_map.78.pool_hbm = bf16[32,128,512]{2,1,0:T(8,128)(2,1)} custom-call(bf16[32,128,512]{2,1,0:T(8,128)(2,1)} %src_ref.1), custom_call_target="tpu_custom_call" | custom-call | tf_op jit(solution)/shard_map/pallas_call | solution.py:163
  79.7 2.0 %copy.26 = bf16[8,16,16,512]{3,2,0,1:T(8,128)(2,1)S(1)} copy(bf16[8,16,16,512]{3,2,1,0:T(8,128)(2,1)} %bitcast.58) | data formatting | bytes 4194304 | tf_op jit(solution)/shard_map/all_gather | solution.py:206
  81.9 0.4 copy-done.1
  82.3 20.4 %shard_map.77 = bf16[256,2560]{1,0:T(8,128)(2,1)} custom-call(s32[2]{0:T(128)S(1)} %pad_add_fusion.meta, bf16[256,2560]{1,0:T(8,128)(2,1)S(1)} %bitcast.57, bf16[2048,512]{1,0:T(8,128)(2,1)S(1)} %bitcast.54, bf16[2048,512]{1,0:T(8,128)(2,1)S(1)} %bitcast.56), custom_call_target="tpu_custom_call" | custom-call | tf_op jit(solution)/shard_map/pallas_call | solution.py:90
  102.7 4.1 %shard_map.79 = bf16[32,128,512]{2,1,0:T(8,128)(2,1)} custom-call(s32[16]{0:T(128)} %get-tuple-element.11.targets, bf16[8,16,16,512]{3,2,1,0:T(8,128)(2,1)} %bitcast.59, bf16[32,128,512]{2,1,0:T(8,128)(2,1)} %shard_map.78.pool_hbm), custom_call_target="tpu_custom_call", output_to_operand_aliasing={{}: (2, {})} | custom-call | tf_op jit(solution)/shard_map/pallas_call | solution.py:138
  (33 shorter events, 1.2 us)
Async XLA Ops:
  7.2 36.2 %all-gather.6.cloned.1.call-start = ((), (), s32[]{:S(2)}) async-start(), calls=%async_computation.2 | async-start | bytes 2359296 | tf_op jit(solution)/shard_map/all_gather | solution.py:190
  12.8 28.3 %all-to-all-start = ((bf16[32,16,512]{2,1,0:T(8,128)(2,1)}), bf16[32,16,512]{2,1,0:T(8,128)(2,1)S(1)}, u32[]{:S(2)}, u32[]{:S(2)}) async-start(bf16[32,16,512]{2,1,0:T(8,128)(2,1)} %gather_fusion), calls=%async_computation | async-start | bytes 1048576 | tf_op jit(solution)/shard_map/all_to_all | solution.py:203
  24.8 29.7 %copy-start.2 = (s32[32,16]{0,1:T(8,128)S(1)}, s32[32,16]{0,1:T(8,128)}, u32[]{:S(2)}) copy-start(s32[32,16]{0,1:T(8,128)} %param.12) | copy-start | bytes 6148
  24.8 54.9 %all-gather.8.cloned.1.call-start = ((), (), s32[]{:S(2)}) async-start(), calls=%async_computation.3 | async-start | bytes 2359296 | tf_op jit(solution)/shard_map/all_gather | solution.py:206
  44.3 27.4 %copy-start.3 = (s32[32]{0:T(128)S(1)}, s32[32]{0:T(128)}, u32[]{:S(2)}) copy-start(s32[32]{0:T(128)} %param.13) | copy-start | bytes 388
  45.7 24.7 %all-to-all-start.1 = ((bf16[32,16,512]{2,1,0:T(8,128)(2,1)}), bf16[32,16,512]{2,1,0:T(8,128)(2,1)S(1)}, u32[]{:S(2)}, u32[]{:S(2)}) async-start(bf16[32,16,512]{2,1,0:T(8,128)(2,1)} %gather_fusion.2), calls=%async_computation.1 | async-start | bytes 1048576 | tf_op jit(solution)/shard_map/all_to_all | solution.py:219
  53.8 48.9 %all-gather.10.cloned.1.call-start = ((), (), s32[]{:S(2)}) async-start(), calls=%async_computation.4 | async-start | bytes 2359296 | tf_op jit(solution)/shard_map/all_gather | solution.py:225
  79.7 2.2 %copy-start = (bf16[1,2048,512]{2,1,0:T(8,128)(2,1)S(1)}, bf16[1,2048,512]{2,1,0:T(8,128)(2,1)}, u32[]{:S(2)}) copy-start(bf16[1,2048,512]{2,1,0:T(8,128)(2,1)} %all-gather.6.cloned.1.call-done) | copy-start | bytes 6291460
  79.7 2.6 %copy-start.1 = (bf16[1,256,2560]{2,1,0:T(8,128)(2,1)S(1)}, bf16[1,256,2560]{2,1,0:T(8,128)(2,1)}, u32[]{:S(2)}) copy-start(bf16[1,256,2560]{2,1,0:T(8,128)(2,1)} %param.8) | copy-start | bytes 3932164
Sparse Core Ops, SparseCore 0:
  9.8 31.9 all-gather.5
  43.7 28.2 all-gather.7
  73.9 28.2 all-gather.9

commit v9 on v8

--- a/solution.py
+++ b/solution.py
@@ -213,8 +213,19 @@
         mine_rank[None, None, :] == jnp.arange(cap_new)[None, :, None]
     )
     page_pick = jnp.sum(jnp.where(dest_wanted, jnp.arange(new_pages)[None, None, :], 0), axis=2)
-    fresh_pages = fresh_keys.reshape(new_pages, page_rows, key_width)
-    fresh_piece = lax.dynamic_slice_in_dim(fresh_pages, piece_start, piece_rows, axis=1)
+    own_pages = new_kv[0].reshape(-1, groups, piece_rows, key_width)
+    shifted = [lax.dynamic_index_in_dim(own_pages, piece_index, 1, keepdims=False)]
+    for shift in range(1, groups):
+        outgoing_piece = lax.dynamic_index_in_dim(
+            own_pages, (piece_index + shift) % groups, 1, keepdims=False
+        )
+        shifted.append(lax.ppermute(
+            outgoing_piece, "group", [(i, (i + shift) % groups) for i in range(groups)]
+        ))
+    by_shift = jnp.stack(shifted)
+    fresh_piece = by_shift[(piece_index - jnp.arange(groups)) % groups].reshape(
+        new_pages, piece_rows, key_width
+    )
     parcels = fresh_piece[page_pick.reshape(-1)]
     arrived = lax.all_to_all(parcels, "blk", split_axis=0, concat_axis=0, tiled=True)
     land_here = new_owner == my_block

time: 114 us -> 143 us (1.25)
  blocking collectives: 0 us -> 20.8 us
  waiting for transfers between devices: 31.3 us -> 35.7 us
  starting transfers between devices: 20.2 us -> 23.4 us
    all_to_all x0 -> x1, blocking collectives: none -> 20.8 us  [shards_body(): lax.all_to_all(parcels, 'blk', split_axis=0, concat_axis=0, tiled=True)]
    all_to_all x1 -> x0, waiting for transfers between devices: 14.5 us -> none  [shards_body(): lax.all_to_all(parcels, 'blk', split_axis=0, concat_axis=0, tiled=True)]
    ppermute x0 -> x7, starting transfers between devices: none -> 11.2 us  [shards_body(): lax.ppermute(outgoing_piece, 'group', [(i, (i + shift) % groups) for i in...]
    all_gather x1, waiting for transfers between devices: 0.02 us -> 8.18 us  [shards_body(): landed = lax.all_gather(arrived[land_slot], 'group', axis=0, tiled=False)]
    all_to_all x1 -> x0, starting transfers between devices: 8.09 us -> none  [shards_body(): lax.all_to_all(parcels, 'blk', split_axis=0, concat_axis=0, tiled=True)]
    all_gather x1, waiting for transfers between devices: 0.01 us -> 6.93 us  [shards_body(): fresh_keys = lax.all_gather(new_kv, 'group', axis=1, tiled=True)[0]]
    ppermute x0 -> x7, waiting for transfers between devices: none -> 3.81 us  [shards_body(): lax.ppermute(outgoing_piece, 'group', [(i, (i + shift) % groups) for i in...]
  transfers between devices with their start and end apart: 5 -> 11, of which waited for: 2 -> 6; matrix products, arithmetic and copies ran while one was open for 14% -> 4% of each run, Pallas kernels for 22% -> 18%
where the time goes in v9:
time: 143 us; the launch traced here: 142 us
  waiting for transfers between devices  35.7 us (25%)
  Pallas kernels  29.3 us (20%)
  starting transfers between devices  23.4 us (16%)
  blocking collectives  20.8 us (15%)
  between operations  16.4 us (11%)
  local copies, waits for them, and re-layouts  11.8 us (8%)
  other arithmetic  4.9 us (3%)
    all_to_all x1, blocking collectives, shards_body(): lax.all_to_all(parcels, 'blk', split_axis=0, concat_axis=0, tiled=True)  20.8 us
    pallas_call x1, Pallas kernels, window_attention(): pl.pallas_call(body, out_shape=jax.ShapeDtypeStruct((tok_rows, width), qu...  20.4 us
    all_to_all x1, waiting for transfers between devices, shards_body(): lax.all_to_all(outgoing, 'blk', split_axis=0, concat_axis=0, tiled=True)  16 us
    all_to_all x1, starting transfers between devices, shards_body(): lax.all_to_all(outgoing, 'blk', split_axis=0, concat_axis=0, tiled=True)  12 us
    ppermute x7, starting transfers between devices, shards_body(): lax.ppermute(outgoing_piece, 'group', [(i, (i + shift) % groups) for i in...  11.2 us
    all_gather x1, waiting for transfers between devices, shards_body(): landed = lax.all_gather(arrived[land_slot], 'group', axis=0, tiled=False)  8.18 us
    all_gather x1, waiting for transfers between devices, shards_body(): fresh_keys = lax.all_gather(new_kv, 'group', axis=1, tiled=True)[0]  6.93 us
    pallas_call x1, Pallas kernels, copy_pool(): pl.pallas_call(copy_kernel, out_shape=jax.ShapeDtypeStruct(kv_pool.shape,...  4.79 us
  transfers between devices with their start and end apart: 11, of which 6 were waited for; matrix products, arithmetic and copies ran while one was open for 4% of the time, Pallas kernels for 18%

profile of v9, /device:TPU:1, one launch (start us, length us, event | category | flops | bytes accessed | tf_op | source)
XLA Modules:
  0.0 142.2 jit_solution(9551178587391755409)
XLA Ops:
  7.2 0.7 add_select_fusion
  7.9 0.8 fusion.14
  11.6 0.7 fusion.1
  12.8 1.1 constant_dynamic-slice_fusion
  14.0 1.4 gather_fusion
  15.3 12.0 %all-to-all-start = ((bf16[32,16,512]{2,1,0:T(8,128)(2,1)}), bf16[32,16,512]{2,1,0:T(8,128)(2,1)S(1)}, u32[]{:S(2)}, u32[]{:S(2)}) async-start(bf16[32,16,512]{2,1,0:T(8,128)(2,1)} %gather_fusion), calls=%async_computation | async-start | bytes 1048576 | tf_op jit(solution)/shard_map/all_to_all | solution.py:203
  27.6 16.0 %all-to-all-done = bf16[32,16,512]{2,1,0:T(8,128)(2,1)S(1)} async-done(((bf16[32,16,512]{2,1,0:T(8,128)(2,1)}), bf16[32,16,512]{2,1,0:T(8,128)(2,1)S(1)}, u32[]{:S(2)}, u32[]{:S(2)}) %all-to-all-start) | async-done | bytes 524320 | tf_op jit(solution)/shard_map/all_to_all | solution.py:203
  43.7 1.3 gather_fusion.1
  45.9 3.5 %collective-permute-start = (bf16[2,16,512]{2,1,0:T(8,128)(2,1)S(1)}, bf16[2,16,512]{2,1,0:T(8,128)(2,1)S(1)}, u32[]{:S(2)}, u32[]{:S(2)}) collective-permute-start(bf16[2,16,512]{2,1,0:T(8,128)(2,1)S(1)} %get-tuple-element.16), channel_id=1, source_target_pairs={{0,1},{1,2},{2,3},{3,4},{4,5},{5,6},{6,7},{7,0},{8,9},{9,10},{10,1... | collective-permute-start | bytes 98312 | tf_op jit(solution)/shard_map/ppermute | solution.py:222
  49.4 1.2 collective-permute-start.1
  50.6 1.6 %collective-permute-start.2 = (bf16[2,16,512]{2,1,0:T(8,128)(2,1)S(1)}, bf16[2,16,512]{2,1,0:T(8,128)(2,1)S(1)}, u32[]{:S(2)}, u32[]{:S(2)}) collective-permute-start(bf16[2,16,512]{2,1,0:T(8,128)(2,1)S(1)} %get-tuple-element.14), channel_id=1, source_target_pairs={{0,3},{1,4},{2,5},{3,6},{4,7},{5,0},{6,1},{7,2},{8,11},{9,12},{10,... | collective-permute-start | bytes 98312 | tf_op jit(solution)/shard_map/ppermute | solution.py:222
  52.8 1.9 %collective-permute-start.4 = (bf16[2,16,512]{2,1,0:T(8,128)(2,1)S(1)}, bf16[2,16,512]{2,1,0:T(8,128)(2,1)S(1)}, u32[]{:S(2)}, u32[]{:S(2)}) collective-permute-start(bf16[2,16,512]{2,1,0:T(8,128)(2,1)S(1)} %get-tuple-element.12), channel_id=1, source_target_pairs={{0,5},{1,6},{2,7},{3,0},{4,1},{5,2},{6,3},{7,4},{8,13},{9,14},{10,... | collective-permute-start | bytes 98312 | tf_op jit(solution)/shard_map/ppermute | solution.py:222
  55.1 0.7 collective-permute-start.5
  55.8 1.7 %collective-permute-start.6 = (bf16[2,16,512]{2,1,0:T(8,128)(2,1)S(1)}, bf16[2,16,512]{2,1,0:T(8,128)(2,1)S(1)}, u32[]{:S(2)}, u32[]{:S(2)}) collective-permute-start(bf16[2,16,512]{2,1,0:T(8,128)(2,1)S(1)} %get-tuple-element.10), channel_id=1, source_target_pairs={{0,7},{1,0},{2,1},{3,2},{4,3},{5,4},{6,5},{7,6},{8,15},{9,8},{10,9... | collective-permute-start | bytes 98312 | tf_op jit(solution)/shard_map/ppermute | solution.py:222
  58.0 3.3 %collective-permute-done.6 = bf16[2,16,512]{2,1,0:T(8,128)(2,1)S(1)} collective-permute-done((bf16[2,16,512]{2,1,0:T(8,128)(2,1)S(1)}, bf16[2,16,512]{2,1,0:T(8,128)(2,1)S(1)}, u32[]{:S(2)}, u32[]{:S(2)}) %collective-permute-start.6) | collective-permute-done | bytes 32800 | tf_op jit(solution)/shard_map/ppermute | solution.py:222
  62.5 20.8 %all_to_all.10 = bf16[32,16,512]{2,1,0:T(8,128)(2,1)S(1)} all-to-all(bf16[32,16,512]{2,1,0:T(8,128)(2,1)S(1)} %gather_fusion.3), channel_id=1, replica_groups=mesh['blk'=32,'group'=8] {'blk'}, dimensions={0} | all-to-all | bytes 1048576 | tf_op jit(solution)/shard_map/all_to_all | solution.py:230
  83.3 1.3 gather_fusion.4
  84.6 4.8 %shard_map.78.pool_hbm = bf16[32,128,512]{2,1,0:T(8,128)(2,1)} custom-call(bf16[32,128,512]{2,1,0:T(8,128)(2,1)} %src_ref.1), custom_call_target="tpu_custom_call" | custom-call | tf_op jit(solution)/shard_map/pallas_call | solution.py:163
  92.4 2.0 %copy.26 = bf16[8,16,16,512]{3,2,0,1:T(8,128)(2,1)S(1)} copy(bf16[8,16,16,512]{3,2,1,0:T(8,128)(2,1)} %bitcast.91) | data formatting | bytes 4194304 | tf_op jit(solution)/shard_map/all_gather | solution.py:206
  94.4 6.9 %all-gather.6.cloned.1.call-done = bf16[1,2048,512]{2,1,0:T(8,128)(2,1)} async-done(((bf16[1,256,512]{2,1,0:T(8,128)(2,1)}), bf16[1,2048,512]{2,1,0:T(8,128)(2,1)}) %all-gather.6.cloned.1.call-update) | async-done | bytes 2097168 | tf_op jit(solution)/shard_map/all_gather | solution.py:190
  101.4 1.6 %copy-done = bf16[1,2048,512]{2,1,0:T(8,128)(2,1)S(1)} copy-done((bf16[1,2048,512]{2,1,0:T(8,128)(2,1)S(1)}, bf16[1,2048,512]{2,1,0:T(8,128)(2,1)}, u32[]{:S(2)}) %copy-start) | copy-done | bytes 2097176
  103.0 20.4 %shard_map.77 = bf16[256,2560]{1,0:T(8,128)(2,1)} custom-call(s32[2]{0:T(128)S(1)} %pad_add_fusion.meta, bf16[256,2560]{1,0:T(8,128)(2,1)S(1)} %bitcast.89, bf16[2048,512]{1,0:T(8,128)(2,1)S(1)} %bitcast.87, bf16[2048,512]{1,0:T(8,128)(2,1)S(1)} %bitcast.88), custom_call_target="tpu_custom_call" | custom-call | tf_op jit(solution)/shard_map/pallas_call | solution.py:90
  123.3 8.2 %all-gather.10.cloned.1.call-done = bf16[128,16,512]{2,1,0:T(8,128)(2,1)} async-done(((bf16[16,16,512]{2,1,0:T(8,128)(2,1)}), bf16[128,16,512]{2,1,0:T(8,128)(2,1)}) %all-gather.10.cloned.1.call-update) | async-done | bytes 2097168 | tf_op jit(solution)/shard_map/all_gather | solution.py:236
  131.5 4.1 %shard_map.79 = bf16[32,128,512]{2,1,0:T(8,128)(2,1)} custom-call(s32[16]{0:T(128)} %get-tuple-element.18.targets, bf16[8,16,16,512]{3,2,1,0:T(8,128)(2,1)} %bitcast.92, bf16[32,128,512]{2,1,0:T(8,128)(2,1)} %shard_map.78.pool_hbm), custom_call_target="tpu_custom_call", output_to_operand_aliasing={{}: (2, {})} | custom-call | tf_op jit(solution)/shard_map/pallas_call | solution.py:138
  (56 shorter events, 7.7 us)
Async XLA Ops:
  12.8 33.0 %copy-start.2 = (bf16[1,256,512]{2,1,0:T(8,128)(2,1)S(1)}, bf16[1,256,512]{2,1,0:T(8,128)(2,1)}, u32[]{:S(2)}) copy-start(bf16[1,256,512]{2,1,0:T(8,128)(2,1)} %param.9) | copy-start | bytes 786436
  15.3 28.3 %all-to-all-start = ((bf16[32,16,512]{2,1,0:T(8,128)(2,1)}), bf16[32,16,512]{2,1,0:T(8,128)(2,1)S(1)}, u32[]{:S(2)}, u32[]{:S(2)}) async-start(bf16[32,16,512]{2,1,0:T(8,128)(2,1)} %gather_fusion), calls=%async_computation | async-start | bytes 1048576 | tf_op jit(solution)/shard_map/all_to_all | solution.py:203
  27.4 65.0 %all-gather.8.cloned.1.call-start = ((), (), s32[]{:S(2)}) async-start(), calls=%async_computation.3 | async-start | bytes 2359296 | tf_op jit(solution)/shard_map/all_gather | solution.py:206
  44.9 56.4 %all-gather.6.cloned.1.call-start = ((), (), s32[]{:S(2)}) async-start(), calls=%async_computation.2 | async-start | bytes 2359296 | tf_op jit(solution)/shard_map/all_gather | solution.py:190
  45.7 85.8 %all-gather.10.cloned.1.call-start = ((), (), s32[]{:S(2)}) async-start(), calls=%async_computation.4 | async-start | bytes 2359296 | tf_op jit(solution)/shard_map/all_gather | solution.py:236
  45.9 9.2 %collective-permute-start = (bf16[2,16,512]{2,1,0:T(8,128)(2,1)S(1)}, bf16[2,16,512]{2,1,0:T(8,128)(2,1)S(1)}, u32[]{:S(2)}, u32[]{:S(2)}) collective-permute-start(bf16[2,16,512]{2,1,0:T(8,128)(2,1)S(1)} %get-tuple-element.16), channel_id=1, source_target_pairs={{0,1},{1,2},{2,3},{3,4},{4,5},{5,6},{6,7},{7,0},{8,9},{9,10},{10,1... | collective-permute-start | bytes 98312 | tf_op jit(solution)/shard_map/ppermute | solution.py:222
  49.4 6.4 %collective-permute-start.1 = (bf16[2,16,512]{2,1,0:T(8,128)(2,1)S(1)}, bf16[2,16,512]{2,1,0:T(8,128)(2,1)S(1)}, u32[]{:S(2)}, u32[]{:S(2)}) collective-permute-start(bf16[2,16,512]{2,1,0:T(8,128)(2,1)S(1)} %get-tuple-element.15), channel_id=1, source_target_pairs={{0,2},{1,3},{2,4},{3,5},{4,6},{5,7},{6,0},{7,1},{8,10},{9,11},{10,... | collective-permute-start | bytes 98312 | tf_op jit(solution)/shard_map/ppermute | solution.py:222
  50.6 6.9 %collective-permute-start.2 = (bf16[2,16,512]{2,1,0:T(8,128)(2,1)S(1)}, bf16[2,16,512]{2,1,0:T(8,128)(2,1)S(1)}, u32[]{:S(2)}, u32[]{:S(2)}) collective-permute-start(bf16[2,16,512]{2,1,0:T(8,128)(2,1)S(1)} %get-tuple-element.14), channel_id=1, source_target_pairs={{0,3},{1,4},{2,5},{3,6},{4,7},{5,0},{6,1},{7,2},{8,11},{9,12},{10,... | collective-permute-start | bytes 98312 | tf_op jit(solution)/shard_map/ppermute | solution.py:222
  52.2 5.3 %collective-permute-start.3 = (bf16[2,16,512]{2,1,0:T(8,128)(2,1)S(1)}, bf16[2,16,512]{2,1,0:T(8,128)(2,1)S(1)}, u32[]{:S(2)}, u32[]{:S(2)}) collective-permute-start(bf16[2,16,512]{2,1,0:T(8,128)(2,1)S(1)} %get-tuple-element.13), channel_id=1, source_target_pairs={{0,4},{1,5},{2,6},{3,7},{4,0},{5,1},{6,2},{7,3},{8,12},{9,13},{10,... | collective-permute-start | bytes 98312 | tf_op jit(solution)/shard_map/ppermute | solution.py:222
  52.8 4.8 %collective-permute-start.4 = (bf16[2,16,512]{2,1,0:T(8,128)(2,1)S(1)}, bf16[2,16,512]{2,1,0:T(8,128)(2,1)S(1)}, u32[]{:S(2)}, u32[]{:S(2)}) collective-permute-start(bf16[2,16,512]{2,1,0:T(8,128)(2,1)S(1)} %get-tuple-element.12), channel_id=1, source_target_pairs={{0,5},{1,6},{2,7},{3,0},{4,1},{5,2},{6,3},{7,4},{8,13},{9,14},{10,... | collective-permute-start | bytes 98312 | tf_op jit(solution)/shard_map/ppermute | solution.py:222
  55.1 3.0 %collective-permute-start.5 = (bf16[2,16,512]{2,1,0:T(8,128)(2,1)S(1)}, bf16[2,16,512]{2,1,0:T(8,128)(2,1)S(1)}, u32[]{:S(2)}, u32[]{:S(2)}) collective-permute-start(bf16[2,16,512]{2,1,0:T(8,128)(2,1)S(1)} %get-tuple-element.11), channel_id=1, source_target_pairs={{0,6},{1,7},{2,0},{3,1},{4,2},{5,3},{6,4},{7,5},{8,14},{9,15},{10,... | collective-permute-start | bytes 98312 | tf_op jit(solution)/shard_map/ppermute | solution.py:222
  55.8 5.5 %collective-permute-start.6 = (bf16[2,16,512]{2,1,0:T(8,128)(2,1)S(1)}, bf16[2,16,512]{2,1,0:T(8,128)(2,1)S(1)}, u32[]{:S(2)}, u32[]{:S(2)}) collective-permute-start(bf16[2,16,512]{2,1,0:T(8,128)(2,1)S(1)} %get-tuple-element.10), channel_id=1, source_target_pairs={{0,7},{1,0},{2,1},{3,2},{4,3},{5,4},{6,5},{7,6},{8,15},{9,8},{10,9... | collective-permute-start | bytes 98312 | tf_op jit(solution)/shard_map/ppermute | solution.py:222
  84.6 4.8 %copy-start.3 = (s32[32]{0:T(128)S(1)}, s32[32]{0:T(128)}, u32[]{:S(2)}) copy-start(s32[32]{0:T(128)} %param.13) | copy-start | bytes 388
  92.4 9.0 %copy-start.1 = (bf16[1,256,2560]{2,1,0:T(8,128)(2,1)S(1)}, bf16[1,256,2560]{2,1,0:T(8,128)(2,1)}, u32[]{:S(2)}) copy-start(bf16[1,256,2560]{2,1,0:T(8,128)(2,1)} %param.8) | copy-start | bytes 3932164
  101.4 1.6 %copy-start = (bf16[1,2048,512]{2,1,0:T(8,128)(2,1)S(1)}, bf16[1,2048,512]{2,1,0:T(8,128)(2,1)}, u32[]{:S(2)}) copy-start(bf16[1,2048,512]{2,1,0:T(8,128)(2,1)} %all-gather.6.cloned.1.call-done) | copy-start | bytes 6291460
Sparse Core Ops, SparseCore 0:
  45.1 26.0 all-gather.7
  73.1 28.2 all-gather.5
  103.2 28.2 all-gather.9

commit v10 on v8

--- a/solution.py
+++ b/solution.py
@@ -17,11 +17,6 @@
 
 def pick_rows(wanted, values):
     return jnp.sum(jnp.where(wanted, values[:, None, :], 0), axis=2)
-
-
-def regroup(pieces):
-    groups, pages, piece_rows, width = pieces.shape
-    return pieces.transpose(1, 0, 2, 3).reshape(pages, groups * piece_rows, width)
 
 
 def window_kernel(meta, q_ref, cached_hbm, fresh_hbm, out_ref, keys, bias, sems, *, chunk, chunks,
@@ -110,31 +105,27 @@
 
 
 def pool_kernel(targets, landed_hbm, pool_hbm, out_hbm, staged, in_sems, out_sems):
-    groups, pages, piece_rows, _ = landed_hbm.shape
-    for grp in range(groups):
-        pltpu.make_async_copy(landed_hbm.at[grp], staged.at[grp], in_sems.at[grp]).start()
-
-    def each_target(grp, begin):
-        for page in range(pages):
-            target = targets[page]
-
-            @pl.when(target < pool_hbm.shape[0])
-            def _():
-                cp = pltpu.make_async_copy(
-                    staged.at[grp, page], out_hbm.at[target, pl.ds(grp * piece_rows, piece_rows)],
-                    out_sems.at[page, grp],
-                )
-                cp.start() if begin else cp.wait()
-
-    for grp in range(groups):
-        pltpu.make_async_copy(landed_hbm.at[grp], staged.at[grp], in_sems.at[grp]).wait()
-        each_target(grp, True)
-    for grp in range(groups):
-        each_target(grp, False)
+    pages = landed_hbm.shape[0]
+    for page in range(pages):
+        pltpu.make_async_copy(landed_hbm.at[page], staged.at[page], in_sems.at[page]).start()
+
+    def each_target(page, begin):
+        target = targets[page]
+
+        @pl.when(target < pool_hbm.shape[0])
+        def _():
+            cp = pltpu.make_async_copy(staged.at[page], out_hbm.at[target], out_sems.at[page])
+            cp.start() if begin else cp.wait()
+
+    for page in range(pages):
+        pltpu.make_async_copy(landed_hbm.at[page], staged.at[page], in_sems.at[page]).wait()
+        each_target(page, True)
+    for page in range(pages):
+        each_target(page, False)
 
 
 def write_pool(kv_pool, landed, targets):
-    groups, pages = landed.shape[:2]
+    pages = landed.shape[0]
     return pl.pallas_call(
         pool_kernel,
         out_shape=jax.ShapeDtypeStruct(kv_pool.shape, kv_pool.dtype),
@@ -145,8 +136,8 @@
             out_specs=pl.BlockSpec(memory_space=pl.ANY),
             scratch_shapes=[
                 pltpu.VMEM(landed.shape, landed.dtype),
-                pltpu.SemaphoreType.DMA((groups,)),
-                pltpu.SemaphoreType.DMA((pages, groups)),
+                pltpu.SemaphoreType.DMA((pages,)),
+                pltpu.SemaphoreType.DMA((pages,)),
             ],
         ),
         input_output_aliases={2: 0},
@@ -203,7 +194,7 @@
     received = lax.all_to_all(outgoing, "blk", split_axis=0, concat_axis=0, tiled=True)
     pool_out = copy_pool(kv_pool)
     cached_piece = received[arrival]
-    cached = regroup(lax.all_gather(cached_piece, "group", axis=0, tiled=False))
+    cached = lax.all_gather(cached_piece, "group", axis=1, tiled=True)
 
     new_owner = append_table // per_owner
     new_rank = earlier_same(new_owner)
@@ -222,7 +213,7 @@
     land_slot = land_source * cap_new + jnp.take_along_axis(new_rank, land_source[None, :], axis=0)[0]
     land_ids = jnp.take_along_axis(append_table % per_owner, land_source[None, :], axis=0)[0]
     land_live = jnp.any(land_here, axis=0)
-    landed = lax.all_gather(arrived[land_slot], "group", axis=0, tiled=False)
+    landed = lax.all_gather(arrived[land_slot], "group", axis=1, tiled=True)
     targets = jnp.where(land_live, land_ids, per_owner)
     new_pool = write_pool(pool_out, landed, targets)
 

time: 114 us -> 112 us (0.982)
    all_gather x1 -> x0, local copies, waits for them, and re-layouts: 1.97 us -> none  [shards_body(): cached = regroup(lax.all_gather(cached_piece, 'group', axis=0, tiled=False))]
  transfers between devices with their start and end apart: 5 -> 5, of which waited for: 2 -> 3; matrix products, arithmetic and copies ran while one was open for 14% -> 12% of each run, Pallas kernels for 22% -> 23%
where the time goes in v10:
time: 112 us
  waiting for transfers between devices  31.3 us (28%)
  Pallas kernels  28.7 us (26%)
  starting transfers between devices  20.2 us (18%)
  between operations  16.5 us (15%)
  local copies, waits for them, and re-layouts  10.9 us (10%)
  other arithmetic  4.25 us (4%)
    pallas_call x1, Pallas kernels, window_attention(): pl.pallas_call(body, out_shape=jax.ShapeDtypeStruct((tok_rows, width), qu...  20.4 us
    all_to_all x1, waiting for transfers between devices, shards_body(): lax.all_to_all(outgoing, 'blk', split_axis=0, concat_axis=0, tiled=True)  16 us
    all_to_all x1, waiting for transfers between devices, shards_body(): lax.all_to_all(parcels, 'blk', split_axis=0, concat_axis=0, tiled=True)  14.5 us
    all_to_all x1, starting transfers between devices, shards_body(): lax.all_to_all(outgoing, 'blk', split_axis=0, concat_axis=0, tiled=True)  12 us
    all_to_all x1, starting transfers between devices, shards_body(): lax.all_to_all(parcels, 'blk', split_axis=0, concat_axis=0, tiled=True)  8.09 us
    pallas_call x1, Pallas kernels, copy_pool(): pl.pallas_call(copy_kernel, out_shape=jax.ShapeDtypeStruct(kv_pool.shape,...  5.06 us
    pallas_call x1, Pallas kernels, write_pool(): pl.pallas_call(pool_kernel, out_shape=jax.ShapeDtypeStruct(kv_pool.shape,...  3.23 us
  transfers between devices with their start and end apart: 5, of which 3 were waited for; matrix products, arithmetic and copies ran while one was open for 12% of the time, Pallas kernels for 23%

profile of v10, /device:TPU:1, one launch (start us, length us, event | category | flops | bytes accessed | tf_op | source)
XLA Modules:
  0.0 111.9 jit_solution(7171407059883577433)
XLA Ops:
  7.2 0.7 all-gather.6.cloned.1.call-update
  7.9 0.7 add_select_fusion.3
  8.6 0.8 fusion.12
  9.6 0.7 fusion.1
  10.3 1.1 constant_dynamic-slice_fusion.1
  11.4 1.4 %gather_fusion = bf16[32,16,512]{2,1,0:T(8,128)(2,1)} fusion(bf16[32,16,512]{2,1,0:T(8,128)(2,1)S(1)} %constant_dynamic-slice_fusion.1, s32[1024]{0:T(1024)S(1)} %pad_clamp_fusion.3), kind=kCustom, calls=%fused_computation.2 | custom fusion | bytes 1048704 | tf_op jit(solution)/shard_map/gather | solution.py:193
  12.8 12.0 %all-to-all-start = ((bf16[32,16,512]{2,1,0:T(8,128)(2,1)}), bf16[32,16,512]{2,1,0:T(8,128)(2,1)S(1)}, u32[]{:S(2)}, u32[]{:S(2)}) async-start(bf16[32,16,512]{2,1,0:T(8,128)(2,1)} %gather_fusion), calls=%async_computation | async-start | bytes 1048576 | tf_op jit(solution)/shard_map/all_to_all | solution.py:194
  24.9 0.2 dynamic-slice_reduce_fusion
  25.1 16.0 %all-to-all-done = bf16[32,16,512]{2,1,0:T(8,128)(2,1)S(1)} async-done(((bf16[32,16,512]{2,1,0:T(8,128)(2,1)}), bf16[32,16,512]{2,1,0:T(8,128)(2,1)S(1)}, u32[]{:S(2)}, u32[]{:S(2)}) %all-to-all-start) | async-done | bytes 524320 | tf_op jit(solution)/shard_map/all_to_all | solution.py:194
  41.1 1.3 %gather_fusion.1 = bf16[16,16,512]{2,1,0:T(8,128)(2,1)} fusion(bf16[32,16,512]{2,1,0:T(8,128)(2,1)S(1)} %all-to-all-done, s32[1024]{0:T(1024)S(1)} %pad_clamp_fusion.2), kind=kCustom, calls=%fused_computation.3 | custom fusion | bytes 524352 | tf_op jit(solution)/shard_map/gather | solution.py:196
  42.7 0.6 iota_reduce_fusion
  43.3 1.0 constant_dynamic-slice_fusion
  44.3 1.4 %gather_fusion.2 = bf16[32,16,512]{2,1,0:T(8,128)(2,1)} fusion(bf16[16,16,512]{2,1,0:T(8,128)(2,1)S(1)} %constant_dynamic-slice_fusion, s32[1024]{0:T(1024)S(1)} %pad_clamp_fusion.1), kind=kCustom, calls=%fused_computation.4 | custom fusion | bytes 1048704 | tf_op jit(solution)/shard_map/gather | solution.py:209
  45.7 8.1 %all-to-all-start.1 = ((bf16[32,16,512]{2,1,0:T(8,128)(2,1)}), bf16[32,16,512]{2,1,0:T(8,128)(2,1)S(1)}, u32[]{:S(2)}, u32[]{:S(2)}) async-start(bf16[32,16,512]{2,1,0:T(8,128)(2,1)} %gather_fusion.2), calls=%async_computation.1 | async-start | bytes 1048576 | tf_op jit(solution)/shard_map/all_to_all | solution.py:210
  53.9 0.7 gather_fusion.5
  54.6 0.7 gather_fusion.4
  55.3 0.6 compare_select_fusion.1
  55.9 14.5 %all-to-all-done.1 = bf16[32,16,512]{2,1,0:T(8,128)(2,1)S(1)} async-done(((bf16[32,16,512]{2,1,0:T(8,128)(2,1)}), bf16[32,16,512]{2,1,0:T(8,128)(2,1)S(1)}, u32[]{:S(2)}, u32[]{:S(2)}) %all-to-all-start.1) | async-done | bytes 524320 | tf_op jit(solution)/shard_map/all_to_all | solution.py:210
  70.4 1.3 %gather_fusion.3 = bf16[16,16,512]{2,1,0:T(8,128)(2,1)} fusion(bf16[32,16,512]{2,1,0:T(8,128)(2,1)S(1)} %all-to-all-done.1, s32[1024]{0:T(1024)S(1)} %pad_clamp_fusion), kind=kCustom, calls=%fused_computation.5 | custom fusion | bytes 524352 | tf_op jit(solution)/shard_map/gather | solution.py:216
  71.7 0.6 dynamic_slice.25
  74.2 5.1 %shard_map.78.pool_hbm = bf16[32,128,512]{2,1,0:T(8,128)(2,1)} custom-call(bf16[32,128,512]{2,1,0:T(8,128)(2,1)} %src_ref.1), custom_call_target="tpu_custom_call" | custom-call | tf_op jit(solution)/shard_map/pallas_call | solution.py:154
  80.1 1.6 %copy-done.1 = bf16[16,128,512]{2,1,0:T(8,128)(2,1)S(1)} copy-done((bf16[16,128,512]{2,1,0:T(8,128)(2,1)S(1)}, bf16[16,128,512]{2,1,0:T(8,128)(2,1)}, u32[]{:S(2)}) %copy-start.1) | copy-done | bytes 2097176
  81.6 20.4 %shard_map.77 = bf16[256,2560]{1,0:T(8,128)(2,1)} custom-call(s32[2]{0:T(128)S(1)} %pad_add_fusion.meta, bf16[256,2560]{1,0:T(8,128)(2,1)S(1)} %bitcast.53, bf16[2048,512]{1,0:T(8,128)(2,1)S(1)} %bitcast.52, bf16[2048,512]{1,0:T(8,128)(2,1)S(1)} %bitcast.51), custom_call_target="tpu_custom_call" | custom-call | tf_op jit(solution)/shard_map/pallas_call | solution.py:85
  102.1 3.2 %shard_map.79 = bf16[32,128,512]{2,1,0:T(8,128)(2,1)} custom-call(s32[16]{0:T(128)} %get-tuple-element.11.targets, bf16[16,128,512]{2,1,0:T(8,128)(2,1)} %all-gather.10.cloned.1.call-done.landed_hbm, bf16[32,128,512]{2,1,0:T(8,128)(2,1)} %shard_map.78.pool_hbm), custom_call_target="tpu_custom_call", output_to_operand_aliasing={{}: (2, {})} | custom-call | tf_op jit(solution)/shard_map/pallas_call | solution.py:129
  (34 shorter events, 0.8 us)
Async XLA Ops:
  7.2 36.2 %all-gather.6.cloned.1.call-start = ((), (), s32[]{:S(2)}) async-start(), calls=%async_computation.2 | async-start | bytes 2359296 | tf_op jit(solution)/shard_map/all_gather | solution.py:181
  12.8 28.3 %all-to-all-start = ((bf16[32,16,512]{2,1,0:T(8,128)(2,1)}), bf16[32,16,512]{2,1,0:T(8,128)(2,1)S(1)}, u32[]{:S(2)}, u32[]{:S(2)}) async-start(bf16[32,16,512]{2,1,0:T(8,128)(2,1)} %gather_fusion), calls=%async_computation | async-start | bytes 1048576 | tf_op jit(solution)/shard_map/all_to_all | solution.py:194
  24.8 29.7 %copy-start.3 = (s32[32,16]{0,1:T(8,128)S(1)}, s32[32,16]{0,1:T(8,128)}, u32[]{:S(2)}) copy-start(s32[32,16]{0,1:T(8,128)} %param.12) | copy-start | bytes 6148
  24.8 55.2 %all-gather.8.cloned.1.call-start = ((), (), s32[]{:S(2)}) async-start(), calls=%async_computation.3 | async-start | bytes 2359296 | tf_op jit(solution)/shard_map/all_gather | solution.py:197
  44.3 27.4 %copy-start.4 = (s32[32]{0:T(128)S(1)}, s32[32]{0:T(128)}, u32[]{:S(2)}) copy-start(s32[32]{0:T(128)} %param.13) | copy-start | bytes 388
  45.7 24.7 %all-to-all-start.1 = ((bf16[32,16,512]{2,1,0:T(8,128)(2,1)}), bf16[32,16,512]{2,1,0:T(8,128)(2,1)S(1)}, u32[]{:S(2)}, u32[]{:S(2)}) async-start(bf16[32,16,512]{2,1,0:T(8,128)(2,1)} %gather_fusion.2), calls=%async_computation.1 | async-start | bytes 1048576 | tf_op jit(solution)/shard_map/all_to_all | solution.py:210
  53.8 48.3 %all-gather.10.cloned.1.call-start = ((), (), s32[]{:S(2)}) async-start(), calls=%async_computation.4 | async-start | bytes 2359296 | tf_op jit(solution)/shard_map/all_gather | solution.py:216
  74.2 5.8 %copy-start = (bf16[1,2048,512]{2,1,0:T(8,128)(2,1)S(1)}, bf16[1,2048,512]{2,1,0:T(8,128)(2,1)}, u32[]{:S(2)}) copy-start(bf16[1,2048,512]{2,1,0:T(8,128)(2,1)} %all-gather.6.cloned.1.call-done) | copy-start | bytes 6291460
  74.2 5.8 %copy-start.2 = (bf16[1,256,2560]{2,1,0:T(8,128)(2,1)S(1)}, bf16[1,256,2560]{2,1,0:T(8,128)(2,1)}, u32[]{:S(2)}) copy-start(bf16[1,256,2560]{2,1,0:T(8,128)(2,1)} %param.8) | copy-start | bytes 3932164
  80.1 1.6 %copy-start.1 = (bf16[16,128,512]{2,1,0:T(8,128)(2,1)S(1)}, bf16[16,128,512]{2,1,0:T(8,128)(2,1)}, u32[]{:S(2)}) copy-start(bf16[16,128,512]{2,1,0:T(8,128)(2,1)} %all-gather.8.cloned.1.call-done) | copy-start | bytes 6291460
Sparse Core Ops, SparseCore 0:
  9.8 31.9 all-gather.5
  43.7 28.2 all-gather.7
  73.9 28.1 all-gather.9

commit v11 on v10

--- a/solution.py
+++ b/solution.py
@@ -5,7 +5,7 @@
 from jax import lax
 from jax.experimental import pallas as pl
 from jax.experimental.pallas import tpu as pltpu
-from jax.sharding import PartitionSpec as P
+from jax.sharding import Mesh, PartitionSpec as P
 
 
 def earlier_same(owners):
@@ -162,9 +162,9 @@
 
 def shards_body(queries, new_kv, kv_pool, window_table, append_table, cache_lengths):
     blocks = lax.axis_size("blk")
-    groups = lax.axis_size("group")
+    groups = lax.axis_size("gx") * lax.axis_size("gc")
     my_block = lax.axis_index("blk")
-    piece_index = lax.axis_index("group")
+    piece_index = lax.axis_index("gx") * lax.axis_size("gc") + lax.axis_index("gc")
     tok_rows = queries.shape[1]
     per_owner = kv_pool.shape[0]
     page_rows = kv_pool.shape[1]
@@ -178,7 +178,7 @@
     cap_new = (new_pages + blocks - 1) // blocks
     piece_rows = page_rows // groups
     piece_start = piece_index * piece_rows
-    fresh_keys = lax.all_gather(new_kv, "group", axis=1, tiled=True)[0]
+    fresh_keys = lax.all_gather(new_kv, ("gx", "gc"), axis=1, tiled=True)[0]
 
     win_owner = window_table // per_owner
     win_rank = earlier_same(win_owner)
@@ -194,7 +194,7 @@
     received = lax.all_to_all(outgoing, "blk", split_axis=0, concat_axis=0, tiled=True)
     pool_out = copy_pool(kv_pool)
     cached_piece = received[arrival]
-    cached = lax.all_gather(cached_piece, "group", axis=1, tiled=True)
+    cached = lax.all_gather(cached_piece, ("gx", "gc"), axis=1, tiled=True)
 
     new_owner = append_table // per_owner
     new_rank = earlier_same(new_owner)
@@ -213,7 +213,7 @@
     land_slot = land_source * cap_new + jnp.take_along_axis(new_rank, land_source[None, :], axis=0)[0]
     land_ids = jnp.take_along_axis(append_table % per_owner, land_source[None, :], axis=0)[0]
     land_live = jnp.any(land_here, axis=0)
-    landed = lax.all_gather(arrived[land_slot], "group", axis=1, tiled=True)
+    landed = lax.all_gather(arrived[land_slot], ("gx", "gc"), axis=1, tiled=True)
     targets = jnp.where(land_live, land_ids, per_owner)
     new_pool = write_pool(pool_out, landed, targets)
 
@@ -230,13 +230,16 @@
 
 
 def solution(mesh):
+    chip_count = mesh.shape["group"] // 2
+    split = Mesh(mesh.devices.reshape(mesh.shape["blk"], chip_count, 2), ("blk", "gx", "gc"))
+    tokens = ("gx", "gc")
     in_specs = (
-        P("blk", "group", None),
-        P("blk", "group", None),
+        P("blk", tokens, None),
+        P("blk", tokens, None),
         P("blk", None, None),
         P(),
         P(),
         P(),
     )
-    out_specs = (P("blk", "group", None), P("blk", None, None))
-    return jax.shard_map(shards_body, mesh=mesh, in_specs=in_specs, out_specs=out_specs, check_vma=False)
+    out_specs = (P("blk", tokens, None), P("blk", None, None))
+    return jax.shard_map(shards_body, mesh=split, in_specs=in_specs, out_specs=out_specs, check_vma=False)

time: 112 us -> 112 us (level)
  no operation moved by 1% of the time
where the time goes in v11:
time: 112 us
  waiting for transfers between devices  31.3 us (28%)
  Pallas kernels  28.7 us (26%)
  starting transfers between devices  20.2 us (18%)
  between operations  16.5 us (15%)
  local copies, waits for them, and re-layouts  10.9 us (10%)
  other arithmetic  4.25 us (4%)
    pallas_call x1, Pallas kernels, window_attention(): pl.pallas_call(body, out_shape=jax.ShapeDtypeStruct((tok_rows, width), qu...  20.4 us
    all_to_all x1, waiting for transfers between devices, shards_body(): lax.all_to_all(outgoing, 'blk', split_axis=0, concat_axis=0, tiled=True)  16 us
    all_to_all x1, waiting for transfers between devices, shards_body(): lax.all_to_all(parcels, 'blk', split_axis=0, concat_axis=0, tiled=True)  14.5 us
    all_to_all x1, starting transfers between devices, shards_body(): lax.all_to_all(outgoing, 'blk', split_axis=0, concat_axis=0, tiled=True)  12 us
    all_to_all x1, starting transfers between devices, shards_body(): lax.all_to_all(parcels, 'blk', split_axis=0, concat_axis=0, tiled=True)  8.09 us
    pallas_call x1, Pallas kernels, copy_pool(): pl.pallas_call(copy_kernel, out_shape=jax.ShapeDtypeStruct(kv_pool.shape,...  5.06 us
    pallas_call x1, Pallas kernels, write_pool(): pl.pallas_call(pool_kernel, out_shape=jax.ShapeDtypeStruct(kv_pool.shape,...  3.23 us
  transfers between devices with their start and end apart: 5, of which 3 were waited for; matrix products, arithmetic and copies ran while one was open for 12% of the time, Pallas kernels for 23%

profile of v11, /device:TPU:1, one launch (start us, length us, event | category | flops | bytes accessed | tf_op | source)
XLA Modules:
  0.0 111.9 jit_solution(212986322713311020)
XLA Ops:
  7.2 0.7 all-gather.6.cloned.1.call-update
  7.9 0.7 add_select_fusion.3
  8.6 0.8 fusion.12
  9.6 0.7 fusion.1
  10.3 1.1 constant_dynamic-slice_fusion.1
  11.4 1.4 %gather_fusion = bf16[32,16,512]{2,1,0:T(8,128)(2,1)} fusion(bf16[32,16,512]{2,1,0:T(8,128)(2,1)S(1)} %constant_dynamic-slice_fusion.1, s32[1024]{0:T(1024)S(1)} %pad_clamp_fusion.3), kind=kCustom, calls=%fused_computation.2 | custom fusion | bytes 1048704 | tf_op jit(solution)/shard_map/gather | solution.py:193
  12.8 12.0 %all-to-all-start = ((bf16[32,16,512]{2,1,0:T(8,128)(2,1)}), bf16[32,16,512]{2,1,0:T(8,128)(2,1)S(1)}, u32[]{:S(2)}, u32[]{:S(2)}) async-start(bf16[32,16,512]{2,1,0:T(8,128)(2,1)} %gather_fusion), calls=%async_computation | async-start | bytes 1048576 | tf_op jit(solution)/shard_map/all_to_all | solution.py:194
  24.9 0.2 dynamic-slice_reduce_fusion
  25.1 16.0 %all-to-all-done = bf16[32,16,512]{2,1,0:T(8,128)(2,1)S(1)} async-done(((bf16[32,16,512]{2,1,0:T(8,128)(2,1)}), bf16[32,16,512]{2,1,0:T(8,128)(2,1)S(1)}, u32[]{:S(2)}, u32[]{:S(2)}) %all-to-all-start) | async-done | bytes 524320 | tf_op jit(solution)/shard_map/all_to_all | solution.py:194
  41.1 1.3 %gather_fusion.1 = bf16[16,16,512]{2,1,0:T(8,128)(2,1)} fusion(bf16[32,16,512]{2,1,0:T(8,128)(2,1)S(1)} %all-to-all-done, s32[1024]{0:T(1024)S(1)} %pad_clamp_fusion.2), kind=kCustom, calls=%fused_computation.3 | custom fusion | bytes 524352 | tf_op jit(solution)/shard_map/gather | solution.py:196
  42.7 0.6 iota_reduce_fusion
  43.4 1.0 constant_dynamic-slice_fusion
  44.3 1.4 %gather_fusion.2 = bf16[32,16,512]{2,1,0:T(8,128)(2,1)} fusion(bf16[16,16,512]{2,1,0:T(8,128)(2,1)S(1)} %constant_dynamic-slice_fusion, s32[1024]{0:T(1024)S(1)} %pad_clamp_fusion.1), kind=kCustom, calls=%fused_computation.4 | custom fusion | bytes 1048704 | tf_op jit(solution)/shard_map/gather | solution.py:209
  45.7 8.1 %all-to-all-start.1 = ((bf16[32,16,512]{2,1,0:T(8,128)(2,1)}), bf16[32,16,512]{2,1,0:T(8,128)(2,1)S(1)}, u32[]{:S(2)}, u32[]{:S(2)}) async-start(bf16[32,16,512]{2,1,0:T(8,128)(2,1)} %gather_fusion.2), calls=%async_computation.1 | async-start | bytes 1048576 | tf_op jit(solution)/shard_map/all_to_all | solution.py:210
  53.9 0.7 gather_fusion.5
  54.6 0.7 gather_fusion.4
  55.3 0.6 compare_select_fusion.1
  55.9 14.5 %all-to-all-done.1 = bf16[32,16,512]{2,1,0:T(8,128)(2,1)S(1)} async-done(((bf16[32,16,512]{2,1,0:T(8,128)(2,1)}), bf16[32,16,512]{2,1,0:T(8,128)(2,1)S(1)}, u32[]{:S(2)}, u32[]{:S(2)}) %all-to-all-start.1) | async-done | bytes 524320 | tf_op jit(solution)/shard_map/all_to_all | solution.py:210
  70.4 1.3 %gather_fusion.3 = bf16[16,16,512]{2,1,0:T(8,128)(2,1)} fusion(bf16[32,16,512]{2,1,0:T(8,128)(2,1)S(1)} %all-to-all-done.1, s32[1024]{0:T(1024)S(1)} %pad_clamp_fusion), kind=kCustom, calls=%fused_computation.5 | custom fusion | bytes 524352 | tf_op jit(solution)/shard_map/gather | solution.py:216
  71.7 0.6 dynamic_slice.25
  74.2 5.1 %shard_map.78.pool_hbm = bf16[32,128,512]{2,1,0:T(8,128)(2,1)} custom-call(bf16[32,128,512]{2,1,0:T(8,128)(2,1)} %src_ref.1), custom_call_target="tpu_custom_call" | custom-call | tf_op jit(solution)/shard_map/pallas_call | solution.py:154
  80.1 1.6 %copy-done.1 = bf16[16,128,512]{2,1,0:T(8,128)(2,1)S(1)} copy-done((bf16[16,128,512]{2,1,0:T(8,128)(2,1)S(1)}, bf16[16,128,512]{2,1,0:T(8,128)(2,1)}, u32[]{:S(2)}) %copy-start.1) | copy-done | bytes 2097176
  81.6 20.4 %shard_map.77 = bf16[256,2560]{1,0:T(8,128)(2,1)} custom-call(s32[2]{0:T(128)S(1)} %pad_add_fusion.meta, bf16[256,2560]{1,0:T(8,128)(2,1)S(1)} %bitcast.53, bf16[2048,512]{1,0:T(8,128)(2,1)S(1)} %bitcast.52, bf16[2048,512]{1,0:T(8,128)(2,1)S(1)} %bitcast.51), custom_call_target="tpu_custom_call" | custom-call | tf_op jit(solution)/shard_map/pallas_call | solution.py:85
  102.1 3.2 %shard_map.79 = bf16[32,128,512]{2,1,0:T(8,128)(2,1)} custom-call(s32[16]{0:T(128)} %get-tuple-element.11.targets, bf16[16,128,512]{2,1,0:T(8,128)(2,1)} %all-gather.10.cloned.1.call-done.landed_hbm, bf16[32,128,512]{2,1,0:T(8,128)(2,1)} %shard_map.78.pool_hbm), custom_call_target="tpu_custom_call", output_to_operand_aliasing={{}: (2, {})} | custom-call | tf_op jit(solution)/shard_map/pallas_call | solution.py:129
  (34 shorter events, 0.8 us)
Async XLA Ops:
  7.2 36.2 %all-gather.6.cloned.1.call-start = ((), (), s32[]{:S(2)}) async-start(), calls=%async_computation.2 | async-start | bytes 2359296 | tf_op jit(solution)/shard_map/all_gather | solution.py:181
  12.8 28.3 %all-to-all-start = ((bf16[32,16,512]{2,1,0:T(8,128)(2,1)}), bf16[32,16,512]{2,1,0:T(8,128)(2,1)S(1)}, u32[]{:S(2)}, u32[]{:S(2)}) async-start(bf16[32,16,512]{2,1,0:T(8,128)(2,1)} %gather_fusion), calls=%async_computation | async-start | bytes 1048576 | tf_op jit(solution)/shard_map/all_to_all | solution.py:194
  24.8 29.7 %copy-start.3 = (s32[32,16]{0,1:T(8,128)S(1)}, s32[32,16]{0,1:T(8,128)}, u32[]{:S(2)}) copy-start(s32[32,16]{0,1:T(8,128)} %param.12) | copy-start | bytes 6148
  24.8 55.2 %all-gather.8.cloned.1.call-start = ((), (), s32[]{:S(2)}) async-start(), calls=%async_computation.3 | async-start | bytes 2359296 | tf_op jit(solution)/shard_map/all_gather | solution.py:197
  44.3 27.4 %copy-start.4 = (s32[32]{0:T(128)S(1)}, s32[32]{0:T(128)}, u32[]{:S(2)}) copy-start(s32[32]{0:T(128)} %param.13) | copy-start | bytes 388
  45.7 24.7 %all-to-all-start.1 = ((bf16[32,16,512]{2,1,0:T(8,128)(2,1)}), bf16[32,16,512]{2,1,0:T(8,128)(2,1)S(1)}, u32[]{:S(2)}, u32[]{:S(2)}) async-start(bf16[32,16,512]{2,1,0:T(8,128)(2,1)} %gather_fusion.2), calls=%async_computation.1 | async-start | bytes 1048576 | tf_op jit(solution)/shard_map/all_to_all | solution.py:210
  53.8 48.3 %all-gather.10.cloned.1.call-start = ((), (), s32[]{:S(2)}) async-start(), calls=%async_computation.4 | async-start | bytes 2359296 | tf_op jit(solution)/shard_map/all_gather | solution.py:216
  74.2 5.8 %copy-start = (bf16[1,2048,512]{2,1,0:T(8,128)(2,1)S(1)}, bf16[1,2048,512]{2,1,0:T(8,128)(2,1)}, u32[]{:S(2)}) copy-start(bf16[1,2048,512]{2,1,0:T(8,128)(2,1)} %all-gather.6.cloned.1.call-done) | copy-start | bytes 6291460
  74.2 5.8 %copy-start.2 = (bf16[1,256,2560]{2,1,0:T(8,128)(2,1)S(1)}, bf16[1,256,2560]{2,1,0:T(8,128)(2,1)}, u32[]{:S(2)}) copy-start(bf16[1,256,2560]{2,1,0:T(8,128)(2,1)} %param.8) | copy-start | bytes 3932164
  80.1 1.6 %copy-start.1 = (bf16[16,128,512]{2,1,0:T(8,128)(2,1)S(1)}, bf16[16,128,512]{2,1,0:T(8,128)(2,1)}, u32[]{:S(2)}) copy-start(bf16[16,128,512]{2,1,0:T(8,128)(2,1)} %all-gather.8.cloned.1.call-done) | copy-start | bytes 6291460
Sparse Core Ops, SparseCore 0:
  9.8 31.9 all-gather.5
  43.7 28.2 all-gather.7
  73.9 28.1 all-gather.9

commit v12 on v10

--- a/solution.py
+++ b/solution.py
@@ -144,6 +144,29 @@
     )(targets.astype(jnp.int32), landed, kv_pool)
 
 
+def pick_kernel(slots, src_hbm, out_ref, sems):
+    for row in range(out_ref.shape[0]):
+        pltpu.make_async_copy(src_hbm.at[slots[row]], out_ref.at[row], sems.at[row]).start()
+    for row in range(out_ref.shape[0]):
+        pltpu.make_async_copy(src_hbm.at[slots[row]], out_ref.at[row], sems.at[row]).wait()
+
+
+def pick_slots(slots_array, slots):
+    count = slots.shape[0]
+    shape = (count,) + slots_array.shape[1:]
+    return pl.pallas_call(
+        pick_kernel,
+        out_shape=jax.ShapeDtypeStruct(shape, slots_array.dtype),
+        grid_spec=pltpu.PrefetchScalarGridSpec(
+            num_scalar_prefetch=1,
+            grid=(1,),
+            in_specs=[pl.BlockSpec(memory_space=pl.ANY)],
+            out_specs=pl.BlockSpec(shape, lambda i, s: (0, 0, 0)),
+            scratch_shapes=[pltpu.SemaphoreType.DMA((count,))],
+        ),
+    )(slots.astype(jnp.int32), slots_array)
+
+
 def copy_kernel(src_ref, dst_ref):
     dst_ref[...] = src_ref[...]
 
@@ -193,7 +216,7 @@
     outgoing = pool_piece[send_ids.reshape(-1)]
     received = lax.all_to_all(outgoing, "blk", split_axis=0, concat_axis=0, tiled=True)
     pool_out = copy_pool(kv_pool)
-    cached_piece = received[arrival]
+    cached_piece = pick_slots(received, arrival)
     cached = lax.all_gather(cached_piece, "group", axis=1, tiled=True)
 
     new_owner = append_table // per_owner
@@ -213,7 +236,7 @@
     land_slot = land_source * cap_new + jnp.take_along_axis(new_rank, land_source[None, :], axis=0)[0]
     land_ids = jnp.take_along_axis(append_table % per_owner, land_source[None, :], axis=0)[0]
     land_live = jnp.any(land_here, axis=0)
-    landed = lax.all_gather(arrived[land_slot], "group", axis=1, tiled=True)
+    landed = lax.all_gather(pick_slots(arrived, land_slot), "group", axis=1, tiled=True)
     targets = jnp.where(land_live, land_ids, per_owner)
     new_pool = write_pool(pool_out, landed, targets)
 

time: 112 us -> 115 us (1.027)
  Pallas kernels: 28.7 us -> 33.5 us
  starting transfers between devices: 20.2 us -> 18.7 us
    pallas_call x0 -> x2, Pallas kernels: none -> 4.8 us  [pick_slots(): pl.pallas_call(pick_kernel, out_shape=jax.ShapeDtypeStruct(shape, slots_a...]
    gather x2 -> x0, local copies, waits for them, and re-layouts: 2.53 us -> none  [the longest x1 1.27 us: shards_body(): cached_piece = received[arrival]]
    unnamed x10 -> x14, local copies, waits for them, and re-layouts: 1.61 us -> 3.19 us
    all_to_all x1, starting transfers between devices: 8.09 us -> 6.57 us  [shards_body(): lax.all_to_all(parcels, 'blk', split_axis=0, concat_axis=0, tiled=True)]
    add x0 -> x2, other arithmetic: none -> 1.31 us  [the longest x1 0.7 us: shards_body(): arrival = own_owner * cap_win + own_rank]
  transfers between devices with their start and end apart: 5 -> 5, of which waited for: 3 -> 2; matrix products, arithmetic and copies ran while one was open for 12% -> 10% of each run, Pallas kernels for 23% -> 27%
where the time goes in v12:
time: 115 us; the launch traced here: 114 us
  Pallas kernels  33.5 us (29%)
  waiting for transfers between devices  30.2 us (26%)
  starting transfers between devices  18.7 us (16%)
  between operations  16.5 us (14%)
  local copies, waits for them, and re-layouts  10.1 us (9%)
  other arithmetic  4.75 us (4%)
    pallas_call x1, Pallas kernels, window_attention(): pl.pallas_call(body, out_shape=jax.ShapeDtypeStruct((tok_rows, width), qu...  20.4 us
    all_to_all x1, waiting for transfers between devices, shards_body(): lax.all_to_all(outgoing, 'blk', split_axis=0, concat_axis=0, tiled=True)  15.5 us
    all_to_all x1, waiting for transfers between devices, shards_body(): lax.all_to_all(parcels, 'blk', split_axis=0, concat_axis=0, tiled=True)  13.9 us
    all_to_all x1, starting transfers between devices, shards_body(): lax.all_to_all(outgoing, 'blk', split_axis=0, concat_axis=0, tiled=True)  12 us
    all_to_all x1, starting transfers between devices, shards_body(): lax.all_to_all(parcels, 'blk', split_axis=0, concat_axis=0, tiled=True)  6.57 us
    pallas_call x1, Pallas kernels, copy_pool(): pl.pallas_call(copy_kernel, out_shape=jax.ShapeDtypeStruct(kv_pool.shape,...  5.06 us
    pallas_call x2, Pallas kernels, pick_slots(): pl.pallas_call(pick_kernel, out_shape=jax.ShapeDtypeStruct(shape, slots_a...  4.8 us
    pallas_call x1, Pallas kernels, write_pool(): pl.pallas_call(pool_kernel, out_shape=jax.ShapeDtypeStruct(kv_pool.shape,...  3.24 us
  transfers between devices with their start and end apart: 5, of which 2 were waited for; matrix products, arithmetic and copies ran while one was open for 10% of the time, Pallas kernels for 27%

profile of v12, /device:TPU:1, one launch (start us, length us, event | category | flops | bytes accessed | tf_op | source)
XLA Modules:
  0.0 113.8 jit_solution(15157645612588324875)
XLA Ops:
  7.2 0.7 all-gather.6.cloned.1.call-update
  7.9 0.7 add_select_fusion.3
  8.6 0.8 fusion.11
  9.6 0.7 fusion.1
  10.3 1.1 constant_dynamic-slice_fusion.1
  11.4 1.4 %gather_fusion = bf16[32,16,512]{2,1,0:T(8,128)(2,1)} fusion(bf16[32,16,512]{2,1,0:T(8,128)(2,1)S(1)} %constant_dynamic-slice_fusion.1, s32[1024]{0:T(1024)S(1)} %pad_clamp_fusion.1), kind=kCustom, calls=%fused_computation.2 | custom fusion | bytes 1048704 | tf_op jit(solution)/shard_map/gather | solution.py:216
  12.8 12.0 %all-to-all-start = ((bf16[32,16,512]{2,1,0:T(8,128)(2,1)}), bf16[32,16,512]{2,1,0:T(8,128)(2,1)S(1)}, u32[]{:S(2)}, u32[]{:S(2)}) async-start(bf16[32,16,512]{2,1,0:T(8,128)(2,1)} %gather_fusion), calls=%async_computation | async-start | bytes 1048576 | tf_op jit(solution)/shard_map/all_to_all | solution.py:217
  24.9 0.7 add_reduce_fusion.slots
  25.6 15.5 %all-to-all-done.src_hbm = bf16[32,16,512]{2,1,0:T(8,128)(2,1)S(1)} async-done(((bf16[32,16,512]{2,1,0:T(8,128)(2,1)}), bf16[32,16,512]{2,1,0:T(8,128)(2,1)S(1)}, u32[]{:S(2)}, u32[]{:S(2)}) %all-to-all-start) | async-done | bytes 524320 | tf_op jit(solution)/shard_map/all_to_all | solution.py:217
  41.1 0.8 copy-done.4
  41.9 2.4 %shard_map.77 = bf16[16,16,512]{2,1,0:T(8,128)(2,1)} custom-call(s32[16]{0:T(128)} %add_reduce_fusion.slots, bf16[32,16,512]{2,1,0:T(8,128)(2,1)} %copy-done.4), custom_call_target="tpu_custom_call" | custom-call | tf_op jit(solution)/shard_map/pallas_call | solution.py:157
  44.9 1.0 constant_dynamic-slice_fusion
  45.9 1.4 %gather_fusion.1 = bf16[32,16,512]{2,1,0:T(8,128)(2,1)} fusion(bf16[16,16,512]{2,1,0:T(8,128)(2,1)S(1)} %constant_dynamic-slice_fusion, s32[1024]{0:T(1024)S(1)} %pad_clamp_fusion), kind=kCustom, calls=%fused_computation.3 | custom fusion | bytes 1048704 | tf_op jit(solution)/shard_map/gather | solution.py:232
  47.2 6.6 %all-to-all-start.1 = ((bf16[32,16,512]{2,1,0:T(8,128)(2,1)}), bf16[32,16,512]{2,1,0:T(8,128)(2,1)S(1)}, u32[]{:S(2)}, u32[]{:S(2)}) async-start(bf16[32,16,512]{2,1,0:T(8,128)(2,1)} %gather_fusion.1), calls=%async_computation.1 | async-start | bytes 1048576 | tf_op jit(solution)/shard_map/all_to_all | solution.py:233
  53.9 0.6 iota_reduce_fusion
  54.5 0.7 gather_fusion.3
  55.2 0.7 gather_fusion.2
  56.5 13.9 %all-to-all-done.1.src_hbm = bf16[32,16,512]{2,1,0:T(8,128)(2,1)S(1)} async-done(((bf16[32,16,512]{2,1,0:T(8,128)(2,1)}), bf16[32,16,512]{2,1,0:T(8,128)(2,1)S(1)}, u32[]{:S(2)}, u32[]{:S(2)}) %all-to-all-start.1) | async-done | bytes 524320 | tf_op jit(solution)/shard_map/all_to_all | solution.py:233
  70.4 0.8 copy-done.3
  71.2 2.4 %shard_map.79 = bf16[16,16,512]{2,1,0:T(8,128)(2,1)} custom-call(s32[16]{0:T(128)} %get-tuple-element.10.slots, bf16[32,16,512]{2,1,0:T(8,128)(2,1)} %copy-done.3), custom_call_target="tpu_custom_call" | custom-call | tf_op jit(solution)/shard_map/pallas_call | solution.py:157
  76.2 5.1 %shard_map.80.pool_hbm = bf16[32,128,512]{2,1,0:T(8,128)(2,1)} custom-call(bf16[32,128,512]{2,1,0:T(8,128)(2,1)} %src_ref.1), custom_call_target="tpu_custom_call" | custom-call | tf_op jit(solution)/shard_map/pallas_call | solution.py:177
  82.0 1.6 %copy-done.1 = bf16[16,128,512]{2,1,0:T(8,128)(2,1)S(1)} copy-done((bf16[16,128,512]{2,1,0:T(8,128)(2,1)S(1)}, bf16[16,128,512]{2,1,0:T(8,128)(2,1)}, u32[]{:S(2)}) %copy-start.1) | copy-done | bytes 2097176
  83.6 20.4 %shard_map.78 = bf16[256,2560]{1,0:T(8,128)(2,1)} custom-call(s32[2]{0:T(128)S(1)} %pad_add_fusion.meta, bf16[256,2560]{1,0:T(8,128)(2,1)S(1)} %bitcast.47, bf16[2048,512]{1,0:T(8,128)(2,1)S(1)} %bitcast.46, bf16[2048,512]{1,0:T(8,128)(2,1)S(1)} %bitcast.45), custom_call_target="tpu_custom_call" | custom-call | tf_op jit(solution)/shard_map/pallas_call | solution.py:85
  104.0 3.2 %shard_map.81 = bf16[32,128,512]{2,1,0:T(8,128)(2,1)} custom-call(s32[16]{0:T(128)} %get-tuple-element.11.targets, bf16[16,128,512]{2,1,0:T(8,128)(2,1)} %all-gather.8.cloned.1.call-done.landed_hbm, bf16[32,128,512]{2,1,0:T(8,128)(2,1)} %shard_map.80.pool_hbm), custom_call_target="tpu_custom_call", output_to_operand_aliasing={{}: (2, {})} | custom-call | tf_op jit(solution)/shard_map/pallas_call | solution.py:129
  (36 shorter events, 2.2 us)
Async XLA Ops:
  7.2 37.7 %all-gather.6.cloned.1.call-start = ((), (), s32[]{:S(2)}) async-start(), calls=%async_computation.3 | async-start | bytes 2359296 | tf_op jit(solution)/shard_map/all_gather | solution.py:204
  12.8 28.3 %all-to-all-start = ((bf16[32,16,512]{2,1,0:T(8,128)(2,1)}), bf16[32,16,512]{2,1,0:T(8,128)(2,1)S(1)}, u32[]{:S(2)}, u32[]{:S(2)}) async-start(bf16[32,16,512]{2,1,0:T(8,128)(2,1)} %gather_fusion), calls=%async_computation | async-start | bytes 1048576 | tf_op jit(solution)/shard_map/all_to_all | solution.py:217
  24.8 57.1 %all-gather.4.cloned.1.call-start = ((), (), s32[]{:S(2)}) async-start(), calls=%async_computation.2 | async-start | bytes 2359296 | tf_op jit(solution)/shard_map/all_gather | solution.py:220
  25.6 29.6 %copy-start.5 = (s32[32,16]{0,1:T(8,128)S(1)}, s32[32,16]{0,1:T(8,128)}, u32[]{:S(2)}) copy-start(s32[32,16]{0,1:T(8,128)} %param.12) | copy-start | bytes 6148
  41.1 0.8 copy-start.4
  45.8 27.8 %copy-start.6 = (s32[32]{0:T(128)S(1)}, s32[32]{0:T(128)}, u32[]{:S(2)}) copy-start(s32[32]{0:T(128)} %param.13) | copy-start | bytes 388
  47.2 23.1 %all-to-all-start.1 = ((bf16[32,16,512]{2,1,0:T(8,128)(2,1)}), bf16[32,16,512]{2,1,0:T(8,128)(2,1)S(1)}, u32[]{:S(2)}, u32[]{:S(2)}) async-start(bf16[32,16,512]{2,1,0:T(8,128)(2,1)} %gather_fusion.1), calls=%async_computation.1 | async-start | bytes 1048576 | tf_op jit(solution)/shard_map/all_to_all | solution.py:233
  53.8 50.2 %all-gather.8.cloned.1.call-start = ((), (), s32[]{:S(2)}) async-start(), calls=%async_computation.4 | async-start | bytes 2359296 | tf_op jit(solution)/shard_map/all_gather | solution.py:239
  70.4 0.8 copy-start.3
  76.1 5.8 %copy-start = (bf16[1,2048,512]{2,1,0:T(8,128)(2,1)S(1)}, bf16[1,2048,512]{2,1,0:T(8,128)(2,1)}, u32[]{:S(2)}) copy-start(bf16[1,2048,512]{2,1,0:T(8,128)(2,1)} %all-gather.6.cloned.1.call-done) | copy-start | bytes 6291460
  76.2 5.8 %copy-start.2 = (bf16[1,256,2560]{2,1,0:T(8,128)(2,1)S(1)}, bf16[1,256,2560]{2,1,0:T(8,128)(2,1)}, u32[]{:S(2)}) copy-start(bf16[1,256,2560]{2,1,0:T(8,128)(2,1)} %param.8) | copy-start | bytes 3932164
  82.0 1.6 %copy-start.1 = (bf16[16,128,512]{2,1,0:T(8,128)(2,1)S(1)}, bf16[16,128,512]{2,1,0:T(8,128)(2,1)}, u32[]{:S(2)}) copy-start(bf16[16,128,512]{2,1,0:T(8,128)(2,1)} %all-gather.4.cloned.1.call-done) | copy-start | bytes 6291460
Sparse Core Ops, SparseCore 0:
  9.8 31.9 all-gather.5
  44.5 27.4 all-gather.3
  73.8 28.1 all-gather.7

commit v13 on v7

--- a/solution.py
+++ b/solution.py
@@ -222,9 +222,13 @@
     land_slot = land_source * cap_new + jnp.take_along_axis(new_rank, land_source[None, :], axis=0)[0]
     land_ids = jnp.take_along_axis(append_table % per_owner, land_source[None, :], axis=0)[0]
     land_live = jnp.any(land_here, axis=0)
-    landed = lax.all_gather(arrived[land_slot], "group", axis=0, tiled=False)
+    landing = arrived[land_slot]
     targets = jnp.where(land_live, land_ids, per_owner)
-    new_pool = write_pool(pool_out, landed, targets)
+    half = new_pages // 2
+    new_pool = pool_out
+    for lo, hi in ((0, half), (half, new_pages)):
+        landed = lax.all_gather(landing[lo:hi], "group", axis=0, tiled=False)
+        new_pool = write_pool(new_pool, landed, targets[lo:hi])
 
     own_length = lax.dynamic_index_in_dim(cache_lengths, my_block, 0, keepdims=False)
     filled = jnp.minimum(own_length // page_rows, win_pages)

time: 115 us -> 138 us (1.20)
  waiting for transfers between devices: 31.3 us -> 52.6 us
  Pallas kernels: 29.8 us -> 31.9 us
    all_gather x1 -> x2, waiting for transfers between devices: 0.02 us -> 20.2 us  [shards_body(): landed = lax.all_gather(landing[lo:hi], 'group', axis=0, tiled=False)]
    pallas_call x1 -> x2, Pallas kernels: 4.67 us -> 6.79 us  [write_pool(): pl.pallas_call(pool_kernel, out_shape=jax.ShapeDtypeStruct(kv_pool.shape,...]
  transfers between devices with their start and end apart: 5 -> 6, of which waited for: 2 -> 3; matrix products, arithmetic and copies ran while one was open for 14% -> 11% of each run, Pallas kernels for 22% -> 21%
where the time goes in v13:
time: 138 us
  waiting for transfers between devices  52.6 us (38%)
  Pallas kernels  31.9 us (23%)
  starting transfers between devices  20.3 us (15%)
  between operations  16.6 us (12%)
  local copies, waits for them, and re-layouts  12.5 us (9%)
  other arithmetic  3.66 us (3%)
    pallas_call x1, Pallas kernels, window_attention(): pl.pallas_call(body, out_shape=jax.ShapeDtypeStruct((tok_rows, width), qu...  20.4 us
    all_gather x2, waiting for transfers between devices, shards_body(): landed = lax.all_gather(landing[lo:hi], 'group', axis=0, tiled=False)  20.2 us
    all_to_all x1, waiting for transfers between devices, shards_body(): lax.all_to_all(outgoing, 'blk', split_axis=0, concat_axis=0, tiled=True)  16 us
    all_to_all x1, waiting for transfers between devices, shards_body(): lax.all_to_all(parcels, 'blk', split_axis=0, concat_axis=0, tiled=True)  15.1 us
    all_to_all x1, starting transfers between devices, shards_body(): lax.all_to_all(outgoing, 'blk', split_axis=0, concat_axis=0, tiled=True)  12 us
    all_to_all x1, starting transfers between devices, shards_body(): lax.all_to_all(parcels, 'blk', split_axis=0, concat_axis=0, tiled=True)  8.09 us
    pallas_call x2, Pallas kernels, write_pool(): pl.pallas_call(pool_kernel, out_shape=jax.ShapeDtypeStruct(kv_pool.shape,...  6.79 us
    pallas_call x1, Pallas kernels, copy_pool(): pl.pallas_call(copy_kernel, out_shape=jax.ShapeDtypeStruct(kv_pool.shape,...  4.74 us
  transfers between devices with their start and end apart: 6, of which 3 were waited for; matrix products, arithmetic and copies ran while one was open for 11% of the time, Pallas kernels for 21%

profile of v13, /device:TPU:1, one launch (start us, length us, event | category | flops | bytes accessed | tf_op | source)
XLA Modules:
  0.0 137.5 jit_solution(10936950557341100981)
XLA Ops:
  7.2 0.7 all-gather.8.cloned.1.call-update
  7.9 0.7 add_select_fusion.3
  8.6 0.8 fusion.12
  9.6 0.7 fusion.1
  10.3 1.1 constant_dynamic-slice_fusion.1
  11.4 1.4 gather_fusion
  12.8 12.0 %all-to-all-start = ((bf16[32,16,512]{2,1,0:T(8,128)(2,1)}), bf16[32,16,512]{2,1,0:T(8,128)(2,1)S(1)}, u32[]{:S(2)}, u32[]{:S(2)}) async-start(bf16[32,16,512]{2,1,0:T(8,128)(2,1)} %gather_fusion), calls=%async_computation | async-start | bytes 1048576 | tf_op jit(solution)/shard_map/all_to_all | solution.py:203
  25.1 16.0 %all-to-all-done = bf16[32,16,512]{2,1,0:T(8,128)(2,1)S(1)} async-done(((bf16[32,16,512]{2,1,0:T(8,128)(2,1)}), bf16[32,16,512]{2,1,0:T(8,128)(2,1)S(1)}, u32[]{:S(2)}, u32[]{:S(2)}) %all-to-all-start) | async-done | bytes 524320 | tf_op jit(solution)/shard_map/all_to_all | solution.py:203
  41.1 1.3 gather_fusion.1
  42.7 0.6 iota_reduce_fusion
  43.3 1.0 constant_dynamic-slice_fusion
  44.3 1.4 gather_fusion.2
  45.7 8.1 %all-to-all-start.1 = ((bf16[32,16,512]{2,1,0:T(8,128)(2,1)}), bf16[32,16,512]{2,1,0:T(8,128)(2,1)S(1)}, u32[]{:S(2)}, u32[]{:S(2)}) async-start(bf16[32,16,512]{2,1,0:T(8,128)(2,1)} %gather_fusion.2), calls=%async_computation.1 | async-start | bytes 1048576 | tf_op jit(solution)/shard_map/all_to_all | solution.py:219
  53.9 0.7 gather_fusion.5
  54.6 0.7 gather_fusion.4
  55.3 15.1 %all-to-all-done.1 = bf16[32,16,512]{2,1,0:T(8,128)(2,1)S(1)} async-done(((bf16[32,16,512]{2,1,0:T(8,128)(2,1)}), bf16[32,16,512]{2,1,0:T(8,128)(2,1)S(1)}, u32[]{:S(2)}, u32[]{:S(2)}) %all-to-all-start.1) | async-done | bytes 524320 | tf_op jit(solution)/shard_map/all_to_all | solution.py:219
  70.9 0.7 fusion.13
  72.3 4.7 %shard_map.78.pool_hbm = bf16[32,128,512]{2,1,0:T(8,128)(2,1)} custom-call(bf16[32,128,512]{2,1,0:T(8,128)(2,1)} %src_ref.1), custom_call_target="tpu_custom_call" | custom-call | tf_op jit(solution)/shard_map/pallas_call | solution.py:144
  80.3 0.7 fusion.14
  81.0 2.0 %copy.27 = bf16[8,16,16,512]{3,2,0,1:T(8,128)(2,1)S(1)} copy(bf16[8,16,16,512]{3,2,1,0:T(8,128)(2,1)} %bitcast.59) | data formatting | bytes 4194304 | tf_op jit(solution)/shard_map/all_gather | solution.py:206
  83.5 20.4 %shard_map.77 = bf16[256,2560]{1,0:T(8,128)(2,1)} custom-call(s32[2]{0:T(128)S(1)} %pad_add_fusion.meta, bf16[256,2560]{1,0:T(8,128)(2,1)S(1)} %bitcast.58, bf16[2048,512]{1,0:T(8,128)(2,1)S(1)} %bitcast.55, bf16[2048,512]{1,0:T(8,128)(2,1)S(1)} %bitcast.57), custom_call_target="tpu_custom_call" | custom-call | tf_op jit(solution)/shard_map/pallas_call | solution.py:90
  103.9 3.4 %shard_map.79.pool_hbm = bf16[32,128,512]{2,1,0:T(8,128)(2,1)} custom-call(s32[8]{0:T(128)} %get-tuple-element.12.targets, bf16[8,8,16,512]{3,2,1,0:T(8,128)(2,1)} %bitcast.61, bf16[32,128,512]{2,1,0:T(8,128)(2,1)} %shard_map.78.pool_hbm), custom_call_target="tpu_custom_call", output_to_operand_aliasing={{}: (2, {})} | custom-call | tf_op jit(solution)/shard_map/pallas_call | solution.py:155
  107.3 20.2 %all-gather.12.cloned.1.call-done = bf16[64,16,512]{2,1,0:T(8,128)(2,1)} async-done(((bf16[8,16,512]{2,1,0:T(8,128)(2,1)}), bf16[64,16,512]{2,1,0:T(8,128)(2,1)}) %all-gather.12.cloned.1.call-update) | async-done | bytes 1048592 | tf_op jit(solution)/shard_map/all_gather | solution.py:230
  127.6 3.4 %shard_map.80 = bf16[32,128,512]{2,1,0:T(8,128)(2,1)} custom-call(s32[8]{0:T(128)} %get-tuple-element.13.targets, bf16[8,8,16,512]{3,2,1,0:T(8,128)(2,1)} %bitcast.62, bf16[32,128,512]{2,1,0:T(8,128)(2,1)} %shard_map.79.pool_hbm), custom_call_target="tpu_custom_call", output_to_operand_aliasing={{}: (2, {})} | custom-call | tf_op jit(solution)/shard_map/pallas_call | solution.py:155
  (39 shorter events, 3.3 us)
Async XLA Ops:
  7.2 36.2 %all-gather.8.cloned.1.call-start = ((), (), s32[]{:S(2)}) async-start(), calls=%async_computation.2 | async-start | bytes 2359296 | tf_op jit(solution)/shard_map/all_gather | solution.py:190
  12.8 28.3 %all-to-all-start = ((bf16[32,16,512]{2,1,0:T(8,128)(2,1)}), bf16[32,16,512]{2,1,0:T(8,128)(2,1)S(1)}, u32[]{:S(2)}, u32[]{:S(2)}) async-start(bf16[32,16,512]{2,1,0:T(8,128)(2,1)} %gather_fusion), calls=%async_computation | async-start | bytes 1048576 | tf_op jit(solution)/shard_map/all_to_all | solution.py:203
  24.8 29.7 %copy-start.2 = (s32[32,16]{0,1:T(8,128)S(1)}, s32[32,16]{0,1:T(8,128)}, u32[]{:S(2)}) copy-start(s32[32,16]{0,1:T(8,128)} %param.12) | copy-start | bytes 6148
  24.8 56.1 %all-gather.10.cloned.1.call-start = ((), (), s32[]{:S(2)}) async-start(), calls=%async_computation.3 | async-start | bytes 2359296 | tf_op jit(solution)/shard_map/all_gather | solution.py:206
  45.7 24.7 %all-to-all-start.1 = ((bf16[32,16,512]{2,1,0:T(8,128)(2,1)}), bf16[32,16,512]{2,1,0:T(8,128)(2,1)S(1)}, u32[]{:S(2)}, u32[]{:S(2)}) async-start(bf16[32,16,512]{2,1,0:T(8,128)(2,1)} %gather_fusion.2), calls=%async_computation.1 | async-start | bytes 1048576 | tf_op jit(solution)/shard_map/all_to_all | solution.py:219
  53.8 50.1 %all-gather.14.cloned.1.call-start = ((), (), s32[]{:S(2)}) async-start(), calls=%async_computation.5 | async-start | bytes 1179648 | tf_op jit(solution)/shard_map/all_gather | solution.py:230
  71.7 55.9 %all-gather.12.cloned.1.call-start = ((), (), s32[]{:S(2)}) async-start(), calls=%async_computation.4 | async-start | bytes 1179648 | tf_op jit(solution)/shard_map/all_gather | solution.py:230
  72.3 4.8 %copy-start.3 = (s32[32]{0:T(128)S(1)}, s32[32]{0:T(128)}, u32[]{:S(2)}) copy-start(s32[32]{0:T(128)} %param.13) | copy-start | bytes 388
  80.9 2.2 %copy-start = (bf16[1,2048,512]{2,1,0:T(8,128)(2,1)S(1)}, bf16[1,2048,512]{2,1,0:T(8,128)(2,1)}, u32[]{:S(2)}) copy-start(bf16[1,2048,512]{2,1,0:T(8,128)(2,1)} %all-gather.8.cloned.1.call-done) | copy-start | bytes 6291460
  80.9 2.6 %copy-start.1 = (bf16[1,256,2560]{2,1,0:T(8,128)(2,1)S(1)}, bf16[1,256,2560]{2,1,0:T(8,128)(2,1)}, u32[]{:S(2)}) copy-start(bf16[1,256,2560]{2,1,0:T(8,128)(2,1)} %param.8) | copy-start | bytes 3932164
Sparse Core Ops, SparseCore 0:
  9.8 31.9 all-gather.7
  43.7 28.2 all-gather.9
  73.9 26.1 all-gather.13
  101.9 25.6 all-gather.11

commit v14 on v10

--- a/solution.py
+++ b/solution.py
@@ -17,6 +17,11 @@
 
 def pick_rows(wanted, values):
     return jnp.sum(jnp.where(wanted, values[:, None, :], 0), axis=2)
+
+
+def regroup(pieces):
+    groups, pages, piece_rows, width = pieces.shape
+    return pieces.transpose(1, 0, 2, 3).reshape(pages, groups * piece_rows, width)
 
 
 def window_kernel(meta, q_ref, cached_hbm, fresh_hbm, out_ref, keys, bias, sems, *, chunk, chunks,
@@ -194,7 +199,7 @@
     received = lax.all_to_all(outgoing, "blk", split_axis=0, concat_axis=0, tiled=True)
     pool_out = copy_pool(kv_pool)
     cached_piece = received[arrival]
-    cached = lax.all_gather(cached_piece, "group", axis=1, tiled=True)
+    cached = regroup(lax.all_gather(cached_piece, "group", axis=0, tiled=False))
 
     new_owner = append_table // per_owner
     new_rank = earlier_same(new_owner)

time: 112 us -> 113 us (level)
    all_gather x0 -> x1, local copies, waits for them, and re-layouts: none -> 1.97 us  [shards_body(): cached = regroup(lax.all_gather(cached_piece, 'group', axis=0, tiled=False))]
  transfers between devices with their start and end apart: 5 -> 5, of which waited for: 3 -> 2; matrix products, arithmetic and copies ran while one was open for 12% -> 14% of each run, Pallas kernels for 23% -> 22%
where the time goes in v14:
time: 113 us; the launch traced here: 112 us
  waiting for transfers between devices  31.3 us (28%)
  Pallas kernels  28.4 us (25%)
  starting transfers between devices  20.2 us (18%)
  between operations  16.5 us (15%)
  local copies, waits for them, and re-layouts  11.8 us (10%)
  other arithmetic  4.25 us (4%)
    pallas_call x1, Pallas kernels, window_attention(): pl.pallas_call(body, out_shape=jax.ShapeDtypeStruct((tok_rows, width), qu...  20.4 us
    all_to_all x1, waiting for transfers between devices, shards_body(): lax.all_to_all(outgoing, 'blk', split_axis=0, concat_axis=0, tiled=True)  16 us
    all_to_all x1, waiting for transfers between devices, shards_body(): lax.all_to_all(parcels, 'blk', split_axis=0, concat_axis=0, tiled=True)  14.5 us
    all_to_all x1, starting transfers between devices, shards_body(): lax.all_to_all(outgoing, 'blk', split_axis=0, concat_axis=0, tiled=True)  12 us
    all_to_all x1, starting transfers between devices, shards_body(): lax.all_to_all(parcels, 'blk', split_axis=0, concat_axis=0, tiled=True)  8.09 us
    pallas_call x1, Pallas kernels, copy_pool(): pl.pallas_call(copy_kernel, out_shape=jax.ShapeDtypeStruct(kv_pool.shape,...  4.74 us
    pallas_call x1, Pallas kernels, write_pool(): pl.pallas_call(pool_kernel, out_shape=jax.ShapeDtypeStruct(kv_pool.shape,...  3.24 us
  transfers between devices with their start and end apart: 5, of which 2 were waited for; matrix products, arithmetic and copies ran while one was open for 14% of the time, Pallas kernels for 22%

profile of v14, /device:TPU:1, one launch (start us, length us, event | category | flops | bytes accessed | tf_op | source)
XLA Modules:
  0.0 112.5 jit_solution(7384053465980379504)
XLA Ops:
  7.2 0.7 all-gather.6.cloned.1.call-update
  7.9 0.7 add_select_fusion.3
  8.6 0.8 fusion.12
  9.6 0.7 fusion.1
  10.3 1.1 constant_dynamic-slice_fusion.1
  11.4 1.4 %gather_fusion = bf16[32,16,512]{2,1,0:T(8,128)(2,1)} fusion(bf16[32,16,512]{2,1,0:T(8,128)(2,1)S(1)} %constant_dynamic-slice_fusion.1, s32[1024]{0:T(1024)S(1)} %pad_clamp_fusion.3), kind=kCustom, calls=%fused_computation.2 | custom fusion | bytes 1048704 | tf_op jit(solution)/shard_map/gather | solution.py:198
  12.8 12.0 %all-to-all-start = ((bf16[32,16,512]{2,1,0:T(8,128)(2,1)}), bf16[32,16,512]{2,1,0:T(8,128)(2,1)S(1)}, u32[]{:S(2)}, u32[]{:S(2)}) async-start(bf16[32,16,512]{2,1,0:T(8,128)(2,1)} %gather_fusion), calls=%async_computation | async-start | bytes 1048576 | tf_op jit(solution)/shard_map/all_to_all | solution.py:199
  25.1 16.0 %all-to-all-done = bf16[32,16,512]{2,1,0:T(8,128)(2,1)S(1)} async-done(((bf16[32,16,512]{2,1,0:T(8,128)(2,1)}), bf16[32,16,512]{2,1,0:T(8,128)(2,1)S(1)}, u32[]{:S(2)}, u32[]{:S(2)}) %all-to-all-start) | async-done | bytes 524320 | tf_op jit(solution)/shard_map/all_to_all | solution.py:199
  41.1 1.3 %gather_fusion.1 = bf16[16,16,512]{2,1,0:T(8,128)(2,1)} fusion(bf16[32,16,512]{2,1,0:T(8,128)(2,1)S(1)} %all-to-all-done, s32[1024]{0:T(1024)S(1)} %pad_clamp_fusion.2), kind=kCustom, calls=%fused_computation.3 | custom fusion | bytes 524352 | tf_op jit(solution)/shard_map/gather | solution.py:201
  42.7 0.6 iota_reduce_fusion
  43.3 1.0 constant_dynamic-slice_fusion
  44.3 1.4 %gather_fusion.2 = bf16[32,16,512]{2,1,0:T(8,128)(2,1)} fusion(bf16[16,16,512]{2,1,0:T(8,128)(2,1)S(1)} %constant_dynamic-slice_fusion, s32[1024]{0:T(1024)S(1)} %pad_clamp_fusion.1), kind=kCustom, calls=%fused_computation.4 | custom fusion | bytes 1048704 | tf_op jit(solution)/shard_map/gather | solution.py:214
  45.7 8.1 %all-to-all-start.1 = ((bf16[32,16,512]{2,1,0:T(8,128)(2,1)}), bf16[32,16,512]{2,1,0:T(8,128)(2,1)S(1)}, u32[]{:S(2)}, u32[]{:S(2)}) async-start(bf16[32,16,512]{2,1,0:T(8,128)(2,1)} %gather_fusion.2), calls=%async_computation.1 | async-start | bytes 1048576 | tf_op jit(solution)/shard_map/all_to_all | solution.py:215
  53.9 0.7 gather_fusion.5
  54.6 0.7 gather_fusion.4
  55.3 0.6 compare_select_fusion.1
  55.9 14.5 %all-to-all-done.1 = bf16[32,16,512]{2,1,0:T(8,128)(2,1)S(1)} async-done(((bf16[32,16,512]{2,1,0:T(8,128)(2,1)}), bf16[32,16,512]{2,1,0:T(8,128)(2,1)S(1)}, u32[]{:S(2)}, u32[]{:S(2)}) %all-to-all-start.1) | async-done | bytes 524320 | tf_op jit(solution)/shard_map/all_to_all | solution.py:215
  70.4 1.3 %gather_fusion.3 = bf16[16,16,512]{2,1,0:T(8,128)(2,1)} fusion(bf16[32,16,512]{2,1,0:T(8,128)(2,1)S(1)} %all-to-all-done.1, s32[1024]{0:T(1024)S(1)} %pad_clamp_fusion), kind=kCustom, calls=%fused_computation.5 | custom fusion | bytes 524352 | tf_op jit(solution)/shard_map/gather | solution.py:221
  71.7 0.6 dynamic_slice.25
  74.2 4.7 %shard_map.78.pool_hbm = bf16[32,128,512]{2,1,0:T(8,128)(2,1)} custom-call(bf16[32,128,512]{2,1,0:T(8,128)(2,1)} %src_ref.1), custom_call_target="tpu_custom_call" | custom-call | tf_op jit(solution)/shard_map/pallas_call | solution.py:159
  79.7 2.0 %copy.26 = bf16[8,16,16,512]{3,2,0,1:T(8,128)(2,1)S(1)} copy(bf16[8,16,16,512]{3,2,1,0:T(8,128)(2,1)} %bitcast.57) | data formatting | bytes 4194304 | tf_op jit(solution)/shard_map/all_gather | solution.py:202
  81.9 0.4 copy-done.1
  82.3 20.4 %shard_map.77 = bf16[256,2560]{1,0:T(8,128)(2,1)} custom-call(s32[2]{0:T(128)S(1)} %pad_add_fusion.meta, bf16[256,2560]{1,0:T(8,128)(2,1)S(1)} %bitcast.56, bf16[2048,512]{1,0:T(8,128)(2,1)S(1)} %bitcast.53, bf16[2048,512]{1,0:T(8,128)(2,1)S(1)} %bitcast.55), custom_call_target="tpu_custom_call" | custom-call | tf_op jit(solution)/shard_map/pallas_call | solution.py:90
  102.7 3.2 %shard_map.79 = bf16[32,128,512]{2,1,0:T(8,128)(2,1)} custom-call(s32[16]{0:T(128)} %get-tuple-element.11.targets, bf16[16,128,512]{2,1,0:T(8,128)(2,1)} %all-gather.10.cloned.1.call-done.landed_hbm, bf16[32,128,512]{2,1,0:T(8,128)(2,1)} %shard_map.78.pool_hbm), custom_call_target="tpu_custom_call", output_to_operand_aliasing={{}: (2, {})} | custom-call | tf_op jit(solution)/shard_map/pallas_call | solution.py:134
  (33 shorter events, 1.2 us)
Async XLA Ops:
  7.2 36.2 %all-gather.6.cloned.1.call-start = ((), (), s32[]{:S(2)}) async-start(), calls=%async_computation.2 | async-start | bytes 2359296 | tf_op jit(solution)/shard_map/all_gather | solution.py:186
  12.8 28.3 %all-to-all-start = ((bf16[32,16,512]{2,1,0:T(8,128)(2,1)}), bf16[32,16,512]{2,1,0:T(8,128)(2,1)S(1)}, u32[]{:S(2)}, u32[]{:S(2)}) async-start(bf16[32,16,512]{2,1,0:T(8,128)(2,1)} %gather_fusion), calls=%async_computation | async-start | bytes 1048576 | tf_op jit(solution)/shard_map/all_to_all | solution.py:199
  24.8 29.7 %copy-start.2 = (s32[32,16]{0,1:T(8,128)S(1)}, s32[32,16]{0,1:T(8,128)}, u32[]{:S(2)}) copy-start(s32[32,16]{0,1:T(8,128)} %param.12) | copy-start | bytes 6148
  24.8 54.9 %all-gather.8.cloned.1.call-start = ((), (), s32[]{:S(2)}) async-start(), calls=%async_computation.3 | async-start | bytes 2359296 | tf_op jit(solution)/shard_map/all_gather | solution.py:202
  44.3 27.4 %copy-start.3 = (s32[32]{0:T(128)S(1)}, s32[32]{0:T(128)}, u32[]{:S(2)}) copy-start(s32[32]{0:T(128)} %param.13) | copy-start | bytes 388
  45.7 24.7 %all-to-all-start.1 = ((bf16[32,16,512]{2,1,0:T(8,128)(2,1)}), bf16[32,16,512]{2,1,0:T(8,128)(2,1)S(1)}, u32[]{:S(2)}, u32[]{:S(2)}) async-start(bf16[32,16,512]{2,1,0:T(8,128)(2,1)} %gather_fusion.2), calls=%async_computation.1 | async-start | bytes 1048576 | tf_op jit(solution)/shard_map/all_to_all | solution.py:215
  53.8 48.9 %all-gather.10.cloned.1.call-start = ((), (), s32[]{:S(2)}) async-start(), calls=%async_computation.4 | async-start | bytes 2359296 | tf_op jit(solution)/shard_map/all_gather | solution.py:221
  79.7 2.2 %copy-start = (bf16[1,2048,512]{2,1,0:T(8,128)(2,1)S(1)}, bf16[1,2048,512]{2,1,0:T(8,128)(2,1)}, u32[]{:S(2)}) copy-start(bf16[1,2048,512]{2,1,0:T(8,128)(2,1)} %all-gather.6.cloned.1.call-done) | copy-start | bytes 6291460
  79.7 2.6 %copy-start.1 = (bf16[1,256,2560]{2,1,0:T(8,128)(2,1)S(1)}, bf16[1,256,2560]{2,1,0:T(8,128)(2,1)}, u32[]{:S(2)}) copy-start(bf16[1,256,2560]{2,1,0:T(8,128)(2,1)} %param.8) | copy-start | bytes 3932164
Sparse Core Ops, SparseCore 0:
  9.8 31.9 all-gather.5
  43.7 28.2 all-gather.7
  73.9 28.2 all-gather.9

commit v15 on v14

--- a/solution.py
+++ b/solution.py
@@ -111,8 +111,10 @@
 
 def pool_kernel(targets, landed_hbm, pool_hbm, out_hbm, staged, in_sems, out_sems):
     pages = landed_hbm.shape[0]
-    for page in range(pages):
-        pltpu.make_async_copy(landed_hbm.at[page], staged.at[page], in_sems.at[page]).start()
+    ahead = min(4, pages)
+
+    def fetch(page):
+        return pltpu.make_async_copy(landed_hbm.at[page], staged.at[page], in_sems.at[page])
 
     def each_target(page, begin):
         target = targets[page]
@@ -122,9 +124,13 @@
             cp = pltpu.make_async_copy(staged.at[page], out_hbm.at[target], out_sems.at[page])
             cp.start() if begin else cp.wait()
 
+    for page in range(ahead):
+        fetch(page).start()
     for page in range(pages):
-        pltpu.make_async_copy(landed_hbm.at[page], staged.at[page], in_sems.at[page]).wait()
+        fetch(page).wait()
         each_target(page, True)
+        if page + ahead < pages:
+            fetch(page + ahead).start()
     for page in range(pages):
         each_target(page, False)
 

time: 113 us -> 116 us (1.027)
  Pallas kernels: 28.4 us -> 31.1 us
    pallas_call x1, Pallas kernels: 3.24 us -> 5.95 us  [write_pool(): pl.pallas_call(pool_kernel, out_shape=jax.ShapeDtypeStruct(kv_pool.shape,...]
  transfers between devices with their start and end apart: 5 -> 5, of which waited for: 2 -> 2; matrix products, arithmetic and copies ran while one was open for 14% -> 13% of each run, Pallas kernels for 22% -> 22%
where the time goes in v15:
time: 116 us; the launch traced here: 115 us
  waiting for transfers between devices  31.3 us (27%)
  Pallas kernels  31.1 us (27%)
  starting transfers between devices  20.2 us (17%)
  between operations  16.5 us (14%)
  local copies, waits for them, and re-layouts  11.8 us (10%)
  other arithmetic  4.25 us (4%)
    pallas_call x1, Pallas kernels, window_attention(): pl.pallas_call(body, out_shape=jax.ShapeDtypeStruct((tok_rows, width), qu...  20.4 us
    all_to_all x1, waiting for transfers between devices, shards_body(): lax.all_to_all(outgoing, 'blk', split_axis=0, concat_axis=0, tiled=True)  16 us
    all_to_all x1, waiting for transfers between devices, shards_body(): lax.all_to_all(parcels, 'blk', split_axis=0, concat_axis=0, tiled=True)  14.5 us
    all_to_all x1, starting transfers between devices, shards_body(): lax.all_to_all(outgoing, 'blk', split_axis=0, concat_axis=0, tiled=True)  12 us
    all_to_all x1, starting transfers between devices, shards_body(): lax.all_to_all(parcels, 'blk', split_axis=0, concat_axis=0, tiled=True)  8.09 us
    pallas_call x1, Pallas kernels, write_pool(): pl.pallas_call(pool_kernel, out_shape=jax.ShapeDtypeStruct(kv_pool.shape,...  5.95 us
    pallas_call x1, Pallas kernels, copy_pool(): pl.pallas_call(copy_kernel, out_shape=jax.ShapeDtypeStruct(kv_pool.shape,...  4.74 us
  transfers between devices with their start and end apart: 5, of which 2 were waited for; matrix products, arithmetic and copies ran while one was open for 13% of the time, Pallas kernels for 22%

profile of v15, /device:TPU:1, one launch (start us, length us, event | category | flops | bytes accessed | tf_op | source)
XLA Modules:
  0.0 115.2 jit_solution(2924835764255402709)
XLA Ops:
  7.2 0.7 all-gather.6.cloned.1.call-update
  7.9 0.7 add_select_fusion.3
  8.6 0.8 fusion.12
  9.6 0.7 fusion.1
  10.3 1.1 constant_dynamic-slice_fusion.1
  11.4 1.4 %gather_fusion = bf16[32,16,512]{2,1,0:T(8,128)(2,1)} fusion(bf16[32,16,512]{2,1,0:T(8,128)(2,1)S(1)} %constant_dynamic-slice_fusion.1, s32[1024]{0:T(1024)S(1)} %pad_clamp_fusion.3), kind=kCustom, calls=%fused_computation.2 | custom fusion | bytes 1048704 | tf_op jit(solution)/shard_map/gather | solution.py:204
  12.8 12.0 %all-to-all-start = ((bf16[32,16,512]{2,1,0:T(8,128)(2,1)}), bf16[32,16,512]{2,1,0:T(8,128)(2,1)S(1)}, u32[]{:S(2)}, u32[]{:S(2)}) async-start(bf16[32,16,512]{2,1,0:T(8,128)(2,1)} %gather_fusion), calls=%async_computation | async-start | bytes 1048576 | tf_op jit(solution)/shard_map/all_to_all | solution.py:205
  25.1 16.0 %all-to-all-done = bf16[32,16,512]{2,1,0:T(8,128)(2,1)S(1)} async-done(((bf16[32,16,512]{2,1,0:T(8,128)(2,1)}), bf16[32,16,512]{2,1,0:T(8,128)(2,1)S(1)}, u32[]{:S(2)}, u32[]{:S(2)}) %all-to-all-start) | async-done | bytes 524320 | tf_op jit(solution)/shard_map/all_to_all | solution.py:205
  41.1 1.3 %gather_fusion.1 = bf16[16,16,512]{2,1,0:T(8,128)(2,1)} fusion(bf16[32,16,512]{2,1,0:T(8,128)(2,1)S(1)} %all-to-all-done, s32[1024]{0:T(1024)S(1)} %pad_clamp_fusion.2), kind=kCustom, calls=%fused_computation.3 | custom fusion | bytes 524352 | tf_op jit(solution)/shard_map/gather | solution.py:207
  42.7 0.6 iota_reduce_fusion
  43.3 1.0 constant_dynamic-slice_fusion
  44.3 1.4 %gather_fusion.2 = bf16[32,16,512]{2,1,0:T(8,128)(2,1)} fusion(bf16[16,16,512]{2,1,0:T(8,128)(2,1)S(1)} %constant_dynamic-slice_fusion, s32[1024]{0:T(1024)S(1)} %pad_clamp_fusion.1), kind=kCustom, calls=%fused_computation.4 | custom fusion | bytes 1048704 | tf_op jit(solution)/shard_map/gather | solution.py:220
  45.7 8.1 %all-to-all-start.1 = ((bf16[32,16,512]{2,1,0:T(8,128)(2,1)}), bf16[32,16,512]{2,1,0:T(8,128)(2,1)S(1)}, u32[]{:S(2)}, u32[]{:S(2)}) async-start(bf16[32,16,512]{2,1,0:T(8,128)(2,1)} %gather_fusion.2), calls=%async_computation.1 | async-start | bytes 1048576 | tf_op jit(solution)/shard_map/all_to_all | solution.py:221
  53.9 0.7 gather_fusion.5
  54.6 0.7 gather_fusion.4
  55.3 0.6 compare_select_fusion.1
  55.9 14.5 %all-to-all-done.1 = bf16[32,16,512]{2,1,0:T(8,128)(2,1)S(1)} async-done(((bf16[32,16,512]{2,1,0:T(8,128)(2,1)}), bf16[32,16,512]{2,1,0:T(8,128)(2,1)S(1)}, u32[]{:S(2)}, u32[]{:S(2)}) %all-to-all-start.1) | async-done | bytes 524320 | tf_op jit(solution)/shard_map/all_to_all | solution.py:221
  70.4 1.3 %gather_fusion.3 = bf16[16,16,512]{2,1,0:T(8,128)(2,1)} fusion(bf16[32,16,512]{2,1,0:T(8,128)(2,1)S(1)} %all-to-all-done.1, s32[1024]{0:T(1024)S(1)} %pad_clamp_fusion), kind=kCustom, calls=%fused_computation.5 | custom fusion | bytes 524352 | tf_op jit(solution)/shard_map/gather | solution.py:227
  71.7 0.6 dynamic_slice.25
  74.2 4.7 %shard_map.78.pool_hbm = bf16[32,128,512]{2,1,0:T(8,128)(2,1)} custom-call(bf16[32,128,512]{2,1,0:T(8,128)(2,1)} %src_ref.1), custom_call_target="tpu_custom_call" | custom-call | tf_op jit(solution)/shard_map/pallas_call | solution.py:165
  79.7 2.0 %copy.26 = bf16[8,16,16,512]{3,2,0,1:T(8,128)(2,1)S(1)} copy(bf16[8,16,16,512]{3,2,1,0:T(8,128)(2,1)} %bitcast.57) | data formatting | bytes 4194304 | tf_op jit(solution)/shard_map/all_gather | solution.py:208
  81.9 0.4 copy-done.1
  82.3 20.4 %shard_map.77 = bf16[256,2560]{1,0:T(8,128)(2,1)} custom-call(s32[2]{0:T(128)S(1)} %pad_add_fusion.meta, bf16[256,2560]{1,0:T(8,128)(2,1)S(1)} %bitcast.56, bf16[2048,512]{1,0:T(8,128)(2,1)S(1)} %bitcast.53, bf16[2048,512]{1,0:T(8,128)(2,1)S(1)} %bitcast.55), custom_call_target="tpu_custom_call" | custom-call | tf_op jit(solution)/shard_map/pallas_call | solution.py:90
  102.7 6.0 %shard_map.79 = bf16[32,128,512]{2,1,0:T(8,128)(2,1)} custom-call(s32[16]{0:T(128)} %get-tuple-element.11.targets, bf16[16,128,512]{2,1,0:T(8,128)(2,1)} %all-gather.10.cloned.1.call-done.landed_hbm, bf16[32,128,512]{2,1,0:T(8,128)(2,1)} %shard_map.78.pool_hbm), custom_call_target="tpu_custom_call", output_to_operand_aliasing={{}: (2, {})} | custom-call | tf_op jit(solution)/shard_map/pallas_call | solution.py:140
  (33 shorter events, 1.2 us)
Async XLA Ops:
  7.2 36.2 %all-gather.6.cloned.1.call-start = ((), (), s32[]{:S(2)}) async-start(), calls=%async_computation.2 | async-start | bytes 2359296 | tf_op jit(solution)/shard_map/all_gather | solution.py:192
  12.8 28.3 %all-to-all-start = ((bf16[32,16,512]{2,1,0:T(8,128)(2,1)}), bf16[32,16,512]{2,1,0:T(8,128)(2,1)S(1)}, u32[]{:S(2)}, u32[]{:S(2)}) async-start(bf16[32,16,512]{2,1,0:T(8,128)(2,1)} %gather_fusion), calls=%async_computation | async-start | bytes 1048576 | tf_op jit(solution)/shard_map/all_to_all | solution.py:205
  24.8 29.7 %copy-start.2 = (s32[32,16]{0,1:T(8,128)S(1)}, s32[32,16]{0,1:T(8,128)}, u32[]{:S(2)}) copy-start(s32[32,16]{0,1:T(8,128)} %param.12) | copy-start | bytes 6148
  24.8 54.9 %all-gather.8.cloned.1.call-start = ((), (), s32[]{:S(2)}) async-start(), calls=%async_computation.3 | async-start | bytes 2359296 | tf_op jit(solution)/shard_map/all_gather | solution.py:208
  44.3 27.4 %copy-start.3 = (s32[32]{0:T(128)S(1)}, s32[32]{0:T(128)}, u32[]{:S(2)}) copy-start(s32[32]{0:T(128)} %param.13) | copy-start | bytes 388
  45.7 24.7 %all-to-all-start.1 = ((bf16[32,16,512]{2,1,0:T(8,128)(2,1)}), bf16[32,16,512]{2,1,0:T(8,128)(2,1)S(1)}, u32[]{:S(2)}, u32[]{:S(2)}) async-start(bf16[32,16,512]{2,1,0:T(8,128)(2,1)} %gather_fusion.2), calls=%async_computation.1 | async-start | bytes 1048576 | tf_op jit(solution)/shard_map/all_to_all | solution.py:221
  53.8 48.9 %all-gather.10.cloned.1.call-start = ((), (), s32[]{:S(2)}) async-start(), calls=%async_computation.4 | async-start | bytes 2359296 | tf_op jit(solution)/shard_map/all_gather | solution.py:227
  79.7 2.2 %copy-start = (bf16[1,2048,512]{2,1,0:T(8,128)(2,1)S(1)}, bf16[1,2048,512]{2,1,0:T(8,128)(2,1)}, u32[]{:S(2)}) copy-start(bf16[1,2048,512]{2,1,0:T(8,128)(2,1)} %all-gather.6.cloned.1.call-done) | copy-start | bytes 6291460
  79.7 2.6 %copy-start.1 = (bf16[1,256,2560]{2,1,0:T(8,128)(2,1)S(1)}, bf16[1,256,2560]{2,1,0:T(8,128)(2,1)}, u32[]{:S(2)}) copy-start(bf16[1,256,2560]{2,1,0:T(8,128)(2,1)} %param.8) | copy-start | bytes 3932164
Sparse Core Ops, SparseCore 0:
  9.8 31.9 all-gather.5
  43.7 28.2 all-gather.7
  73.9 28.2 all-gather.9
